TPU v7x, 32 devices: a whole 2x2x4 slice. The times are simulated.
32 devices in a mesh: groups: 2 (over y), lat: 16 (over z, x, core).
Axes of the slice: x: 2, y: 2, z: 4, core: 2. Of those that a mesh axis runs over, the one named last changes fastest.
Arguments:
- latent: bfloat16 [16384, 1536], P(('groups', 'lat')), parts along dimension 0, may hold values from -400 to 400
- query_gain: float32 [1536], replicated, may hold values from 0.1 to 1.9
- key_gain: float32 [1536], replicated, may hold values from 0.1 to 1.9
- output_gain: float32 [1536], replicated, may hold values from 0.1 to 1.9
- output_weight: bfloat16 [1536, 1536], replicated, may hold values from -0.15625 to 0.15625
- observations: bfloat16 [128, 128, 128], P(('groups', 'lat')), parts along dimension 0, may hold values from -6 to 6
- panels: bfloat16 [1024, 1536], P('lat'), may hold values from -0.5 to 0.5
- instrument: int32 [128], P('groups'), parts along dimension 0, may hold values from 0 to 7
- observed_count: int32 [128], P('groups'), parts along dimension 0, may hold values from 1 to 128
- footprint: int32 [128, 6], P(('groups', 'lat')), parts along dimension 0, may hold values from 0 to 63, as said below
- tile_blocks: int32 [128], P(('groups', 'lat')), parts along dimension 0, may hold values from 1 to 6
Outputs:
- encoded: bfloat16 [16384, 1536], P(('groups', 'lat')), parts along dimension 0
There are 2 independent parts, one for each index of `groups`. A program takes and returns all parts, laid end to end along the dimension named above; an argument that names none is the same for every part. Nothing has to cross between parts.
Inputs may be any that keep to these rules, and one draw needn't show every extreme that they name: `footprint`: tile t lies on latitude device t // 4 and block b on b // 4; every entry of tile t's list names a block on that device or on one of the two beside it.
All inputs are finite; a program needn't handle non-finite values.
Results may differ from a plain program's by a relative error of at most 0.0039.
Values may be sent and summed in bfloat16 or wider, within the bound.
No kernel may reach another device: no remote copies, remote signals or barrier semaphores. Data moves between devices by JAX's collectives and lax.ppermute only.
A program may use at most 128 MiB of HBM per device.

v0:
```python
import math

import jax
import jax.numpy as jnp
from jax import lax
from jax.sharding import PartitionSpec as P

D = 1536
HD = 64
NINST = 8
CH = 128
CELLS = 128
OBS = 128
MAXB = 6


def padded(value, sides, width):
    for axis, dim in sides:
        peers, length = (lax.axis_size(axis), value.shape[dim])
        up = [(i, (i + 1) % peers) for i in range(peers - 1)]
        down = [(j, i) for i, j in up]
        last = lax.slice_in_dim(value, length - width, length, axis=dim)
        first = lax.slice_in_dim(value, 0, width, axis=dim)
        before = lax.ppermute(last, axis, up)
        after = lax.ppermute(first, axis, down)
        value = jnp.concatenate([before, value, after], axis=dim)
    return value


def normalize(values, gain):
    values = values.astype(jnp.float32)
    return values * lax.rsqrt(jnp.mean(values * values, axis=-1, keepdims=True) + 1e-06) * gain


def body(
    latent,
    query_gain,
    key_gain,
    output_gain,
    output_weight,
    observations,
    panels,
    instrument,
    observed_count,
    footprint,
    tile_blocks,
):
    block_count = observations.shape[0]
    position = lax.axis_index("lat")
    first_block = (position - 1) * block_count
    all_blocks = instrument.shape[0]
    table = lax.all_gather(panels, "lat", axis=0, tiled=True)
    near_count = 3 * block_count
    near_ids = jnp.clip(first_block + jnp.arange(near_count, dtype=jnp.int32), 0, all_blocks - 1)
    kind_range = jnp.arange(NINST, dtype=jnp.int32)
    own_kinds = lax.dynamic_slice_in_dim(instrument, position * block_count, block_count)
    select = (own_kinds[:, None] == kind_range[None, :]).astype(jnp.bfloat16)
    widened = (observations[:, :, None, :] * select[:, None, :, None]).reshape(
        observations.shape[0], OBS, NINST * CH
    )
    embedded = jnp.einsum("bop,pd->bod", widened, table, preferred_element_type=jnp.float32).astype(
        jnp.bfloat16
    )
    nearby = padded(embedded, (("lat", 0),), block_count)
    keys = normalize(nearby, key_gain).astype(jnp.bfloat16)
    counts = observed_count[near_ids]
    tiles = latent.shape[0] // CELLS
    heads = D // HD
    keys_t = keys.reshape(near_count, OBS, heads, HD).transpose(0, 2, 3, 1)
    values_t = nearby.reshape(near_count, OBS, heads, HD).transpose(0, 2, 3, 1)
    queries = (latent.astype(jnp.float32) * query_gain).astype(jnp.bfloat16)
    queries_t = queries.reshape(tiles, CELLS, heads, HD).transpose(0, 2, 3, 1)
    local_ids = footprint - first_block
    scale = 1.0 / math.sqrt(HD)
    slot_rows = jnp.arange(OBS, dtype=jnp.int32)
    near_range = jnp.arange(near_count, dtype=jnp.int32)

    def attend(slot_index, carry):
        running, total, accum = carry
        chosen = lax.dynamic_index_in_dim(local_ids, slot_index, 1, keepdims=False)
        pick = chosen[:, None] == near_range[None, :]
        select = pick.astype(jnp.bfloat16)
        slot_keys = jnp.einsum(
            "tn,nhdk->thdk", select, keys_t, preferred_element_type=jnp.float32
        ).astype(jnp.bfloat16)
        slot_values = jnp.einsum(
            "tn,nhdk->thdk", select, values_t, preferred_element_type=jnp.float32
        ).astype(jnp.bfloat16)
        slot_counts = jnp.sum(jnp.where(pick, counts[None, :], 0), axis=1)
        scores = (
            jnp.einsum("thdq,thdk->thqk", queries_t, slot_keys, preferred_element_type=jnp.float32)
            * scale
        )
        usable = (slot_index < tile_blocks)[:, None] & (slot_rows[None, :] < slot_counts[:, None])
        usable = usable[:, None, None, :]
        highest = jnp.maximum(running, jnp.max(jnp.where(usable, scores, -1e30), axis=-1))
        factor = jnp.exp(running - highest)
        weights = jnp.where(usable, jnp.exp(scores - highest[..., None]), 0.0)
        total = total * factor + jnp.sum(weights, axis=-1)
        update = jnp.einsum(
            "thdk,thqk->thdq",
            slot_values,
            weights.astype(jnp.bfloat16),
            preferred_element_type=jnp.float32,
        )
        accum = accum * factor[:, :, None, :] + update
        return (highest, total, accum)

    start = (
        jnp.full((tiles, heads, CELLS), -1e30, jnp.float32),
        jnp.zeros((tiles, heads, CELLS), jnp.float32),
        jnp.zeros((tiles, heads, HD, CELLS), jnp.float32),
    )
    running, total, accum = lax.fori_loop(0, MAXB, attend, start)
    attended = (
        (accum / total[:, :, None, :])
        .astype(jnp.bfloat16)
        .transpose(0, 3, 1, 2)
        .reshape(tiles * CELLS, D)
    )
    mixed = latent.astype(jnp.float32) + jnp.dot(
        attended, output_weight, preferred_element_type=jnp.float32
    )
    return normalize(mixed, output_gain).astype(jnp.bfloat16)


def solution(mesh):
    return jax.shard_map(
        body,
        mesh=mesh,
        in_specs=(
            P(("groups", "lat"), None),
            P(),
            P(),
            P(),
            P(),
            P(("groups", "lat"), None, None),
            P("lat", None),
            P("groups"),
            P("groups"),
            P(("groups", "lat"), None),
            P(("groups", "lat")),
        ),
        out_specs=P(("groups", "lat"), None),
        check_vma=False,
    )
```

profile of v0, /device:TPU:5, one launch (start us, length us, event | category | flops | bytes accessed | tf_op | source)
XLA Modules:
  0.0 224.0 jit_solution(17268411297548896115)
XLA Ops:
  9.7 47.0 %all-gather.2.cloned.1.call-done = bf16[1024,1536]{1,0:T(8,128)(2,1)} async-done(((bf16[64,1536]{1,0:T(8,128)(2,1)}), bf16[1024,1536]{1,0:T(8,128)(2,1)}) %all-gather.2.cloned.1.call-update) | async-done | bytes 3145744 | tf_op jit(solution)/shard_map/all_gather | solution.py:52
  56.7 5.0 %fusion.30 = bf16[4,128,1536]{2,1,0:T(8,128)(2,1)} fusion(bf16[1024,1536]{1,0:T(8,128)(2,1)} %all-gather.2.cloned.1.call-done, bf16[4,128,1024]{2,1,0:T(8,128)(2,1)S(1)} %mul.113, bf16[4,1024]{1,0:T(4,128)(2,1)S(1)} %bitcast.76), kind=kOutput, calls=%fused_computation.47 | convolution fusion | flops 1611923456 | bytes 5775360 | tf_op jit(solution)/shard_map/bop,pd->bod/dot_general | solution.py:61
  61.7 2.2 collective-permute-start.1
  63.9 3.4 %collective-permute-start = (bf16[4,128,1536]{2,1,0:T(8,128)(2,1)}, bf16[4,128,1536]{2,1,0:T(8,128)(2,1)}, u32[]{:S(2)}, u32[]{:S(2)}) collective-permute-start(bf16[4,128,1536]{2,1,0:T(8,128)(2,1)} %fusion.30), channel_id=1, source_target_pairs={{0,1},{1,2},{2,3},{3,4},{4,5},{5,6},{6,7},{7,8},{8,9},{9,10},{10,1... | collective-permute-start | bytes 4718600 | tf_op jit(solution)/shard_map/ppermute | solution.py:24
  70.0 1.9 copy.33
  71.9 11.8 %collective-permute-done.1 = bf16[4,128,1536]{2,1,0:T(8,128)(2,1)} collective-permute-done((bf16[4,128,1536]{2,1,0:T(8,128)(2,1)}, bf16[4,128,1536]{2,1,0:T(8,128)(2,1)}, u32[]{:S(2)}, u32[]{:S(2)}) %collective-permute-start.1) | collective-permute-done | bytes 1572896 | tf_op jit(solution)/shard_map/ppermute | solution.py:25
  83.7 16.1 %collective-permute-done = bf16[4,128,1536]{2,1,0:T(8,128)(2,1)} collective-permute-done((bf16[4,128,1536]{2,1,0:T(8,128)(2,1)}, bf16[4,128,1536]{2,1,0:T(8,128)(2,1)}, u32[]{:S(2)}, u32[]{:S(2)}) %collective-permute-start) | collective-permute-done | bytes 1572896 | tf_op jit(solution)/shard_map/ppermute | solution.py:24
  99.8 5.7 %multiply_reduce_fusion = (f32[12,128]{1,0:T(8,128)S(1)}, bf16[12,128,1536]{2,1,0:T(8,128)(2,1)}) fusion(bf16[4,128,1536]{2,1,0:T(8,128)(2,1)} %collective-permute-done.1, bf16[4,128,1536]{2,1,0:T(8,128)(2,1)} %fusion.30, bf16[4,128,1536]{2,1,0:T(8,128)(2,1)} %collective-permute-done), kind=kLoop, calls=%fused_computation.36 | loop fusion | flops 11794944 | bytes 9443328 | tf_op jit(solution)/shard_map/reduce_sum | solution.py:32
  105.6 2.6 %copy.34 = bf16[4,128,1536]{1,2,0:T(8,128)(2,1)} copy(bf16[4,128,1536]{2,1,0:T(8,128)(2,1)} %collective-permute-done.1) | data formatting | bytes 3145728 | tf_op jit(solution)/shard_map/ppermute | solution.py:25
  108.1 2.6 %copy.32 = bf16[4,128,1536]{1,2,0:T(8,128)(2,1)} copy(bf16[4,128,1536]{2,1,0:T(8,128)(2,1)} %collective-permute-done) | data formatting | bytes 3145728 | tf_op jit(solution)/shard_map/ppermute | solution.py:24
  110.7 3.7 %fusion.26 = bf16[12,24,64,128]{3,2,1,0:T(8,128)(2,1)S(1)} fusion(bf16[4,128,24,64]{1,3,2,0:T(8,128)(2,1)} %bitcast.73, bf16[4,128,24,64]{1,3,2,0:T(8,128)(2,1)S(1)} %bitcast.72, bf16[4,128,24,64]{1,3,2,0:T(8,128)(2,1)} %bitcast.74, f32[24,64]{1,0:T(8,128)S(1)} %mul.122, f32[12,128]{1,0:T(8,128)S(1)} %add_rsqrt_fusion), kind=kLoop, calls=%fused_computation.37 | loop fusion | flops 14155776 | bytes 9449472 | tf_op jit(solution)/shard_map/transpose | solution.py:69
  114.4 6.9 %copy.37 = bf16[12,24,64,128]{3,0,2,1:T(8,128)(2,1)} copy(bf16[12,24,64,128]{3,2,1,0:T(8,128)(2,1)S(1)} %fusion.26) | data formatting | bytes 9437184
  121.3 9.1 %copy.43 = bf16[12,128,1536]{1,0,2:T(8,128)(2,1)} copy(bf16[12,128,1536]{2,1,0:T(8,128)(2,1)} %get-tuple-element.287) | data formatting | bytes 9437184 | tf_op jit(solution)/shard_map/transpose | solution.py:70
  130.4 78.2 %while.18 = (s32[]{:T(128)}, f32[4,24,128]{2,1,0:T(8,128)S(1)}, f32[4,24,128]{2,1,0:T(8,128)S(1)}, f32[4,24,64,128]{3,2,1,0:T(8,128)}, s32[4]{0:T(128)S(1)}, /*i...) while((s32[]{:T(128)}, f32[4,24,128]{2,1,0:T(8,128)S(1)}, ...), condition=%wide.region_5.6_spmd.clone, body=%wide.region_1.5_spmd.clone.sunk | while | flops 461698304 | bytes 87296416 | solution.py:114
  130.7 4.0 %convolution_convert_fusion.5 = bf16[4,24,64,128]{3,0,2,1:T(4,128)(2,1)S(1)} fusion(bf16[12,24,64,128]{3,0,2,1:T(8,128)(2,1)} %get-tuple-element.394, s32[4]{0:T(128)S(1)} %dynamic-slice_bitcast_fusion.2), kind=kOutput, calls=%fused_computation.14.clone.1 | convolution fusion | flops 19660848 | bytes 6291472 | tf_op jit(solution)/shard_map/while/body/eval_jaxpr/tn,nhdk->thdk/dot_general | solution.py:86
  143.7 4.0 %convolution_convert_fusion.5 = bf16[4,24,64,128]{3,0,2,1:T(4,128)(2,1)S(1)} fusion(bf16[12,24,64,128]{3,0,2,1:T(8,128)(2,1)} %get-tuple-element.394, s32[4]{0:T(128)S(1)} %dynamic-slice_bitcast_fusion.2), kind=kOutput, calls=%fused_computation.14.clone.1 | convolution fusion | flops 19660848 | bytes 6291472 | tf_op jit(solution)/shard_map/while/body/eval_jaxpr/tn,nhdk->thdk/dot_general | solution.py:86
  153.1 1.8 fusion.63
  156.8 4.0 %convolution_convert_fusion.5 = bf16[4,24,64,128]{3,0,2,1:T(4,128)(2,1)S(1)} fusion(bf16[12,24,64,128]{3,0,2,1:T(8,128)(2,1)} %get-tuple-element.394, s32[4]{0:T(128)S(1)} %dynamic-slice_bitcast_fusion.2), kind=kOutput, calls=%fused_computation.14.clone.1 | convolution fusion | flops 19660848 | bytes 6291472 | tf_op jit(solution)/shard_map/while/body/eval_jaxpr/tn,nhdk->thdk/dot_general | solution.py:86
  169.8 4.0 %convolution_convert_fusion.5 = bf16[4,24,64,128]{3,0,2,1:T(4,128)(2,1)S(1)} fusion(bf16[12,24,64,128]{3,0,2,1:T(8,128)(2,1)} %get-tuple-element.394, s32[4]{0:T(128)S(1)} %dynamic-slice_bitcast_fusion.2), kind=kOutput, calls=%fused_computation.14.clone.1 | convolution fusion | flops 19660848 | bytes 6291472 | tf_op jit(solution)/shard_map/while/body/eval_jaxpr/tn,nhdk->thdk/dot_general | solution.py:86
  179.1 1.8 fusion.63
  182.8 4.0 %convolution_convert_fusion.5 = bf16[4,24,64,128]{3,0,2,1:T(4,128)(2,1)S(1)} fusion(bf16[12,24,64,128]{3,0,2,1:T(8,128)(2,1)} %get-tuple-element.394, s32[4]{0:T(128)S(1)} %dynamic-slice_bitcast_fusion.2), kind=kOutput, calls=%fused_computation.14.clone.1 | convolution fusion | flops 19660848 | bytes 6291472 | tf_op jit(solution)/shard_map/while/body/eval_jaxpr/tn,nhdk->thdk/dot_general | solution.py:86
  195.9 4.0 %convolution_convert_fusion.5 = bf16[4,24,64,128]{3,0,2,1:T(4,128)(2,1)S(1)} fusion(bf16[12,24,64,128]{3,0,2,1:T(8,128)(2,1)} %get-tuple-element.394, s32[4]{0:T(128)S(1)} %dynamic-slice_bitcast_fusion.2), kind=kOutput, calls=%fused_computation.14.clone.1 | convolution fusion | flops 19660848 | bytes 6291472 | tf_op jit(solution)/shard_map/while/body/eval_jaxpr/tn,nhdk->thdk/dot_general | solution.py:86
  208.7 2.5 %fusion.35 = bf16[4,128,24,64]{1,3,2,0:T(8,128)(2,1)S(1)} fusion(f32[4,24,64,128]{3,2,1,0:T(8,128)} %get-tuple-element.205, f32[4,24,128]{2,1,0:T(8,128)S(1)} %get-tuple-element.206), kind=kLoop, calls=%fused_computation.50 | loop fusion | flops 1572864 | bytes 4767744 | tf_op jit(solution)/shard_map/transpose | solution.py:118
  212.7 3.0 %multiply_reduce_fusion.1 = (f32[512]{0:T(512)S(1)}, f32[512,1536]{1,0:T(8,128)S(1)}) fusion(bf16[1536,1536]{1,0:T(8,128)(2,1)S(1)} %copy-done.11, bf16[192,8,4,128]{3,2,1,0:T(4,128)(2,1)S(1)} %bitcast.75, bf16[512,1536]{1,0:T(8,128)(2,1)S(1)} %copy-done.6), kind=kOutput, calls=%fused_computation.45 | convolution fusion | flops 2419064320 | bytes 11012096 | tf_op jit(solution)/shard_map/dot_general | solution.py:121
  (145 shorter events, 59.1 us)
Async XLA Ops:
  6.5 62.8 %copy-start = (s32[64]{0:T(128)S(1)}, s32[64]{0:T(128)}, u32[]{:S(2)}) copy-start(s32[64]{0:T(128)} %param.21) | copy-start | bytes 772
  6.5 50.2 %all-gather.2.cloned.1.call-start = ((), (), s32[]{:S(2)}) async-start(), calls=%async_computation | async-start | bytes 3342336 | tf_op jit(solution)/shard_map/all_gather | solution.py:52
  56.7 10.6 %copy-start.10 = (s32[4,6]{1,0:T(4,128)S(1)}, s32[4,6]{1,0:T(4,128)}, u32[]{:S(2)}) copy-start(s32[4,6]{1,0:T(4,128)} %param.22) | copy-start | bytes 292
  56.7 10.7 %copy-start.9 = (f32[1536]{0:T(1024)S(1)}, f32[1536]{0:T(1024)}, u32[]{:S(2)}) copy-start(f32[1536]{0:T(1024)} %param.15) | copy-start | bytes 18436
  56.7 10.7 %copy-start.5 = (bf16[512,1536]{1,0:T(8,128)(2,1)S(1)}, bf16[512,1536]{1,0:T(8,128)(2,1)}, u32[]{:S(2)}) copy-start(bf16[512,1536]{1,0:T(8,128)(2,1)} %param.13) | copy-start | bytes 4718596
  56.7 10.7 %copy-start.7 = (f32[1536]{0:T(1024)S(1)}, f32[1536]{0:T(1024)}, u32[]{:S(2)}) copy-start(f32[1536]{0:T(1024)} %param.14) | copy-start | bytes 18436
  61.7 22.0 %collective-permute-start.1 = (bf16[4,128,1536]{2,1,0:T(8,128)(2,1)}, bf16[4,128,1536]{2,1,0:T(8,128)(2,1)}, u32[]{:S(2)}, u32[]{:S(2)}) collective-permute-start(bf16[4,128,1536]{2,1,0:T(8,128)(2,1)} %fusion.30), channel_id=1, source_target_pairs={{1,0},{2,1},{3,2},{4,3},{5,4},{6,5},{7,6},{8,7},{9,8},{10,9},{11,1... | collective-permute-start | bytes 4718600 | tf_op jit(solution)/shard_map/ppermute | solution.py:25
  63.9 36.0 %collective-permute-start = (bf16[4,128,1536]{2,1,0:T(8,128)(2,1)}, bf16[4,128,1536]{2,1,0:T(8,128)(2,1)}, u32[]{:S(2)}, u32[]{:S(2)}) collective-permute-start(bf16[4,128,1536]{2,1,0:T(8,128)(2,1)} %fusion.30), channel_id=1, source_target_pairs={{0,1},{1,2},{2,3},{3,4},{4,5},{5,6},{6,7},{7,8},{8,9},{9,10},{10,1... | collective-permute-start | bytes 4718600 | tf_op jit(solution)/shard_map/ppermute | solution.py:24
  121.3 9.1 %copy-start.12 = (s32[4]{0:T(128)S(1)}, s32[4]{0:T(128)}, u32[]{:S(2)}) copy-start(s32[4]{0:T(128)} %param.23) | copy-start | bytes 52
  130.7 4.6 %copy-start.2 = (bf16[12,24,64,128]{3,0,2,1:T(8,128)(2,1)S(1)}, bf16[12,24,64,128]{3,0,2,1:T(8,128)(2,1)}, u32[]{:S(2)}) copy-start(bf16[12,24,64,128]{3,0,2,1:T(8,128)(2,1)} %get-tuple-element.392) | copy-start | bytes 14155780 | tf_op jit(solution)/shard_map/while
  138.1 1.9 copy-start.3
  143.7 4.6 %copy-start.2 = (bf16[12,24,64,128]{3,0,2,1:T(8,128)(2,1)S(1)}, bf16[12,24,64,128]{3,0,2,1:T(8,128)(2,1)}, u32[]{:S(2)}) copy-start(bf16[12,24,64,128]{3,0,2,1:T(8,128)(2,1)} %get-tuple-element.392) | copy-start | bytes 14155780 | tf_op jit(solution)/shard_map/while
  151.2 1.9 copy-start.3
  156.8 4.6 %copy-start.2 = (bf16[12,24,64,128]{3,0,2,1:T(8,128)(2,1)S(1)}, bf16[12,24,64,128]{3,0,2,1:T(8,128)(2,1)}, u32[]{:S(2)}) copy-start(bf16[12,24,64,128]{3,0,2,1:T(8,128)(2,1)} %get-tuple-element.392) | copy-start | bytes 14155780 | tf_op jit(solution)/shard_map/while
  164.2 1.9 copy-start.3
  169.8 4.6 %copy-start.2 = (bf16[12,24,64,128]{3,0,2,1:T(8,128)(2,1)S(1)}, bf16[12,24,64,128]{3,0,2,1:T(8,128)(2,1)}, u32[]{:S(2)}) copy-start(bf16[12,24,64,128]{3,0,2,1:T(8,128)(2,1)} %get-tuple-element.392) | copy-start | bytes 14155780 | tf_op jit(solution)/shard_map/while
  177.2 1.9 copy-start.3
  182.8 4.6 %copy-start.2 = (bf16[12,24,64,128]{3,0,2,1:T(8,128)(2,1)S(1)}, bf16[12,24,64,128]{3,0,2,1:T(8,128)(2,1)}, u32[]{:S(2)}) copy-start(bf16[12,24,64,128]{3,0,2,1:T(8,128)(2,1)} %get-tuple-element.392) | copy-start | bytes 14155780 | tf_op jit(solution)/shard_map/while
  190.3 1.9 copy-start.3
  195.9 4.6 %copy-start.2 = (bf16[12,24,64,128]{3,0,2,1:T(8,128)(2,1)S(1)}, bf16[12,24,64,128]{3,0,2,1:T(8,128)(2,1)}, u32[]{:S(2)}) copy-start(bf16[12,24,64,128]{3,0,2,1:T(8,128)(2,1)} %get-tuple-element.392) | copy-start | bytes 14155780 | tf_op jit(solution)/shard_map/while
  208.7 4.0 %copy-start.6 = (bf16[512,1536]{1,0:T(8,128)(2,1)S(1)}, bf16[512,1536]{1,0:T(8,128)(2,1)}, u32[]{:S(2)}) copy-start(bf16[512,1536]{1,0:T(8,128)(2,1)} %param.13) | copy-start | bytes 4718596
  208.7 4.0 %copy-start.11 = (bf16[1536,1536]{1,0:T(8,128)(2,1)S(1)}, bf16[1536,1536]{1,0:T(8,128)(2,1)}, u32[]{:S(2)}) copy-start(bf16[1536,1536]{1,0:T(8,128)(2,1)} %param.17) | copy-start | bytes 14155780
  212.7 3.0 %copy-start.8 = (f32[1536]{0:T(1024)S(1)}, f32[1536]{0:T(1024)}, u32[]{:S(2)}) copy-start(f32[1536]{0:T(1024)} %param.16) | copy-start | bytes 18436
  212.7 4.5 %copy-start.1 = (s32[64]{0:T(128)S(1)}, s32[64]{0:T(128)}, u32[]{:S(2)}) copy-start(s32[64]{0:T(128)} %param.21) | copy-start | bytes 772
  (7 other events, 11.7 us)
Sparse Core Ops, SparseCore 0:
  9.6 47.0 all-gather.1
where the time goes:
time: 226 us; the launch traced here: 224 us
  waiting for transfers between devices  75.7 us (33%)
  matrix products  59.4 us (26%)
  local copies, waits for them, and re-layouts  43.7 us (19%)
  other arithmetic  25.7 us (11%)
  between operations  13.6 us (6%)
  starting transfers between devices  5.56 us (2%)
    all_gather x1, waiting for transfers between devices, body(): table = lax.all_gather(panels, 'lat', axis=0, tiled=True)  47 us
    dot_general x6, matrix products, attend(): jnp.einsum('tn,nhdk->thdk', select, values_t, preferred_element_type=jnp....  23.8 us
    ppermute x1, waiting for transfers between devices, padded(): before = lax.ppermute(last, axis, up)  16.1 us
    while x42, local copies, waits for them, and re-layouts  14.5 us
    ppermute x1, waiting for transfers between devices, padded(): after = lax.ppermute(first, axis, down)  11.8 us
    dot_general x6, matrix products, attend(): jnp.einsum('thdk,thqk->thdq', slot_values, weights.astype(jnp.bfloat16),...  10.8 us
    dot_general x6, matrix products, attend(): jnp.einsum('thdq,thdk->thqk', queries_t, slot_keys, preferred_element_typ...  10.7 us
    reduce_sum x6, other arithmetic, attend(): total = total * factor + jnp.sum(weights, axis=-1)  10 us
  transfers between devices with their start and end apart: 3, of which 3 were waited for; matrix products, arithmetic and copies ran while one was open for 3% of the time, Pallas kernels for 0%

commit v1 on v0

v1 whole, which is shorter than its diff:
```python
import functools
import math

import jax
import jax.numpy as jnp
from jax import lax
from jax.experimental import pallas as pl
from jax.experimental.pallas import tpu as pltpu
from jax.sharding import PartitionSpec as P

D = 1536
HD = 64
CH = 128
CELLS = 128
OBS = 128
MAXB = 6
LANES = 128


def padded(value, axis, width):
    peers, length = lax.axis_size(axis), value.shape[0]
    up = [(i, i + 1) for i in range(peers - 1)]
    down = [(j, i) for i, j in up]
    before = lax.ppermute(value[length - width:], axis, up)
    after = lax.ppermute(value[:width], axis, down)
    return jnp.concatenate([before, value, after], axis=0)


def normalize(values, gain):
    values = values.astype(jnp.float32)
    return values * lax.rsqrt(jnp.mean(values * values, axis=-1, keepdims=True) + 1e-06) * gain


def attend_kernel(ids_ref, nb_ref, cnt_ref, q_ref, k_ref, v_ref, o_ref, s_ref, m_ref, t_ref, a_ref):
    tile = pl.program_id(0)
    used = nb_ref[tile]
    scale = 1.0 / math.sqrt(HD)
    lane = lax.broadcasted_iota(jnp.int32, (1, LANES), 1)
    low = lane < HD
    for pair in range(D // LANES):
        cols = pl.ds(pair * LANES, LANES)
        qp = q_ref[:, cols].astype(jnp.float32)
        qa = jnp.where(low, qp, 0.0).astype(jnp.bfloat16)
        qb = jnp.where(low, 0.0, qp).astype(jnp.bfloat16)
        m_ref[...] = jnp.full(m_ref.shape, -jnp.inf, jnp.float32)
        t_ref[...] = jnp.zeros(t_ref.shape, jnp.float32)
        a_ref[...] = jnp.zeros(a_ref.shape, jnp.float32)

        def score_step(j, carry):
            block = ids_ref[tile * MAXB + j]
            keys = k_ref[block, :, cols]
            valid = lane < cnt_ref[block]
            for h, qh in enumerate((qa, qb)):
                s = lax.dot_general(
                    qh, keys, (((1,), (1,)), ((), ())), preferred_element_type=jnp.float32
                ) * scale
                s = jnp.where(valid, s, -jnp.inf)
                s_ref[h, j] = s
                m_ref[h] = jnp.maximum(m_ref[h], s)
            return carry

        lax.fori_loop(0, used, score_step, 0)
        ma = jnp.max(m_ref[0], axis=1, keepdims=True)
        mb = jnp.max(m_ref[1], axis=1, keepdims=True)

        def value_step(j, carry):
            block = ids_ref[tile * MAXB + j]
            values = v_ref[block, :, cols]
            for h, mh in enumerate((ma, mb)):
                w = jnp.exp(s_ref[h, j] - mh)
                t_ref[h] = t_ref[h] + w
                a_ref[h] = a_ref[h] + jnp.dot(
                    w.astype(jnp.bfloat16), values, preferred_element_type=jnp.float32
                )
            return carry

        lax.fori_loop(0, used, value_step, 0)
        ta = jnp.sum(t_ref[0], axis=1, keepdims=True)
        tb = jnp.sum(t_ref[1], axis=1, keepdims=True)
        out = jnp.where(low, a_ref[0] / ta, a_ref[1] / tb)
        o_ref[:, cols] = out.astype(jnp.bfloat16)


def attend(local_ids, tile_blocks, counts, queries, keys, values):
    tiles = queries.shape[0] // CELLS
    near = keys.shape[0]
    grid_spec = pltpu.PrefetchScalarGridSpec(
        num_scalar_prefetch=3,
        grid=(tiles,),
        in_specs=[
            pl.BlockSpec((CELLS, D), lambda t, *_: (t, 0)),
            pl.BlockSpec((near, OBS, D), lambda t, *_: (0, 0, 0)),
            pl.BlockSpec((near, OBS, D), lambda t, *_: (0, 0, 0)),
        ],
        out_specs=pl.BlockSpec((CELLS, D), lambda t, *_: (t, 0)),
        scratch_shapes=[
            pltpu.VMEM((2, MAXB, CELLS, OBS), jnp.float32),
            pltpu.VMEM((2, CELLS, LANES), jnp.float32),
            pltpu.VMEM((2, CELLS, LANES), jnp.float32),
            pltpu.VMEM((2, CELLS, LANES), jnp.float32),
        ],
    )
    return pl.pallas_call(
        attend_kernel,
        grid_spec=grid_spec,
        out_shape=jax.ShapeDtypeStruct(queries.shape, jnp.bfloat16),
        compiler_params=pltpu.CompilerParams(vmem_limit_bytes=48 * 1024 * 1024),
    )(local_ids.reshape(-1), tile_blocks, counts, queries, keys, values)


def body(
    latent,
    query_gain,
    key_gain,
    output_gain,
    output_weight,
    observations,
    panels,
    instrument,
    observed_count,
    footprint,
    tile_blocks,
):
    block_count = observations.shape[0]
    position = lax.axis_index("lat")
    first_block = (position - 1) * block_count
    all_blocks = instrument.shape[0]
    table = lax.all_gather(panels, "lat", axis=0, tiled=True)
    kinds = table.shape[0] // CH
    near_obs = padded(observations, "lat", block_count)
    near_count = near_obs.shape[0]
    near_ids = jnp.clip(first_block + jnp.arange(near_count, dtype=jnp.int32), 0, all_blocks - 1)
    near_kinds = instrument[near_ids]
    counts = observed_count[near_ids]
    near_panels = table.reshape(kinds, CH, D)[near_kinds]
    embedded = jnp.einsum(
        "boc,bcd->bod", near_obs, near_panels, preferred_element_type=jnp.float32
    ).astype(jnp.bfloat16)
    keys = normalize(embedded, key_gain).astype(jnp.bfloat16)
    queries = (latent.astype(jnp.float32) * query_gain).astype(jnp.bfloat16)
    local_ids = (footprint - first_block).astype(jnp.int32)
    attended = attend(local_ids, tile_blocks.astype(jnp.int32), counts, queries, keys, embedded)
    mixed = latent.astype(jnp.float32) + jnp.dot(
        attended, output_weight, preferred_element_type=jnp.float32
    )
    return normalize(mixed, output_gain).astype(jnp.bfloat16)


def solution(mesh):
    return jax.shard_map(
        body,
        mesh=mesh,
        in_specs=(
            P(("groups", "lat"), None),
            P(),
            P(),
            P(),
            P(),
            P(("groups", "lat"), None, None),
            P("lat", None),
            P("groups"),
            P("groups"),
            P(("groups", "lat"), None),
            P(("groups", "lat")),
        ),
        out_specs=P(("groups", "lat"), None),
        check_vma=False,
    )
```

time: 226 us -> 192 us (0.85); the launches traced: 224 us -> 193 us
  Pallas kernels: 0 us -> 112 us
  matrix products: 59.4 us -> 6.53 us
  local copies, waits for them, and re-layouts: 43.7 us -> 7.6 us
  waiting for transfers between devices: 75.7 us -> 40.7 us
  other arithmetic: 25.7 us -> 7.27 us
    pallas_call x0 -> x1, Pallas kernels: none -> 112 us  [attend(): pl.pallas_call(attend_kernel, grid_spec=grid_spec, out_shape=jax.ShapeDty...]
    dot_general x25 -> x1, matrix products: 56.3 us -> 3.8 us  [body(): jnp.einsum('boc,bcd->bod', near_obs, near_panels, preferred_element_type=...]
    ppermute x2, waiting for transfers between devices: 27.9 us -> 0.01 us  [the longest x1 0.01 us: padded(): before = lax.ppermute(value[length - width:], axis, up)]
    reduce_sum x13 -> x0, other arithmetic: 16.9 us -> none  [the longest x6 10 us: attend(): total = total * factor + jnp.sum(weights, axis=-1)]
    while x42 -> x0, local copies, waits for them, and re-layouts: 14.5 us -> none
    transpose x2 -> x0, local copies, waits for them, and re-layouts: 10.5 us -> none  [the longest x1 9.08 us: body(): values_t = nearby.reshape(near_count, OBS, heads, HD).transpose(0, 2, 3, 1)]
    all_gather x1, waiting for transfers between devices: 47 us -> 40 us  [body(): table = lax.all_gather(panels, 'lat', axis=0, tiled=True)]
    unnamed x25 -> x20, local copies, waits for them, and re-layouts: 7.56 us -> 1.15 us
  transfers between devices with their start and end apart: 3 -> 3, of which waited for: 3 -> 1; matrix products, arithmetic and copies ran while one was open for 3% -> 5% of each run, Pallas kernels for 0% -> 0%
where the time goes in v1:
time: 192 us; the launch traced here: 193 us
  Pallas kernels  112 us (58%)
  waiting for transfers between devices  40.7 us (21%)
  between operations  13.6 us (7%)
  local copies, waits for them, and re-layouts  7.6 us (4%)
  other arithmetic  7.27 us (4%)
  matrix products  6.53 us (3%)
  starting transfers between devices  5.61 us (3%)
    pallas_call x1, Pallas kernels, attend(): pl.pallas_call(attend_kernel, grid_spec=grid_spec, out_shape=jax.ShapeDty...  112 us
    all_gather x1, waiting for transfers between devices, body(): table = lax.all_gather(panels, 'lat', axis=0, tiled=True)  40 us
    gather x1, local copies, waits for them, and re-layouts, body(): near_panels = table.reshape(kinds, CH, D)[near_kinds]  5.05 us
  transfers between devices with their start and end apart: 3, of which 1 were waited for; matrix products, arithmetic and copies ran while one was open for 5% of the time, Pallas kernels for 0%

profile of v1, /device:TPU:5, one launch (start us, length us, event | category | flops | bytes accessed | tf_op | source)
XLA Modules:
  0.0 193.2 jit_solution(3465820987335992659)
XLA Ops:
  6.5 0.0 all-gather.2.cloned.1.call-start
  6.5 0.7 all-gather.2.cloned.1.call-update
  7.3 3.7 %collective-permute-start = (bf16[4,128,128]{2,1,0:T(8,128)(2,1)}, bf16[4,128,128]{2,1,0:T(8,128)(2,1)S(1)}, u32[]{:S(2)}, u32[]{:S(2)}) collective-permute-start(bf16[4,128,128]{2,1,0:T(8,128)(2,1)} %param.16), channel_id=1, source_target_pairs={{0,1},{1,2},{2,3},{3,4},{4,5},{5,6},{6,7},{7,8},{8,9},{9,10},{10,1... | collective-permute-start | bytes 393224 | tf_op jit(solution)/shard_map/ppermute | solution.py:24
  11.0 1.9 collective-permute-start.1
  12.9 0.7 gather_fusion.1
  13.6 0.7 broadcast_subtract_fusion
  14.3 1.7 fusion.3.q_ref
  16.0 0.1 reshape.57.ids_ref
  16.0 0.7 gather_fusion
  16.7 40.0 %all-gather.2.cloned.1.call-done = bf16[1024,1536]{1,0:T(8,128)(2,1)} async-done(((bf16[64,1536]{1,0:T(8,128)(2,1)}), bf16[1024,1536]{1,0:T(8,128)(2,1)}) %all-gather.2.cloned.1.call-update) | async-done | bytes 3145744 | tf_op jit(solution)/shard_map/all_gather | solution.py:128
  56.7 5.1 %gather_fusion.2 = bf16[12,128,1536]{2,1,0:T(8,128)(2,1)} fusion(bf16[8,128,1536]{2,1,0:T(8,128)(2,1)} %bitcast.10, s32[1024]{0:T(1024)S(1)} %pad_clamp_fusion), kind=kCustom, calls=%fused_computation.2 | custom fusion | bytes 9437232 | tf_op jit(solution)/shard_map/gather | solution.py:135
  61.8 0.0 collective-permute-done
  61.8 0.0 collective-permute-done.1
  61.8 3.8 %fusion = (f32[12,128]{1,0:T(8,128)S(1)}, bf16[12,128,1536]{2,1,0:T(8,128)(2,1)S(1)}) fusion(bf16[12,128,1536]{2,1,0:T(8,128)(2,1)} %gather_fusion.2, bf16[4,128,128]{2,1,0:T(8,128)(2,1)S(1)} %collective-permute-done.1, bf16[4,128,128]{2,1,0:T(8,128)(2,1)S(1)} %copy-done.5, bf16[4,128,128]{2,1,0:T(8,128)(2,1)S(1)} %collective-permute-done), kind=kOutput, calls=%fused_computation.5 | convolution fusion | flops 613808640 | bytes 9836544 | tf_op jit(solution)/shard_map/boc,bcd->bod/dot_general | solution.py:136
  65.6 0.0 copy-start.1
  65.6 0.0 slice-start
  65.7 3.4 %fusion.2.k_ref = bf16[12,128,1536]{2,1,0:T(8,128)(2,1)} fusion(bf16[12,128,1536]{2,1,0:T(8,128)(2,1)S(1)} %get-tuple-element.6.v_ref, f32[1536]{0:T(1024)S(1)} %copy-done.6, f32[12,128]{1,0:T(8,128)S(1)} %add_rsqrt_fusion), kind=kLoop, calls=%fused_computation.7 | loop fusion | flops 9437184 | bytes 9449472 | tf_op jit(solution)/shard_map/convert_element_type | solution.py:139
  69.0 1.1 copy-done.3
  70.2 0.0 copy-done.1
  70.2 111.9 %shard_map.109 = bf16[512,1536]{1,0:T(8,128)(2,1)S(1)} custom-call(s32[24]{0:T(128)S(1)} %reshape.57.ids_ref, s32[4]{0:T(128)S(1)} %copy-done.1, s32[12]{0:T(128)S(1)} %gather_fusion, bf16[512,1536]{1,0:T(8,128)(2,1)S(1)} %fusion.3.q_ref, bf16[12,128,1536]{2,1,0:T(8,128)(2,1)} %fusion.2.k_ref, bf16[12,128,1536]{2,1,0:T(8,128)(2,1)} %copy-done.3), custom_call_target="tpu_custom_call" | custom-call | tf_op jit(solution)/shard_map/pallas_call | solution.py:103
  182.1 0.0 slice-done
  182.1 0.0 copy-start.7
  182.1 2.7 %multiply_reduce_fusion = (f32[512]{0:T(512)S(1)}, f32[512,1536]{1,0:T(8,128)S(1)}) fusion(bf16[512,1536]{1,0:T(8,128)(2,1)S(1)} %shard_map.109, bf16[1536,1536]{1,0:T(8,128)(2,1)S(1)} %bitcast.12, bf16[512,1536]{1,0:T(8,128)(2,1)S(1)} %copy-done.4), kind=kOutput, calls=%fused_computation.13 | convolution fusion | flops 2419064320 | bytes 11012096 | tf_op jit(solution)/shard_map/dot_general | solution.py:143
  184.9 1.5 multiply_convert_fusion
  (21 shorter events, 0.1 us)
Async XLA Ops:
  6.5 6.4 %copy-start = (s32[64]{0:T(128)S(1)}, s32[64]{0:T(128)}, u32[]{:S(2)}) copy-start(s32[64]{0:T(128)} %param.18) | copy-start | bytes 772
  6.5 9.5 %copy-start.2 = (s32[64]{0:T(128)S(1)}, s32[64]{0:T(128)}, u32[]{:S(2)}) copy-start(s32[64]{0:T(128)} %param.19) | copy-start | bytes 772
  6.5 50.2 %all-gather.2.cloned.1.call-start = ((), (), s32[]{:S(2)}) async-start(), calls=%async_computation | async-start | bytes 3342336 | tf_op jit(solution)/shard_map/all_gather | solution.py:128
  7.3 54.5 %collective-permute-start = (bf16[4,128,128]{2,1,0:T(8,128)(2,1)}, bf16[4,128,128]{2,1,0:T(8,128)(2,1)S(1)}, u32[]{:S(2)}, u32[]{:S(2)}) collective-permute-start(bf16[4,128,128]{2,1,0:T(8,128)(2,1)} %param.16), channel_id=1, source_target_pairs={{0,1},{1,2},{2,3},{3,4},{4,5},{5,6},{6,7},{7,8},{8,9},{9,10},{10,1... | collective-permute-start | bytes 393224 | tf_op jit(solution)/shard_map/ppermute | solution.py:24
  11.0 50.8 %collective-permute-start.1 = (bf16[4,128,128]{2,1,0:T(8,128)(2,1)}, bf16[4,128,128]{2,1,0:T(8,128)(2,1)S(1)}, u32[]{:S(2)}, u32[]{:S(2)}) collective-permute-start(bf16[4,128,128]{2,1,0:T(8,128)(2,1)} %param.16), channel_id=1, source_target_pairs={{1,0},{2,1},{3,2},{4,3},{5,4},{6,5},{7,6},{8,7},{9,8},{10,9},{11,1... | collective-permute-start | bytes 393224 | tf_op jit(solution)/shard_map/ppermute | solution.py:25
  56.7 5.1 %copy-start.5 = (bf16[4,128,128]{2,1,0:T(8,128)(2,1)S(1)}, bf16[4,128,128]{2,1,0:T(8,128)(2,1)}, u32[]{:S(2)}) copy-start(bf16[4,128,128]{2,1,0:T(8,128)(2,1)} %param.16) | copy-start | bytes 393220
  61.8 3.8 %copy-start.6 = (f32[1536]{0:T(1024)S(1)}, f32[1536]{0:T(1024)}, u32[]{:S(2)}) copy-start(f32[1536]{0:T(1024)} %param.13) | copy-start | bytes 18436
  65.6 4.6 %copy-start.3 = (bf16[12,128,1536]{2,1,0:T(8,128)(2,1)}, bf16[12,128,1536]{2,1,0:T(8,128)(2,1)S(1)}, u32[]{:S(2)}) copy-start(bf16[12,128,1536]{2,1,0:T(8,128)(2,1)S(1)} %get-tuple-element.6.v_ref) | copy-start | bytes 14155780
  65.6 4.5 %copy-start.1 = (s32[4]{0:T(128)S(1)}, s32[4]{0:T(128)}, u32[]{:S(2)}) copy-start(s32[4]{0:T(128)} %nb_ref.1) | copy-start | bytes 52
  65.6 116.4 %slice-start = ((s8[4718592]{0:T(1024)(128)(4,1)}), s8[4194304]{0:T(1024)(128)(4,1)S(1)}, s32[]{:S(2)}) async-start(s8[4718592]{0:T(1024)(128)(4,1)} %bitcast.11), calls=%async_computation.1 | async-start | bytes 8388608
  70.2 111.9 %copy-start.4 = (bf16[512,1536]{1,0:T(8,128)(2,1)S(1)}, bf16[512,1536]{1,0:T(8,128)(2,1)}, u32[]{:S(2)}) copy-start(bf16[512,1536]{1,0:T(8,128)(2,1)} %param.11) | copy-start | bytes 4718596
  70.2 111.9 %slice-start.1 = ((s8[4718592]{0:T(1024)(128)(4,1)}), s8[524288]{0:T(1024)(128)(4,1)S(1)}, s32[]{:S(2)}) async-start(s8[4718592]{0:T(1024)(128)(4,1)} %bitcast.11), calls=%async_computation.2 | async-start | bytes 1048576
  182.1 2.8 %copy-start.7 = (f32[1536]{0:T(1024)S(1)}, f32[1536]{0:T(1024)}, u32[]{:S(2)}) copy-start(f32[1536]{0:T(1024)} %param.14) | copy-start | bytes 18436
Sparse Core Ops, SparseCore 0:
  9.6 47.0 all-gather.1

commit v2 on v1

v2 whole, which is shorter than its diff:
```python
import functools
import math

import jax
import jax.numpy as jnp
from jax import lax
from jax.experimental import pallas as pl
from jax.experimental.pallas import tpu as pltpu
from jax.sharding import PartitionSpec as P

D = 1536
HD = 64
CH = 128
CELLS = 128
OBS = 128
MAXB = 6
LANES = 128


def padded(value, axis, width):
    peers, length = lax.axis_size(axis), value.shape[0]
    up = [(i, i + 1) for i in range(peers - 1)]
    down = [(j, i) for i, j in up]
    before = lax.ppermute(value[length - width:], axis, up)
    after = lax.ppermute(value[:width], axis, down)
    return jnp.concatenate([before, value, after], axis=0)


def normalize(values, gain):
    values = values.astype(jnp.float32)
    return values * lax.rsqrt(jnp.mean(values * values, axis=-1, keepdims=True) + 1e-06) * gain


def attend_kernel(ids_ref, nb_ref, cnt_ref, qt_ref, k_ref, vt_ref, o_ref, s_ref):
    tile = pl.program_id(0)
    used = nb_ref[tile]
    scale = 1.0 / math.sqrt(HD)
    row = lax.broadcasted_iota(jnp.int32, (LANES, 1), 0)
    low = row < HD
    wide = 2 * LANES
    for pair in range(D // LANES):
        rows = pl.ds(pair * LANES, LANES)
        qt = qt_ref[0, rows, :].astype(jnp.float32)
        q2 = jnp.concatenate(
            [jnp.where(low, qt, 0.0), jnp.where(low, 0.0, qt)], axis=1
        ).astype(jnp.bfloat16)

        def score_step(j, high):
            block = ids_ref[tile * MAXB + j]
            keys = k_ref[block, :, rows]
            s = jnp.dot(keys, q2, preferred_element_type=jnp.float32) * scale
            s = jnp.where(row < cnt_ref[block], s, -jnp.inf)
            s_ref[j] = s
            return jnp.maximum(high, jnp.max(s, axis=0, keepdims=True))

        high = lax.fori_loop(
            0, used, score_step, jnp.full((1, wide), -jnp.inf, jnp.float32)
        )

        def value_step(j, carry):
            total, acc = carry
            block = ids_ref[tile * MAXB + j]
            w = jnp.exp(s_ref[j] - high)
            total = total + jnp.sum(w, axis=0, keepdims=True)
            acc = acc + jnp.dot(
                vt_ref[block, rows, :], w.astype(jnp.bfloat16), preferred_element_type=jnp.float32
            )
            return total, acc

        total, acc = lax.fori_loop(
            0,
            used,
            value_step,
            (jnp.zeros((1, wide), jnp.float32), jnp.zeros((LANES, wide), jnp.float32)),
        )
        o_ref[0, pl.ds(pair * LANES, HD), :] = (acc[:HD, :LANES] / total[:, :LANES]).astype(
            jnp.bfloat16
        )
        o_ref[0, pl.ds(pair * LANES + HD, HD), :] = (
            acc[HD:, LANES:] / total[:, LANES:]
        ).astype(jnp.bfloat16)


def attend(local_ids, tile_blocks, counts, queries_t, keys, values_t):
    tiles = queries_t.shape[0]
    near = keys.shape[0]
    grid_spec = pltpu.PrefetchScalarGridSpec(
        num_scalar_prefetch=3,
        grid=(tiles,),
        in_specs=[
            pl.BlockSpec((1, D, CELLS), lambda t, *_: (t, 0, 0)),
            pl.BlockSpec((near, OBS, D), lambda t, *_: (0, 0, 0)),
            pl.BlockSpec((near, D, OBS), lambda t, *_: (0, 0, 0)),
        ],
        out_specs=pl.BlockSpec((1, D, CELLS), lambda t, *_: (t, 0, 0)),
        scratch_shapes=[pltpu.VMEM((MAXB, OBS, 2 * LANES), jnp.float32)],
    )
    return pl.pallas_call(
        attend_kernel,
        grid_spec=grid_spec,
        out_shape=jax.ShapeDtypeStruct(queries_t.shape, jnp.bfloat16),
        compiler_params=pltpu.CompilerParams(vmem_limit_bytes=48 * 1024 * 1024),
    )(local_ids.reshape(-1), tile_blocks, counts, queries_t, keys, values_t)


def body(
    latent,
    query_gain,
    key_gain,
    output_gain,
    output_weight,
    observations,
    panels,
    instrument,
    observed_count,
    footprint,
    tile_blocks,
):
    block_count = observations.shape[0]
    position = lax.axis_index("lat")
    first_block = (position - 1) * block_count
    all_blocks = instrument.shape[0]
    table = lax.all_gather(panels, "lat", axis=0, tiled=True)
    kinds = table.shape[0] // CH
    near_obs = padded(observations, "lat", block_count)
    near_count = near_obs.shape[0]
    near_ids = jnp.clip(first_block + jnp.arange(near_count, dtype=jnp.int32), 0, all_blocks - 1)
    near_kinds = instrument[near_ids]
    counts = observed_count[near_ids]
    near_panels = table.reshape(kinds, CH, D)[near_kinds]
    embedded = jnp.einsum(
        "boc,bcd->bod", near_obs, near_panels, preferred_element_type=jnp.float32
    ).astype(jnp.bfloat16)
    keys = normalize(embedded, key_gain).astype(jnp.bfloat16)
    tiles = latent.shape[0] // CELLS
    queries = (latent.astype(jnp.float32) * query_gain).astype(jnp.bfloat16)
    queries_t = jnp.swapaxes(queries.reshape(tiles, CELLS, D), 1, 2)
    local_ids = (footprint - first_block).astype(jnp.int32)
    attended_t = attend(
        local_ids, tile_blocks.astype(jnp.int32), counts, queries_t, keys, jnp.swapaxes(embedded, 1, 2)
    )
    projected = jnp.einsum(
        "tdq,de->tqe", attended_t, output_weight, preferred_element_type=jnp.float32
    ).reshape(tiles * CELLS, D)
    mixed = latent.astype(jnp.float32) + projected
    return normalize(mixed, output_gain).astype(jnp.bfloat16)


def solution(mesh):
    return jax.shard_map(
        body,
        mesh=mesh,
        in_specs=(
            P(("groups", "lat"), None),
            P(),
            P(),
            P(),
            P(),
            P(("groups", "lat"), None, None),
            P("lat", None),
            P("groups"),
            P("groups"),
            P(("groups", "lat"), None),
            P(("groups", "lat")),
        ),
        out_specs=P(("groups", "lat"), None),
        check_vma=False,
    )
```

time: 192 us -> 188 us (0.979)
  the two profiles are of different devices: /device:TPU:5 before, /device:TPU:24 now
where the time goes in v2:
time: 188 us; the launch traced here: 184 us
  Pallas kernels  93.5 us (50%)
  waiting for transfers between devices  36.7 us (20%)
  local copies, waits for them, and re-layouts  16.4 us (9%)
  between operations  13.5 us (7%)
  matrix products  9.15 us (5%)
  other arithmetic  8.17 us (4%)
  starting transfers between devices  6.47 us (3%)
    pallas_call x1, Pallas kernels, attend(): pl.pallas_call(attend_kernel, grid_spec=grid_spec, out_shape=jax.ShapeDty...  93.5 us
    all_gather x1, waiting for transfers between devices, body(): table = lax.all_gather(panels, 'lat', axis=0, tiled=True)  35.9 us
    convert_element_type x1, local copies, waits for them, and re-layouts, body(): keys = normalize(embedded, key_gain).astype(jnp.bfloat16)  6.74 us
    gather x1, local copies, waits for them, and re-layouts, body(): near_panels = table.reshape(kinds, CH, D)[near_kinds]  5.06 us
    dot_general x1, matrix products, body(): jnp.einsum('tdq,de->tqe', attended_t, output_weight, preferred_element_ty...  4.73 us
    ppermute x1, starting transfers between devices, padded(): after = lax.ppermute(value[:width], axis, down)  4.54 us
    dot_general x1, matrix products, body(): jnp.einsum('boc,bcd->bod', near_obs, near_panels, preferred_element_type=...  4.42 us
  transfers between devices with their start and end apart: 3, of which 1 were waited for; matrix products, arithmetic and copies ran while one was open for 5% of the time, Pallas kernels for 0%

profile of v2, /device:TPU:24, one launch (start us, length us, event | category | flops | bytes accessed | tf_op | source)
XLA Modules:
  0.0 183.9 jit_solution(9000844450839869389)
XLA Ops:
  6.5 0.7 all-gather.2.cloned.1.call-update
  7.3 1.9 %collective-permute-start = (bf16[4,128,128]{2,1,0:T(8,128)(2,1)}, bf16[4,128,128]{2,1,0:T(8,128)(2,1)S(1)}, u32[]{:S(2)}, u32[]{:S(2)}) collective-permute-start(bf16[4,128,128]{2,1,0:T(8,128)(2,1)} %param.16), channel_id=1, source_target_pairs={{0,1},{1,2},{2,3},{3,4},{4,5},{5,6},{6,7},{7,8},{8,9},{9,10},{10,1... | collective-permute-start | bytes 393224 | tf_op jit(solution)/shard_map/ppermute | solution.py:24
  9.2 4.5 %collective-permute-start.1 = (bf16[4,128,128]{2,1,0:T(8,128)(2,1)}, bf16[4,128,128]{2,1,0:T(8,128)(2,1)S(1)}, u32[]{:S(2)}, u32[]{:S(2)}) collective-permute-start(bf16[4,128,128]{2,1,0:T(8,128)(2,1)} %param.16), channel_id=1, source_target_pairs={{1,0},{2,1},{3,2},{4,3},{5,4},{6,5},{7,6},{8,7},{9,8},{10,9},{11,1... | collective-permute-start | bytes 393224 | tf_op jit(solution)/shard_map/ppermute | solution.py:25
  13.8 0.7 gather_fusion.1
  14.4 0.7 broadcast_subtract_fusion
  15.1 1.7 fusion.5
  16.8 0.7 gather_fusion
  17.5 0.1 reshape.63.ids_ref
  17.6 0.9 copy.15
  18.5 35.9 %all-gather.2.cloned.1.call-done = bf16[1024,1536]{1,0:T(8,128)(2,1)} async-done(((bf16[64,1536]{1,0:T(8,128)(2,1)}), bf16[1024,1536]{1,0:T(8,128)(2,1)}) %all-gather.2.cloned.1.call-update) | async-done | bytes 3145744 | tf_op jit(solution)/shard_map/all_gather | solution.py:123
  54.4 5.1 %gather_fusion.2 = bf16[12,128,1536]{2,1,0:T(8,128)(2,1)} fusion(bf16[8,128,1536]{2,1,0:T(8,128)(2,1)} %bitcast.23, s32[1024]{0:T(1024)S(1)} %pad_clamp_fusion), kind=kCustom, calls=%fused_computation.2 | custom fusion | bytes 9437232 | tf_op jit(solution)/shard_map/gather | solution.py:130
  59.5 0.0 collective-permute-done
  59.5 0.0 collective-permute-done.1
  59.5 4.4 %fusion = (f32[12,128]{1,0:T(8,128)S(1)}, bf16[12,128,1536]{1,2,0:T(8,128)(2,1)S(1)}) fusion(bf16[12,128,1536]{2,1,0:T(8,128)(2,1)} %gather_fusion.2, bf16[4,128,128]{2,1,0:T(8,128)(2,1)S(1)} %collective-permute-done.1, bf16[4,128,128]{2,1,0:T(8,128)(2,1)S(1)} %copy-done.5, bf16[4,128,128]{2,1,0:T(8,128)(2,1)S(1)} %collective-permute-done), kind=kOutput, calls=%fused_computation.5 | convolution fusion | flops 613808640 | bytes 9836544 | tf_op jit(solution)/shard_map/boc,bcd->bod/dot_general | solution.py:131
  64.0 2.1 %copy-done.3 = bf16[12,128,1536]{1,2,0:T(8,128)(2,1)} copy-done((bf16[12,128,1536]{1,2,0:T(8,128)(2,1)}, bf16[12,128,1536]{1,2,0:T(8,128)(2,1)S(1)}, u32[]{:S(2)}) %copy-start.3) | copy-done | bytes 4718616
  66.1 3.7 %fusion.2 = bf16[12,128,1536]{1,2,0:T(8,128)(2,1)} fusion(bf16[12,128,1536]{1,2,0:T(8,128)(2,1)S(1)} %get-tuple-element.6, f32[1536]{0:T(1024)S(1)} %copy-done.6, f32[12,128]{1,0:T(8,128)S(1)} %add_rsqrt_fusion), kind=kLoop, calls=%fused_computation.7 | loop fusion | flops 9437184 | bytes 9449472 | tf_op jit(solution)/shard_map/convert_element_type | solution.py:134
  69.7 6.7 %copy.17.k_ref = bf16[12,128,1536]{2,1,0:T(8,128)(2,1)} copy(bf16[12,128,1536]{1,2,0:T(8,128)(2,1)} %fusion.2) | data formatting | bytes 9437184 | tf_op jit(solution)/shard_map/convert_element_type | solution.py:134
  76.5 93.5 %shard_map.109 = bf16[4,1536,128]{2,1,0:T(8,128)(2,1)S(1)} custom-call(s32[24]{0:T(128)S(1)} %reshape.63.ids_ref, s32[4]{0:T(128)S(1)} %copy-done.1, s32[12]{0:T(128)S(1)} %gather_fusion, bf16[4,1536,128]{2,1,0:T(8,128)(2,1)S(1)} %bitcast.21, bf16[12,128,1536]{2,1,0:T(8,128)(2,1)} %copy.17.k_ref, bf16[12,1536,128]{2,1,0:T(8,128)(2,1)} %bitcast.22), custom_call_target="tpu_custom_call" | custom-call | tf_op jit(solution)/shard_map/pallas_call | solution.py:98
  170.0 0.0 copy-start.4
  170.0 4.7 %fusion.3 = f32[4,128,1536]{2,1,0:T(8,128)S(1)} fusion(bf16[4,1536,128]{2,1,0:T(8,128)(2,1)S(1)} %shard_map.109, bf16[1536,1536]{1,0:T(8,128)(2,1)} %param.15), kind=kOutput, calls=%fused_computation.8 | convolution fusion | flops 2415919104 | bytes 9437184 | tf_op jit(solution)/shard_map/tdq,de->tqe/dot_general | solution.py:142
  174.8 0.0 copy-start.7
  174.8 0.5 multiply_reduce_fusion
  175.3 0.2 copy-done.7
  175.5 1.6 multiply_convert_fusion
  (19 shorter events, 0.1 us)
Async XLA Ops:
  6.5 7.2 %copy-start = (s32[64]{0:T(128)S(1)}, s32[64]{0:T(128)}, u32[]{:S(2)}) copy-start(s32[64]{0:T(128)} %param.18) | copy-start | bytes 772
  6.5 10.3 %copy-start.2 = (s32[64]{0:T(128)S(1)}, s32[64]{0:T(128)}, u32[]{:S(2)}) copy-start(s32[64]{0:T(128)} %param.19) | copy-start | bytes 772
  6.5 47.9 %all-gather.2.cloned.1.call-start = ((), (), s32[]{:S(2)}) async-start(), calls=%async_computation | async-start | bytes 3342336 | tf_op jit(solution)/shard_map/all_gather | solution.py:123
  7.3 52.2 %collective-permute-start = (bf16[4,128,128]{2,1,0:T(8,128)(2,1)}, bf16[4,128,128]{2,1,0:T(8,128)(2,1)S(1)}, u32[]{:S(2)}, u32[]{:S(2)}) collective-permute-start(bf16[4,128,128]{2,1,0:T(8,128)(2,1)} %param.16), channel_id=1, source_target_pairs={{0,1},{1,2},{2,3},{3,4},{4,5},{5,6},{6,7},{7,8},{8,9},{9,10},{10,1... | collective-permute-start | bytes 393224 | tf_op jit(solution)/shard_map/ppermute | solution.py:24
  9.2 50.3 %collective-permute-start.1 = (bf16[4,128,128]{2,1,0:T(8,128)(2,1)}, bf16[4,128,128]{2,1,0:T(8,128)(2,1)S(1)}, u32[]{:S(2)}, u32[]{:S(2)}) collective-permute-start(bf16[4,128,128]{2,1,0:T(8,128)(2,1)} %param.16), channel_id=1, source_target_pairs={{1,0},{2,1},{3,2},{4,3},{5,4},{6,5},{7,6},{8,7},{9,8},{10,9},{11,1... | collective-permute-start | bytes 393224 | tf_op jit(solution)/shard_map/ppermute | solution.py:25
  54.4 5.1 %copy-start.5 = (bf16[4,128,128]{2,1,0:T(8,128)(2,1)S(1)}, bf16[4,128,128]{2,1,0:T(8,128)(2,1)}, u32[]{:S(2)}) copy-start(bf16[4,128,128]{2,1,0:T(8,128)(2,1)} %param.16) | copy-start | bytes 393220
  59.5 6.6 %copy-start.6 = (f32[1536]{0:T(1024)S(1)}, f32[1536]{0:T(1024)}, u32[]{:S(2)}) copy-start(f32[1536]{0:T(1024)} %param.13) | copy-start | bytes 18436
  63.9 2.1 %copy-start.3 = (bf16[12,128,1536]{1,2,0:T(8,128)(2,1)}, bf16[12,128,1536]{1,2,0:T(8,128)(2,1)S(1)}, u32[]{:S(2)}) copy-start(bf16[12,128,1536]{1,2,0:T(8,128)(2,1)S(1)} %get-tuple-element.6) | copy-start | bytes 14155780
  69.7 6.7 %copy-start.1 = (s32[4]{0:T(128)S(1)}, s32[4]{0:T(128)}, u32[]{:S(2)}) copy-start(s32[4]{0:T(128)} %nb_ref.1) | copy-start | bytes 52
  170.0 4.8 %copy-start.4 = (bf16[512,1536]{1,0:T(8,128)(2,1)S(1)}, bf16[512,1536]{1,0:T(8,128)(2,1)}, u32[]{:S(2)}) copy-start(bf16[512,1536]{1,0:T(8,128)(2,1)} %param.11) | copy-start | bytes 4718596
  174.8 0.7 copy-start.7
Sparse Core Ops, SparseCore 0:
  9.6 44.7 all-gather.1

commit v3 on v2

--- a/solution.py
+++ b/solution.py
@@ -45,34 +45,23 @@
             [jnp.where(low, qt, 0.0), jnp.where(low, 0.0, qt)], axis=1
         ).astype(jnp.bfloat16)
 
-        def score_step(j, high):
+        high = jnp.full((1, wide), -jnp.inf, jnp.float32)
+        for j in range(MAXB):
             block = ids_ref[tile * MAXB + j]
             keys = k_ref[block, :, rows]
             s = jnp.dot(keys, q2, preferred_element_type=jnp.float32) * scale
-            s = jnp.where(row < cnt_ref[block], s, -jnp.inf)
+            s = jnp.where((row < cnt_ref[block]) & (j < used), s, -jnp.inf)
             s_ref[j] = s
-            return jnp.maximum(high, jnp.max(s, axis=0, keepdims=True))
-
-        high = lax.fori_loop(
-            0, used, score_step, jnp.full((1, wide), -jnp.inf, jnp.float32)
-        )
-
-        def value_step(j, carry):
-            total, acc = carry
+            high = jnp.maximum(high, jnp.max(s, axis=0, keepdims=True))
+        total = jnp.zeros((1, wide), jnp.float32)
+        acc = jnp.zeros((LANES, wide), jnp.float32)
+        for j in range(MAXB):
             block = ids_ref[tile * MAXB + j]
             w = jnp.exp(s_ref[j] - high)
             total = total + jnp.sum(w, axis=0, keepdims=True)
             acc = acc + jnp.dot(
                 vt_ref[block, rows, :], w.astype(jnp.bfloat16), preferred_element_type=jnp.float32
             )
-            return total, acc
-
-        total, acc = lax.fori_loop(
-            0,
-            used,
-            value_step,
-            (jnp.zeros((1, wide), jnp.float32), jnp.zeros((LANES, wide), jnp.float32)),
-        )
         o_ref[0, pl.ds(pair * LANES, HD), :] = (acc[:HD, :LANES] / total[:, :LANES]).astype(
             jnp.bfloat16
         )
@@ -135,7 +124,7 @@
     tiles = latent.shape[0] // CELLS
     queries = (latent.astype(jnp.float32) * query_gain).astype(jnp.bfloat16)
     queries_t = jnp.swapaxes(queries.reshape(tiles, CELLS, D), 1, 2)
-    local_ids = (footprint - first_block).astype(jnp.int32)
+    local_ids = jnp.clip(footprint - first_block, 0, near_count - 1).astype(jnp.int32)
     attended_t = attend(
         local_ids, tile_blocks.astype(jnp.int32), counts, queries_t, keys, jnp.swapaxes(embedded, 1, 2)
     )

time: 188 us -> 116 us (0.62)
  the two profiles are of different devices: /device:TPU:24 before, /device:TPU:5 now
where the time goes in v3:
time: 116 us; the launch traced here: 115 us
  waiting for transfers between devices  39.8 us (34%)
  Pallas kernels  22.2 us (19%)
  local copies, waits for them, and re-layouts  16.4 us (14%)
  between operations  13.5 us (12%)
  matrix products  9.15 us (8%)
  other arithmetic  8.17 us (7%)
  starting transfers between devices  5.61 us (5%)
    all_gather x1, waiting for transfers between devices, body(): table = lax.all_gather(panels, 'lat', axis=0, tiled=True)  39.1 us
    pallas_call x1, Pallas kernels, attend(): pl.pallas_call(attend_kernel, grid_spec=grid_spec, out_shape=jax.ShapeDty...  22.2 us
    convert_element_type x1, local copies, waits for them, and re-layouts, body(): keys = normalize(embedded, key_gain).astype(jnp.bfloat16)  6.74 us
    gather x1, local copies, waits for them, and re-layouts, body(): near_panels = table.reshape(kinds, CH, D)[near_kinds]  5.06 us
    dot_general x1, matrix products, body(): jnp.einsum('tdq,de->tqe', attended_t, output_weight, preferred_element_ty...  4.73 us
    dot_general x1, matrix products, body(): jnp.einsum('boc,bcd->bod', near_obs, near_panels, preferred_element_type=...  4.42 us
    ppermute x1, starting transfers between devices, padded(): before = lax.ppermute(value[length - width:], axis, up)  3.68 us
    convert_element_type x1, other arithmetic, body(): keys = normalize(embedded, key_gain).astype(jnp.bfloat16)  3.66 us
  transfers between devices with their start and end apart: 3, of which 1 were waited for; matrix products, arithmetic and copies ran while one was open for 8% of the time, Pallas kernels for 0%

profile of v3, /device:TPU:5, one launch (start us, length us, event | category | flops | bytes accessed | tf_op | source)
XLA Modules:
  0.0 114.9 jit_solution(12149942192004325298)
XLA Ops:
  6.5 0.7 all-gather.2.cloned.1.call-update
  7.3 3.7 %collective-permute-start = (bf16[4,128,128]{2,1,0:T(8,128)(2,1)}, bf16[4,128,128]{2,1,0:T(8,128)(2,1)S(1)}, u32[]{:S(2)}, u32[]{:S(2)}) collective-permute-start(bf16[4,128,128]{2,1,0:T(8,128)(2,1)} %param.16), channel_id=1, source_target_pairs={{0,1},{1,2},{2,3},{3,4},{4,5},{5,6},{6,7},{7,8},{8,9},{9,10},{10,1... | collective-permute-start | bytes 393224 | tf_op jit(solution)/shard_map/ppermute | solution.py:24
  11.0 1.9 %collective-permute-start.1 = (bf16[4,128,128]{2,1,0:T(8,128)(2,1)}, bf16[4,128,128]{2,1,0:T(8,128)(2,1)S(1)}, u32[]{:S(2)}, u32[]{:S(2)}) collective-permute-start(bf16[4,128,128]{2,1,0:T(8,128)(2,1)} %param.16), channel_id=1, source_target_pairs={{1,0},{2,1},{3,2},{4,3},{5,4},{6,5},{7,6},{8,7},{9,8},{10,9},{11,1... | collective-permute-start | bytes 393224 | tf_op jit(solution)/shard_map/ppermute | solution.py:25
  12.9 0.7 gather_fusion.1
  13.6 0.7 subtract_clamp_fusion
  14.3 1.7 %fusion.5 = bf16[512,1536]{1,0:T(8,128)(2,1)S(1)} fusion(bf16[512,1536]{1,0:T(8,128)(2,1)} %param.11, f32[1536]{0:T(1024)} %param.12), kind=kLoop, calls=%fused_computation.13 | loop fusion | flops 2359296 | bytes 3151872 | tf_op jit(solution)/shard_map/convert_element_type | solution.py:125
  16.0 0.7 gather_fusion
  16.6 0.1 reshape.63.ids_ref
  16.7 0.9 copy.15
  17.6 39.1 %all-gather.2.cloned.1.call-done = bf16[1024,1536]{1,0:T(8,128)(2,1)} async-done(((bf16[64,1536]{1,0:T(8,128)(2,1)}), bf16[1024,1536]{1,0:T(8,128)(2,1)}) %all-gather.2.cloned.1.call-update) | async-done | bytes 3145744 | tf_op jit(solution)/shard_map/all_gather | solution.py:112
  56.7 5.1 %gather_fusion.2 = bf16[12,128,1536]{2,1,0:T(8,128)(2,1)} fusion(bf16[8,128,1536]{2,1,0:T(8,128)(2,1)} %bitcast.23, s32[1024]{0:T(1024)S(1)} %pad_clamp_fusion), kind=kCustom, calls=%fused_computation.2 | custom fusion | bytes 9437232 | tf_op jit(solution)/shard_map/gather | solution.py:119
  61.8 0.0 collective-permute-done
  61.8 0.0 collective-permute-done.1
  61.8 4.4 %fusion = (f32[12,128]{1,0:T(8,128)S(1)}, bf16[12,128,1536]{1,2,0:T(8,128)(2,1)S(1)}) fusion(bf16[12,128,1536]{2,1,0:T(8,128)(2,1)} %gather_fusion.2, bf16[4,128,128]{2,1,0:T(8,128)(2,1)S(1)} %collective-permute-done.1, bf16[4,128,128]{2,1,0:T(8,128)(2,1)S(1)} %copy-done.5, bf16[4,128,128]{2,1,0:T(8,128)(2,1)S(1)} %collective-permute-done), kind=kOutput, calls=%fused_computation.5 | convolution fusion | flops 613808640 | bytes 9836544 | tf_op jit(solution)/shard_map/boc,bcd->bod/dot_general | solution.py:120
  66.2 2.1 %copy-done.3 = bf16[12,128,1536]{1,2,0:T(8,128)(2,1)} copy-done((bf16[12,128,1536]{1,2,0:T(8,128)(2,1)}, bf16[12,128,1536]{1,2,0:T(8,128)(2,1)S(1)}, u32[]{:S(2)}) %copy-start.3) | copy-done | bytes 4718616
  68.4 3.7 %fusion.2 = bf16[12,128,1536]{1,2,0:T(8,128)(2,1)} fusion(bf16[12,128,1536]{1,2,0:T(8,128)(2,1)S(1)} %get-tuple-element.6, f32[1536]{0:T(1024)S(1)} %copy-done.6, f32[12,128]{1,0:T(8,128)S(1)} %add_rsqrt_fusion), kind=kLoop, calls=%fused_computation.7 | loop fusion | flops 9437184 | bytes 9449472 | tf_op jit(solution)/shard_map/convert_element_type | solution.py:123
  72.0 6.7 %copy.17.k_ref = bf16[12,128,1536]{2,1,0:T(8,128)(2,1)} copy(bf16[12,128,1536]{1,2,0:T(8,128)(2,1)} %fusion.2) | data formatting | bytes 9437184 | tf_op jit(solution)/shard_map/convert_element_type | solution.py:123
  78.8 22.2 %shard_map.109 = bf16[4,1536,128]{2,1,0:T(8,128)(2,1)S(1)} custom-call(s32[24]{0:T(128)S(1)} %reshape.63.ids_ref, s32[4]{0:T(128)S(1)} %copy-done.1, s32[12]{0:T(128)S(1)} %gather_fusion, bf16[4,1536,128]{2,1,0:T(8,128)(2,1)S(1)} %bitcast.21, bf16[12,128,1536]{2,1,0:T(8,128)(2,1)} %copy.17.k_ref, bf16[12,1536,128]{2,1,0:T(8,128)(2,1)} %bitcast.22), custom_call_target="tpu_custom_call" | custom-call | tf_op jit(solution)/shard_map/pallas_call | solution.py:87
  101.0 0.0 copy-start.4
  101.0 4.7 %fusion.3 = f32[4,128,1536]{2,1,0:T(8,128)S(1)} fusion(bf16[4,1536,128]{2,1,0:T(8,128)(2,1)S(1)} %shard_map.109, bf16[1536,1536]{1,0:T(8,128)(2,1)} %param.15), kind=kOutput, calls=%fused_computation.8 | convolution fusion | flops 2415919104 | bytes 9437184 | tf_op jit(solution)/shard_map/tdq,de->tqe/dot_general | solution.py:131
  105.8 0.0 copy-start.7
  105.8 0.5 multiply_reduce_fusion
  106.3 0.2 copy-done.7
  106.5 1.6 %multiply_convert_fusion = bf16[512,1536]{1,0:T(8,128)(2,1)} fusion(f32[4,128,1536]{2,1,0:T(8,128)S(1)} %fusion.3, bf16[512,1536]{1,0:T(8,128)(2,1)S(1)} %copy-done.4, f32[1536]{0:T(1024)S(1)} %copy-done.7, f32[512]{0:T(512)S(1)} %add_rsqrt_fusion.1), kind=kLoop, calls=%fused_computation.14 | loop fusion | flops 3932160 | bytes 6299648 | tf_op jit(solution)/shard_map/convert_element_type | solution.py:135
  (19 shorter events, 0.1 us)
Async XLA Ops:
  6.5 6.4 %copy-start = (s32[64]{0:T(128)S(1)}, s32[64]{0:T(128)}, u32[]{:S(2)}) copy-start(s32[64]{0:T(128)} %param.18) | copy-start | bytes 772
  6.5 9.4 %copy-start.2 = (s32[64]{0:T(128)S(1)}, s32[64]{0:T(128)}, u32[]{:S(2)}) copy-start(s32[64]{0:T(128)} %param.19) | copy-start | bytes 772
  6.5 50.2 %all-gather.2.cloned.1.call-start = ((), (), s32[]{:S(2)}) async-start(), calls=%async_computation | async-start | bytes 3342336 | tf_op jit(solution)/shard_map/all_gather | solution.py:112
  7.3 54.5 %collective-permute-start = (bf16[4,128,128]{2,1,0:T(8,128)(2,1)}, bf16[4,128,128]{2,1,0:T(8,128)(2,1)S(1)}, u32[]{:S(2)}, u32[]{:S(2)}) collective-permute-start(bf16[4,128,128]{2,1,0:T(8,128)(2,1)} %param.16), channel_id=1, source_target_pairs={{0,1},{1,2},{2,3},{3,4},{4,5},{5,6},{6,7},{7,8},{8,9},{9,10},{10,1... | collective-permute-start | bytes 393224 | tf_op jit(solution)/shard_map/ppermute | solution.py:24
  11.0 50.8 %collective-permute-start.1 = (bf16[4,128,128]{2,1,0:T(8,128)(2,1)}, bf16[4,128,128]{2,1,0:T(8,128)(2,1)S(1)}, u32[]{:S(2)}, u32[]{:S(2)}) collective-permute-start(bf16[4,128,128]{2,1,0:T(8,128)(2,1)} %param.16), channel_id=1, source_target_pairs={{1,0},{2,1},{3,2},{4,3},{5,4},{6,5},{7,6},{8,7},{9,8},{10,9},{11,1... | collective-permute-start | bytes 393224 | tf_op jit(solution)/shard_map/ppermute | solution.py:25
  56.7 5.1 %copy-start.5 = (bf16[4,128,128]{2,1,0:T(8,128)(2,1)S(1)}, bf16[4,128,128]{2,1,0:T(8,128)(2,1)}, u32[]{:S(2)}) copy-start(bf16[4,128,128]{2,1,0:T(8,128)(2,1)} %param.16) | copy-start | bytes 393220
  61.8 6.6 %copy-start.6 = (f32[1536]{0:T(1024)S(1)}, f32[1536]{0:T(1024)}, u32[]{:S(2)}) copy-start(f32[1536]{0:T(1024)} %param.13) | copy-start | bytes 18436
  66.2 2.1 %copy-start.3 = (bf16[12,128,1536]{1,2,0:T(8,128)(2,1)}, bf16[12,128,1536]{1,2,0:T(8,128)(2,1)S(1)}, u32[]{:S(2)}) copy-start(bf16[12,128,1536]{1,2,0:T(8,128)(2,1)S(1)} %get-tuple-element.6) | copy-start | bytes 14155780
  72.0 6.7 %copy-start.1 = (s32[4]{0:T(128)S(1)}, s32[4]{0:T(128)}, u32[]{:S(2)}) copy-start(s32[4]{0:T(128)} %nb_ref.1) | copy-start | bytes 52
  101.0 4.8 %copy-start.4 = (bf16[512,1536]{1,0:T(8,128)(2,1)S(1)}, bf16[512,1536]{1,0:T(8,128)(2,1)}, u32[]{:S(2)}) copy-start(bf16[512,1536]{1,0:T(8,128)(2,1)} %param.11) | copy-start | bytes 4718596
  105.8 0.7 copy-start.7
Sparse Core Ops, SparseCore 0:
  9.6 47.0 all-gather.1

commit v4 on v3

--- a/solution.py
+++ b/solution.py
@@ -70,6 +70,39 @@
         ).astype(jnp.bfloat16)
 
 
+def embed_kernel(kinds_ref, obs_ref, panel_ref, gain_ref, k_ref, vt_ref):
+    embedded = jnp.dot(obs_ref[0], panel_ref[...], preferred_element_type=jnp.float32)
+    embedded = embedded.astype(jnp.bfloat16).astype(jnp.float32)
+    scale = lax.rsqrt(jnp.mean(embedded * embedded, axis=1, keepdims=True) + 1e-06)
+    k_ref[0] = (embedded * scale * gain_ref[...]).astype(jnp.bfloat16)
+    vt_ref[0] = embedded.T.astype(jnp.bfloat16)
+
+
+def embed(kinds, near_obs, table, key_gain):
+    near = near_obs.shape[0]
+    grid_spec = pltpu.PrefetchScalarGridSpec(
+        num_scalar_prefetch=1,
+        grid=(near,),
+        in_specs=[
+            pl.BlockSpec((1, OBS, CH), lambda b, kinds: (b, 0, 0)),
+            pl.BlockSpec((CH, D), lambda b, kinds: (kinds[b], 0)),
+            pl.BlockSpec((1, D), lambda b, kinds: (0, 0)),
+        ],
+        out_specs=[
+            pl.BlockSpec((1, OBS, D), lambda b, kinds: (b, 0, 0)),
+            pl.BlockSpec((1, D, OBS), lambda b, kinds: (b, 0, 0)),
+        ],
+    )
+    return pl.pallas_call(
+        embed_kernel,
+        grid_spec=grid_spec,
+        out_shape=[
+            jax.ShapeDtypeStruct((near, OBS, D), jnp.bfloat16),
+            jax.ShapeDtypeStruct((near, D, OBS), jnp.bfloat16),
+        ],
+    )(kinds, near_obs, table, key_gain.reshape(1, D))
+
+
 def attend(local_ids, tile_blocks, counts, queries_t, keys, values_t):
     tiles = queries_t.shape[0]
     near = keys.shape[0]
@@ -116,17 +149,14 @@
     near_ids = jnp.clip(first_block + jnp.arange(near_count, dtype=jnp.int32), 0, all_blocks - 1)
     near_kinds = instrument[near_ids]
     counts = observed_count[near_ids]
-    near_panels = table.reshape(kinds, CH, D)[near_kinds]
-    embedded = jnp.einsum(
-        "boc,bcd->bod", near_obs, near_panels, preferred_element_type=jnp.float32
-    ).astype(jnp.bfloat16)
-    keys = normalize(embedded, key_gain).astype(jnp.bfloat16)
+    near_kinds = jnp.clip(near_kinds, 0, kinds - 1).astype(jnp.int32)
+    keys, values_t = embed(near_kinds, near_obs, table, key_gain.astype(jnp.float32))
     tiles = latent.shape[0] // CELLS
     queries = (latent.astype(jnp.float32) * query_gain).astype(jnp.bfloat16)
     queries_t = jnp.swapaxes(queries.reshape(tiles, CELLS, D), 1, 2)
     local_ids = jnp.clip(footprint - first_block, 0, near_count - 1).astype(jnp.int32)
     attended_t = attend(
-        local_ids, tile_blocks.astype(jnp.int32), counts, queries_t, keys, jnp.swapaxes(embedded, 1, 2)
+        local_ids, tile_blocks.astype(jnp.int32), counts, queries_t, keys, values_t
     )
     projected = jnp.einsum(
         "tdq,de->tqe", attended_t, output_weight, preferred_element_type=jnp.float32

time: 116 us -> 107 us (0.922)
  Pallas kernels: 22.2 us -> 34.2 us
  local copies, waits for them, and re-layouts: 16.4 us -> 4.98 us
  waiting for transfers between devices: 39.8 us -> 35.3 us
  matrix products: 9.15 us -> 4.73 us
  other arithmetic: 8.17 us -> 6.55 us
    pallas_call x0 -> x1, Pallas kernels: none -> 12 us  [embed(): pl.pallas_call(embed_kernel, grid_spec=grid_spec, out_shape=[jax.ShapeDty...]
    convert_element_type x1 -> x0, local copies, waits for them, and re-layouts: 6.74 us -> none  [body(): keys = normalize(embedded, key_gain).astype(jnp.bfloat16)]
    gather x1 -> x0, local copies, waits for them, and re-layouts: 5.06 us -> none  [body(): near_panels = table.reshape(kinds, CH, D)[near_kinds]]
    all_gather x1, waiting for transfers between devices: 39.1 us -> 34.6 us  [body(): table = lax.all_gather(panels, 'lat', axis=0, tiled=True)]
    dot_general x1 -> x0, matrix products: 4.42 us -> none  [body(): jnp.einsum('boc,bcd->bod', near_obs, near_panels, preferred_element_type=...]
    convert_element_type x1 -> x0, other arithmetic: 3.66 us -> none  [body(): keys = normalize(embedded, key_gain).astype(jnp.bfloat16)]
    unnamed x16 -> x10, local copies, waits for them, and re-layouts: 2.34 us -> 0.22 us
    reshape x0 -> x1, local copies, waits for them, and re-layouts: none -> 1.29 us  [embed(): key_gain.reshape(1, D)]
  transfers between devices with their start and end apart: 3 -> 3, of which waited for: 1 -> 1; matrix products, arithmetic and copies ran while one was open for 8% -> 9% of each run, Pallas kernels for 0% -> 0%
where the time goes in v4:
time: 107 us; the launch traced here: 105 us
  waiting for transfers between devices  35.3 us (33%)
  Pallas kernels  34.2 us (32%)
  between operations  13.5 us (13%)
  other arithmetic  6.55 us (6%)
  starting transfers between devices  5.61 us (5%)
  local copies, waits for them, and re-layouts  4.98 us (5%)
  matrix products  4.73 us (4%)
    all_gather x1, waiting for transfers between devices, body(): table = lax.all_gather(panels, 'lat', axis=0, tiled=True)  34.6 us
    pallas_call x1, Pallas kernels, attend(): pl.pallas_call(attend_kernel, grid_spec=grid_spec, out_shape=jax.ShapeDty...  22.2 us
    pallas_call x1, Pallas kernels, embed(): pl.pallas_call(embed_kernel, grid_spec=grid_spec, out_shape=[jax.ShapeDty...  12 us
    dot_general x1, matrix products, body(): jnp.einsum('tdq,de->tqe', attended_t, output_weight, preferred_element_ty...  4.73 us
    ppermute x1, starting transfers between devices, padded(): before = lax.ppermute(value[length - width:], axis, up)  3.68 us
  transfers between devices with their start and end apart: 3, of which 1 were waited for; matrix products, arithmetic and copies ran while one was open for 9% of the time, Pallas kernels for 0%

profile of v4, /device:TPU:5, one launch (start us, length us, event | category | flops | bytes accessed | tf_op | source)
XLA Modules:
  0.0 104.9 jit_solution(7030350396589300856)
XLA Ops:
  6.5 0.7 all-gather.2.cloned.1.call-update
  7.3 3.7 %collective-permute-start = (bf16[4,128,128]{2,1,0:T(8,128)(2,1)}, bf16[4,128,128]{2,1,0:T(8,128)(2,1)S(1)}, u32[]{:S(2)}, u32[]{:S(2)}) collective-permute-start(bf16[4,128,128]{2,1,0:T(8,128)(2,1)} %param.16), channel_id=1, source_target_pairs={{0,1},{1,2},{2,3},{3,4},{4,5},{5,6},{6,7},{7,8},{8,9},{9,10},{10,1... | collective-permute-start | bytes 393224 | tf_op jit(solution)/shard_map/ppermute | solution.py:24
  10.9 1.9 %collective-permute-start.1 = (bf16[4,128,128]{2,1,0:T(8,128)(2,1)}, bf16[4,128,128]{2,1,0:T(8,128)(2,1)S(1)}, u32[]{:S(2)}, u32[]{:S(2)}) collective-permute-start(bf16[4,128,128]{2,1,0:T(8,128)(2,1)} %param.16), channel_id=1, source_target_pairs={{1,0},{2,1},{3,2},{4,3},{5,4},{6,5},{7,6},{8,7},{9,8},{10,9},{11,1... | collective-permute-start | bytes 393224 | tf_op jit(solution)/shard_map/ppermute | solution.py:25
  12.9 1.3 %reshape.43.gain_ref = f32[1,1536]{1,0:T(1,128)} reshape(f32[1536]{0:T(1024)} %param.13) | data formatting | bytes 12288 | tf_op jit(solution)/shard_map/reshape | solution.py:103
  14.2 1.2 %gather_fusion.1 = s32[12]{0:T(128)} fusion(s32[64]{0:T(128)S(1)} %copy-done, s32[1024]{0:T(1024)S(1)} %pad_clamp_fusion), kind=kCustom, calls=%fused_computation.1 | custom fusion | bytes 144 | tf_op jit(solution)/shard_map/gather | solution.py:150
  15.4 1.3 %gather_fusion = s32[12]{0:T(128)S(1)} fusion(s32[64]{0:T(128)} %param.19, s32[1024]{0:T(1024)S(1)} %pad_clamp_fusion), kind=kCustom, calls=%fused_computation | custom fusion | bytes 144 | tf_op jit(solution)/shard_map/gather | solution.py:151
  16.7 0.7 subtract_clamp_fusion
  17.4 0.1 reshape.41.ids_ref
  17.5 1.7 %fusion.2 = bf16[512,1536]{1,0:T(8,128)(2,1)S(1)} fusion(bf16[512,1536]{1,0:T(8,128)(2,1)} %param.11, f32[1536]{0:T(1024)} %param.12), kind=kLoop, calls=%fused_computation.6 | loop fusion | flops 2359296 | bytes 3151872 | tf_op jit(solution)/shard_map/convert_element_type | solution.py:155
  19.2 0.0 copy-start.1
  19.2 0.9 copy.13
  20.1 1.2 %broadcast_clamp_fusion.kinds_ref = s32[12]{0:T(128)} fusion(s32[12]{0:T(128)} %gather_fusion.1), kind=kLoop, calls=%fused_computation.15 | loop fusion | flops 12 | bytes 96 | tf_op jit(solution)/shard_map/jit(clip)/min | solution.py:152
  21.3 0.0 collective-permute-done
  21.3 0.0 collective-permute-done.1
  21.3 0.8 pad_maximum_fusion.obs_ref
  22.1 34.6 %all-gather.2.cloned.1.call-done.panel_ref = bf16[1024,1536]{1,0:T(8,128)(2,1)} async-done(((bf16[64,1536]{1,0:T(8,128)(2,1)}), bf16[1024,1536]{1,0:T(8,128)(2,1)}) %all-gather.2.cloned.1.call-update) | async-done | bytes 3145744 | tf_op jit(solution)/shard_map/all_gather | solution.py:145
  56.7 12.0 %shard_map.109 = (bf16[12,128,1536]{2,1,0:T(8,128)(2,1)}, bf16[12,1536,128]{2,1,0:T(8,128)(2,1)}) custom-call(s32[12]{0:T(128)} %broadcast_clamp_fusion.kinds_ref, bf16[12,128,128]{2,1,0:T(8,128)(2,1)} %pad_maximum_fusion.obs_ref, bf16[1024,1536]{1,0:T(8,128)(2,1)} %all-gather.2.cloned.1.call-done.panel_ref, f32[1,1536]{1,0:T(1,128)} %reshape.43.gain_ref), custom_call_target="tpu_custom_call" | custom-call | tf_op jit(solution)/shard_map/pallas_call | solution.py:96
  68.7 22.2 %shard_map.110 = bf16[4,1536,128]{2,1,0:T(8,128)(2,1)S(1)} custom-call(s32[24]{0:T(128)S(1)} %reshape.41.ids_ref, s32[4]{0:T(128)S(1)} %copy-done.1, s32[12]{0:T(128)S(1)} %gather_fusion, bf16[4,1536,128]{2,1,0:T(8,128)(2,1)S(1)} %bitcast.14, bf16[12,128,1536]{2,1,0:T(8,128)(2,1)} %get-tuple-element.7.k_ref, bf16[12,1536,128]{2,1,0:T(8,128)(2,1)} %get-tuple-element.8.vt_ref), custom_call_target="tpu_custom_call" | custom-call | tf_op jit(solution)/shard_map/pallas_call | solution.py:120
  91.0 0.0 copy-start.2
  91.0 4.7 %fusion = f32[4,128,1536]{2,1,0:T(8,128)S(1)} fusion(bf16[4,1536,128]{2,1,0:T(8,128)(2,1)S(1)} %shard_map.110, bf16[1536,1536]{1,0:T(8,128)(2,1)} %param.15), kind=kOutput, calls=%fused_computation.2 | convolution fusion | flops 2415919104 | bytes 9437184 | tf_op jit(solution)/shard_map/tdq,de->tqe/dot_general | solution.py:161
  95.7 0.0 copy-start.4
  95.7 0.5 multiply_reduce_fusion
  96.2 0.2 copy-done.4
  96.4 1.6 %multiply_convert_fusion = bf16[512,1536]{1,0:T(8,128)(2,1)} fusion(f32[4,128,1536]{2,1,0:T(8,128)S(1)} %fusion, bf16[512,1536]{1,0:T(8,128)(2,1)S(1)} %copy-done.2, f32[1536]{0:T(1024)S(1)} %copy-done.4, f32[512]{0:T(512)S(1)} %add_rsqrt_fusion), kind=kLoop, calls=%fused_computation.7 | loop fusion | flops 3932160 | bytes 6299648 | tf_op jit(solution)/shard_map/convert_element_type | solution.py:165
  (10 shorter events, 0.0 us)
Async XLA Ops:
  6.5 7.7 %copy-start = (s32[64]{0:T(128)S(1)}, s32[64]{0:T(128)}, u32[]{:S(2)}) copy-start(s32[64]{0:T(128)} %param.18) | copy-start | bytes 772
  6.5 50.2 %all-gather.2.cloned.1.call-start = ((), (), s32[]{:S(2)}) async-start(), calls=%async_computation | async-start | bytes 3342336 | tf_op jit(solution)/shard_map/all_gather | solution.py:145
  7.3 14.1 %collective-permute-start = (bf16[4,128,128]{2,1,0:T(8,128)(2,1)}, bf16[4,128,128]{2,1,0:T(8,128)(2,1)S(1)}, u32[]{:S(2)}, u32[]{:S(2)}) collective-permute-start(bf16[4,128,128]{2,1,0:T(8,128)(2,1)} %param.16), channel_id=1, source_target_pairs={{0,1},{1,2},{2,3},{3,4},{4,5},{5,6},{6,7},{7,8},{8,9},{9,10},{10,1... | collective-permute-start | bytes 393224 | tf_op jit(solution)/shard_map/ppermute | solution.py:24
  10.9 10.4 %collective-permute-start.1 = (bf16[4,128,128]{2,1,0:T(8,128)(2,1)}, bf16[4,128,128]{2,1,0:T(8,128)(2,1)S(1)}, u32[]{:S(2)}, u32[]{:S(2)}) collective-permute-start(bf16[4,128,128]{2,1,0:T(8,128)(2,1)} %param.16), channel_id=1, source_target_pairs={{1,0},{2,1},{3,2},{4,3},{5,4},{6,5},{7,6},{8,7},{9,8},{10,9},{11,1... | collective-permute-start | bytes 393224 | tf_op jit(solution)/shard_map/ppermute | solution.py:25
  17.5 3.9 %copy-start.3 = (bf16[4,128,128]{2,1,0:T(8,128)(2,1)S(1)}, bf16[4,128,128]{2,1,0:T(8,128)(2,1)}, u32[]{:S(2)}) copy-start(bf16[4,128,128]{2,1,0:T(8,128)(2,1)} %param.16) | copy-start | bytes 393220
  19.2 49.5 %copy-start.1 = (s32[4]{0:T(128)S(1)}, s32[4]{0:T(128)}, u32[]{:S(2)}) copy-start(s32[4]{0:T(128)} %nb_ref.1) | copy-start | bytes 52
  91.0 4.8 %copy-start.2 = (bf16[512,1536]{1,0:T(8,128)(2,1)S(1)}, bf16[512,1536]{1,0:T(8,128)(2,1)}, u32[]{:S(2)}) copy-start(bf16[512,1536]{1,0:T(8,128)(2,1)} %param.11) | copy-start | bytes 4718596
  95.7 0.7 copy-start.4
Sparse Core Ops, SparseCore 0:
  9.6 47.0 all-gather.1

commit v5 on v4

--- a/solution.py
+++ b/solution.py
@@ -31,7 +31,7 @@
     return values * lax.rsqrt(jnp.mean(values * values, axis=-1, keepdims=True) + 1e-06) * gain
 
 
-def attend_kernel(ids_ref, nb_ref, cnt_ref, qt_ref, k_ref, vt_ref, o_ref, s_ref):
+def attend_kernel(ids_ref, nb_ref, cnt_ref, qt_ref, k_ref, v_ref, o_ref, s_ref):
     tile = pl.program_id(0)
     used = nb_ref[tile]
     scale = 1.0 / math.sqrt(HD)
@@ -54,20 +54,23 @@
             s_ref[j] = s
             high = jnp.maximum(high, jnp.max(s, axis=0, keepdims=True))
         total = jnp.zeros((1, wide), jnp.float32)
-        acc = jnp.zeros((LANES, wide), jnp.float32)
+        acc = jnp.zeros((wide, LANES), jnp.float32)
         for j in range(MAXB):
             block = ids_ref[tile * MAXB + j]
             w = jnp.exp(s_ref[j] - high)
             total = total + jnp.sum(w, axis=0, keepdims=True)
-            acc = acc + jnp.dot(
-                vt_ref[block, rows, :], w.astype(jnp.bfloat16), preferred_element_type=jnp.float32
+            acc = acc + lax.dot_general(
+                w.astype(jnp.bfloat16),
+                v_ref[block, :, rows],
+                (((0,), (0,)), ((), ())),
+                preferred_element_type=jnp.float32,
             )
-        o_ref[0, pl.ds(pair * LANES, HD), :] = (acc[:HD, :LANES] / total[:, :LANES]).astype(
-            jnp.bfloat16
+        total = jnp.broadcast_to(total, (8, wide)).T[:, :1]
+        lane = lax.broadcasted_iota(jnp.int32, (1, LANES), 1)
+        out = jnp.where(
+            lane < HD, acc[:LANES] / total[:LANES], acc[LANES:] / total[LANES:]
         )
-        o_ref[0, pl.ds(pair * LANES + HD, HD), :] = (
-            acc[HD:, LANES:] / total[:, LANES:]
-        ).astype(jnp.bfloat16)
+        o_ref[:, rows] = out.astype(jnp.bfloat16)
 
 
 def embed_kernel(kinds_ref, obs_ref, panel_ref, gain_ref, k_ref, vt_ref):
@@ -75,7 +78,7 @@
     embedded = embedded.astype(jnp.bfloat16).astype(jnp.float32)
     scale = lax.rsqrt(jnp.mean(embedded * embedded, axis=1, keepdims=True) + 1e-06)
     k_ref[0] = (embedded * scale * gain_ref[...]).astype(jnp.bfloat16)
-    vt_ref[0] = embedded.T.astype(jnp.bfloat16)
+    vt_ref[0] = embedded.astype(jnp.bfloat16)
 
 
 def embed(kinds, near_obs, table, key_gain):
@@ -90,7 +93,7 @@
         ],
         out_specs=[
             pl.BlockSpec((1, OBS, D), lambda b, kinds: (b, 0, 0)),
-            pl.BlockSpec((1, D, OBS), lambda b, kinds: (b, 0, 0)),
+            pl.BlockSpec((1, OBS, D), lambda b, kinds: (b, 0, 0)),
         ],
     )
     return pl.pallas_call(
@@ -98,12 +101,12 @@
         grid_spec=grid_spec,
         out_shape=[
             jax.ShapeDtypeStruct((near, OBS, D), jnp.bfloat16),
-            jax.ShapeDtypeStruct((near, D, OBS), jnp.bfloat16),
+            jax.ShapeDtypeStruct((near, OBS, D), jnp.bfloat16),
         ],
     )(kinds, near_obs, table, key_gain.reshape(1, D))
 
 
-def attend(local_ids, tile_blocks, counts, queries_t, keys, values_t):
+def attend(local_ids, tile_blocks, counts, queries_t, keys, values):
     tiles = queries_t.shape[0]
     near = keys.shape[0]
     grid_spec = pltpu.PrefetchScalarGridSpec(
@@ -112,17 +115,17 @@
         in_specs=[
             pl.BlockSpec((1, D, CELLS), lambda t, *_: (t, 0, 0)),
             pl.BlockSpec((near, OBS, D), lambda t, *_: (0, 0, 0)),
-            pl.BlockSpec((near, D, OBS), lambda t, *_: (0, 0, 0)),
+            pl.BlockSpec((near, OBS, D), lambda t, *_: (0, 0, 0)),
         ],
-        out_specs=pl.BlockSpec((1, D, CELLS), lambda t, *_: (t, 0, 0)),
+        out_specs=pl.BlockSpec((CELLS, D), lambda t, *_: (t, 0)),
         scratch_shapes=[pltpu.VMEM((MAXB, OBS, 2 * LANES), jnp.float32)],
     )
     return pl.pallas_call(
         attend_kernel,
         grid_spec=grid_spec,
-        out_shape=jax.ShapeDtypeStruct(queries_t.shape, jnp.bfloat16),
+        out_shape=jax.ShapeDtypeStruct((tiles * CELLS, D), jnp.bfloat16),
         compiler_params=pltpu.CompilerParams(vmem_limit_bytes=48 * 1024 * 1024),
-    )(local_ids.reshape(-1), tile_blocks, counts, queries_t, keys, values_t)
+    )(local_ids.reshape(-1), tile_blocks, counts, queries_t, keys, values)
 
 
 def body(
@@ -150,18 +153,15 @@
     near_kinds = instrument[near_ids]
     counts = observed_count[near_ids]
     near_kinds = jnp.clip(near_kinds, 0, kinds - 1).astype(jnp.int32)
-    keys, values_t = embed(near_kinds, near_obs, table, key_gain.astype(jnp.float32))
+    keys, values = embed(near_kinds, near_obs, table, key_gain.astype(jnp.float32))
     tiles = latent.shape[0] // CELLS
     queries = (latent.astype(jnp.float32) * query_gain).astype(jnp.bfloat16)
     queries_t = jnp.swapaxes(queries.reshape(tiles, CELLS, D), 1, 2)
     local_ids = jnp.clip(footprint - first_block, 0, near_count - 1).astype(jnp.int32)
-    attended_t = attend(
-        local_ids, tile_blocks.astype(jnp.int32), counts, queries_t, keys, values_t
+    attended = attend(local_ids, tile_blocks.astype(jnp.int32), counts, queries_t, keys, values)
+    mixed = latent.astype(jnp.float32) + jnp.dot(
+        attended, output_weight, preferred_element_type=jnp.float32
     )
-    projected = jnp.einsum(
-        "tdq,de->tqe", attended_t, output_weight, preferred_element_type=jnp.float32
-    ).reshape(tiles * CELLS, D)
-    mixed = latent.astype(jnp.float32) + projected
     return normalize(mixed, output_gain).astype(jnp.bfloat16)
 
 

time: 107 us -> 108 us (level)
  Pallas kernels: 34.2 us -> 37 us
    pallas_call x1, Pallas kernels: 22.2 us -> 25.4 us  [attend(): pl.pallas_call(attend_kernel, grid_spec=grid_spec, out_shape=jax.ShapeDty...]
where the time goes in v5:
time: 108 us; the launch traced here: 107 us
  Pallas kernels  37 us (34%)
  waiting for transfers between devices  35.3 us (33%)
  between operations  13.5 us (12%)
  other arithmetic  5.86 us (5%)
  starting transfers between devices  5.61 us (5%)
  local copies, waits for them, and re-layouts  4.79 us (4%)
  matrix products  4.64 us (4%)
    all_gather x1, waiting for transfers between devices, body(): table = lax.all_gather(panels, 'lat', axis=0, tiled=True)  34.6 us
    pallas_call x1, Pallas kernels, attend(): pl.pallas_call(attend_kernel, grid_spec=grid_spec, out_shape=jax.ShapeDty...  25.4 us
    pallas_call x1, Pallas kernels, embed(): pl.pallas_call(embed_kernel, grid_spec=grid_spec, out_shape=[jax.ShapeDty...  11.6 us
    dot_general x1, matrix products, body(): jnp.dot(attended, output_weight, preferred_element_type=jnp.float32)  4.64 us
    ppermute x1, starting transfers between devices, padded(): before = lax.ppermute(value[length - width:], axis, up)  3.68 us
  transfers between devices with their start and end apart: 3, of which 1 were waited for; matrix products, arithmetic and copies ran while one was open for 9% of the time, Pallas kernels for 0%

profile of v5, /device:TPU:5, one launch (start us, length us, event | category | flops | bytes accessed | tf_op | source)
XLA Modules:
  0.0 106.7 jit_solution(8550382700047068739)
XLA Ops:
  6.5 0.0 all-gather.2.cloned.1.call-start
  6.5 0.7 all-gather.2.cloned.1.call-update
  7.3 3.7 %collective-permute-start = (bf16[4,128,128]{2,1,0:T(8,128)(2,1)}, bf16[4,128,128]{2,1,0:T(8,128)(2,1)S(1)}, u32[]{:S(2)}, u32[]{:S(2)}) collective-permute-start(bf16[4,128,128]{2,1,0:T(8,128)(2,1)} %param.16), channel_id=1, source_target_pairs={{0,1},{1,2},{2,3},{3,4},{4,5},{5,6},{6,7},{7,8},{8,9},{9,10},{10,1... | collective-permute-start | bytes 393224 | tf_op jit(solution)/shard_map/ppermute | solution.py:24
  10.9 1.9 %collective-permute-start.1 = (bf16[4,128,128]{2,1,0:T(8,128)(2,1)}, bf16[4,128,128]{2,1,0:T(8,128)(2,1)S(1)}, u32[]{:S(2)}, u32[]{:S(2)}) collective-permute-start(bf16[4,128,128]{2,1,0:T(8,128)(2,1)} %param.16), channel_id=1, source_target_pairs={{1,0},{2,1},{3,2},{4,3},{5,4},{6,5},{7,6},{8,7},{9,8},{10,9},{11,1... | collective-permute-start | bytes 393224 | tf_op jit(solution)/shard_map/ppermute | solution.py:25
  12.9 1.3 %reshape.40.gain_ref = f32[1,1536]{1,0:T(1,128)} reshape(f32[1536]{0:T(1024)} %param.13) | data formatting | bytes 12288 | tf_op jit(solution)/shard_map/reshape | solution.py:106
  14.2 1.2 %gather_fusion.1 = s32[12]{0:T(128)} fusion(s32[64]{0:T(128)S(1)} %copy-done, s32[1024]{0:T(1024)S(1)} %pad_clamp_fusion), kind=kCustom, calls=%fused_computation.1 | custom fusion | bytes 144 | tf_op jit(solution)/shard_map/gather | solution.py:153
  15.4 1.3 %gather_fusion = s32[12]{0:T(128)S(1)} fusion(s32[64]{0:T(128)} %param.19, s32[1024]{0:T(1024)S(1)} %pad_clamp_fusion), kind=kCustom, calls=%fused_computation | custom fusion | bytes 144 | tf_op jit(solution)/shard_map/gather | solution.py:154
  16.7 0.7 subtract_clamp_fusion
  17.4 0.1 reshape.38.ids_ref
  17.5 1.7 %fusion = bf16[512,1536]{1,0:T(8,128)(2,1)S(1)} fusion(bf16[512,1536]{1,0:T(8,128)(2,1)} %param.11, f32[1536]{0:T(1024)} %param.12), kind=kLoop, calls=%fused_computation.4 | loop fusion | flops 2359296 | bytes 3151872 | tf_op jit(solution)/shard_map/convert_element_type | solution.py:158
  19.2 0.0 copy-start.1
  19.2 0.9 copy.12
  20.1 1.1 %broadcast_clamp_fusion.kinds_ref = s32[12]{0:T(128)} fusion(s32[12]{0:T(128)} %gather_fusion.1), kind=kLoop, calls=%fused_computation.13 | loop fusion | flops 12 | bytes 96 | tf_op jit(solution)/shard_map/jit(clip)/min | solution.py:155
  21.3 0.0 collective-permute-done
  21.3 0.0 collective-permute-done.1
  21.3 0.8 pad_maximum_fusion.obs_ref
  22.1 34.6 %all-gather.2.cloned.1.call-done.panel_ref = bf16[1024,1536]{1,0:T(8,128)(2,1)} async-done(((bf16[64,1536]{1,0:T(8,128)(2,1)}), bf16[1024,1536]{1,0:T(8,128)(2,1)}) %all-gather.2.cloned.1.call-update) | async-done | bytes 3145744 | tf_op jit(solution)/shard_map/all_gather | solution.py:148
  56.7 11.6 %shard_map.109 = (bf16[12,128,1536]{2,1,0:T(8,128)(2,1)}, bf16[12,128,1536]{2,1,0:T(8,128)(2,1)}) custom-call(s32[12]{0:T(128)} %broadcast_clamp_fusion.kinds_ref, bf16[12,128,128]{2,1,0:T(8,128)(2,1)} %pad_maximum_fusion.obs_ref, bf16[1024,1536]{1,0:T(8,128)(2,1)} %all-gather.2.cloned.1.call-done.panel_ref, f32[1,1536]{1,0:T(1,128)} %reshape.40.gain_ref), custom_call_target="tpu_custom_call" | custom-call | tf_op jit(solution)/shard_map/pallas_call | solution.py:99
  68.3 0.0 copy-done.1
  68.3 25.4 %shard_map.110 = bf16[512,1536]{1,0:T(8,128)(2,1)S(1)} custom-call(s32[24]{0:T(128)S(1)} %reshape.38.ids_ref, s32[4]{0:T(128)S(1)} %copy-done.1, s32[12]{0:T(128)S(1)} %gather_fusion, bf16[4,1536,128]{2,1,0:T(8,128)(2,1)S(1)} %bitcast.6, bf16[12,128,1536]{2,1,0:T(8,128)(2,1)} %get-tuple-element.7.k_ref, bf16[12,128,1536]{2,1,0:T(8,128)(2,1)} %get-tuple-element.8.v_ref), custom_call_target="tpu_custom_call" | custom-call | tf_op jit(solution)/shard_map/pallas_call | solution.py:123
  93.7 0.0 copy-start.4
  93.8 4.6 %multiply_reduce_fusion = (f32[512]{0:T(512)S(1)}, f32[512,1536]{1,0:T(8,128)S(1)}) fusion(bf16[512,1536]{1,0:T(8,128)(2,1)S(1)} %shard_map.110, bf16[1536,1536]{1,0:T(8,128)(2,1)} %param.15, bf16[512,1536]{1,0:T(8,128)(2,1)S(1)} %copy-done.2), kind=kOutput, calls=%fused_computation.6 | convolution fusion | flops 2419064320 | bytes 11012096 | tf_op jit(solution)/shard_map/dot_general | solution.py:162
  98.4 0.0 copy-done.4
  98.4 1.5 %multiply_convert_fusion = bf16[512,1536]{1,0:T(8,128)(2,1)} fusion(f32[512,1536]{1,0:T(8,128)S(1)} %get-tuple-element.10, f32[1536]{0:T(1024)S(1)} %copy-done.4, f32[512]{0:T(512)S(1)} %add_rsqrt_fusion), kind=kLoop, calls=%fused_computation.5 | loop fusion | flops 2359296 | bytes 4726784 | tf_op jit(solution)/shard_map/convert_element_type | solution.py:165
  (9 shorter events, 0.0 us)
Async XLA Ops:
  6.5 7.7 %copy-start = (s32[64]{0:T(128)S(1)}, s32[64]{0:T(128)}, u32[]{:S(2)}) copy-start(s32[64]{0:T(128)} %param.18) | copy-start | bytes 772
  6.5 50.2 %all-gather.2.cloned.1.call-start = ((), (), s32[]{:S(2)}) async-start(), calls=%async_computation | async-start | bytes 3342336 | tf_op jit(solution)/shard_map/all_gather | solution.py:148
  7.3 14.0 %collective-permute-start = (bf16[4,128,128]{2,1,0:T(8,128)(2,1)}, bf16[4,128,128]{2,1,0:T(8,128)(2,1)S(1)}, u32[]{:S(2)}, u32[]{:S(2)}) collective-permute-start(bf16[4,128,128]{2,1,0:T(8,128)(2,1)} %param.16), channel_id=1, source_target_pairs={{0,1},{1,2},{2,3},{3,4},{4,5},{5,6},{6,7},{7,8},{8,9},{9,10},{10,1... | collective-permute-start | bytes 393224 | tf_op jit(solution)/shard_map/ppermute | solution.py:24
  10.9 10.3 %collective-permute-start.1 = (bf16[4,128,128]{2,1,0:T(8,128)(2,1)}, bf16[4,128,128]{2,1,0:T(8,128)(2,1)S(1)}, u32[]{:S(2)}, u32[]{:S(2)}) collective-permute-start(bf16[4,128,128]{2,1,0:T(8,128)(2,1)} %param.16), channel_id=1, source_target_pairs={{1,0},{2,1},{3,2},{4,3},{5,4},{6,5},{7,6},{8,7},{9,8},{10,9},{11,1... | collective-permute-start | bytes 393224 | tf_op jit(solution)/shard_map/ppermute | solution.py:25
  17.5 3.8 %copy-start.3 = (bf16[4,128,128]{2,1,0:T(8,128)(2,1)S(1)}, bf16[4,128,128]{2,1,0:T(8,128)(2,1)}, u32[]{:S(2)}) copy-start(bf16[4,128,128]{2,1,0:T(8,128)(2,1)} %param.16) | copy-start | bytes 393220
  19.2 49.1 %copy-start.1 = (s32[4]{0:T(128)S(1)}, s32[4]{0:T(128)}, u32[]{:S(2)}) copy-start(s32[4]{0:T(128)} %nb_ref.1) | copy-start | bytes 52
  68.3 25.4 %copy-start.2 = (bf16[512,1536]{1,0:T(8,128)(2,1)S(1)}, bf16[512,1536]{1,0:T(8,128)(2,1)}, u32[]{:S(2)}) copy-start(bf16[512,1536]{1,0:T(8,128)(2,1)} %param.11) | copy-start | bytes 4718596
  93.7 4.7 %copy-start.4 = (f32[1536]{0:T(1024)S(1)}, f32[1536]{0:T(1024)}, u32[]{:S(2)}) copy-start(f32[1536]{0:T(1024)} %param.14) | copy-start | bytes 18436
Sparse Core Ops, SparseCore 0:
  9.6 47.0 all-gather.1

commit v6 on v3

--- a/solution.py
+++ b/solution.py
@@ -70,26 +70,87 @@
         ).astype(jnp.bfloat16)
 
 
-def attend(local_ids, tile_blocks, counts, queries_t, keys, values_t):
+def attend_kernel(
+    kinds_ref, ids_ref, nb_ref, cnt_ref, obs_ref, table_ref, gain_ref, qt_ref, o_ref,
+    k_ref, vt_ref, s_ref,
+):
+    tile = pl.program_id(0)
+
+    @pl.when(tile == 0)
+    def _():
+        for b in range(k_ref.shape[0]):
+            start = pl.multiple_of(kinds_ref[b] * CH, CH)
+            embedded = jnp.dot(
+                obs_ref[b], table_ref[pl.ds(start, CH), :], preferred_element_type=jnp.float32
+            )
+            embedded = embedded.astype(jnp.bfloat16).astype(jnp.float32)
+            norm = lax.rsqrt(jnp.mean(embedded * embedded, axis=1, keepdims=True) + 1e-06)
+            k_ref[b] = (embedded * norm * gain_ref[...]).astype(jnp.bfloat16)
+            vt_ref[b] = embedded.T.astype(jnp.bfloat16)
+
+    used = nb_ref[tile]
+    scale = 1.0 / math.sqrt(HD)
+    row = lax.broadcasted_iota(jnp.int32, (LANES, 1), 0)
+    low = row < HD
+    wide = 2 * LANES
+    for pair in range(D // LANES):
+        rows = pl.ds(pair * LANES, LANES)
+        qt = qt_ref[0, rows, :].astype(jnp.float32)
+        q2 = jnp.concatenate(
+            [jnp.where(low, qt, 0.0), jnp.where(low, 0.0, qt)], axis=1
+        ).astype(jnp.bfloat16)
+        high = jnp.full((1, wide), -jnp.inf, jnp.float32)
+        for j in range(MAXB):
+            block = ids_ref[tile * MAXB + j]
+            keys = k_ref[block, :, rows]
+            s = jnp.dot(keys, q2, preferred_element_type=jnp.float32) * scale
+            s = jnp.where((row < cnt_ref[block]) & (j < used), s, -jnp.inf)
+            s_ref[j] = s
+            high = jnp.maximum(high, jnp.max(s, axis=0, keepdims=True))
+        total = jnp.zeros((1, wide), jnp.float32)
+        acc = jnp.zeros((LANES, wide), jnp.float32)
+        for j in range(MAXB):
+            block = ids_ref[tile * MAXB + j]
+            w = jnp.exp(s_ref[j] - high)
+            total = total + jnp.sum(w, axis=0, keepdims=True)
+            acc = acc + jnp.dot(
+                vt_ref[block, rows, :], w.astype(jnp.bfloat16), preferred_element_type=jnp.float32
+            )
+        o_ref[0, pl.ds(pair * LANES, HD), :] = (acc[:HD, :LANES] / total[:, :LANES]).astype(
+            jnp.bfloat16
+        )
+        o_ref[0, pl.ds(pair * LANES + HD, HD), :] = (
+            acc[HD:, LANES:] / total[:, LANES:]
+        ).astype(jnp.bfloat16)
+
+
+def attend(kinds, local_ids, tile_blocks, counts, near_obs, table, key_gain, queries_t):
     tiles = queries_t.shape[0]
-    near = keys.shape[0]
+    near = near_obs.shape[0]
     grid_spec = pltpu.PrefetchScalarGridSpec(
-        num_scalar_prefetch=3,
+        num_scalar_prefetch=4,
         grid=(tiles,),
         in_specs=[
+            pl.BlockSpec(near_obs.shape, lambda t, *_: (0, 0, 0)),
+            pl.BlockSpec(table.shape, lambda t, *_: (0, 0)),
+            pl.BlockSpec((1, D), lambda t, *_: (0, 0)),
             pl.BlockSpec((1, D, CELLS), lambda t, *_: (t, 0, 0)),
-            pl.BlockSpec((near, OBS, D), lambda t, *_: (0, 0, 0)),
-            pl.BlockSpec((near, D, OBS), lambda t, *_: (0, 0, 0)),
         ],
         out_specs=pl.BlockSpec((1, D, CELLS), lambda t, *_: (t, 0, 0)),
-        scratch_shapes=[pltpu.VMEM((MAXB, OBS, 2 * LANES), jnp.float32)],
+        scratch_shapes=[
+            pltpu.VMEM((near, OBS, D), jnp.bfloat16),
+            pltpu.VMEM((near, D, OBS), jnp.bfloat16),
+            pltpu.VMEM((MAXB, OBS, 2 * LANES), jnp.float32),
+        ],
     )
     return pl.pallas_call(
         attend_kernel,
         grid_spec=grid_spec,
         out_shape=jax.ShapeDtypeStruct(queries_t.shape, jnp.bfloat16),
-        compiler_params=pltpu.CompilerParams(vmem_limit_bytes=48 * 1024 * 1024),
-    )(local_ids.reshape(-1), tile_blocks, counts, queries_t, keys, values_t)
+        compiler_params=pltpu.CompilerParams(
+            dimension_semantics=("arbitrary",), vmem_limit_bytes=48 * 1024 * 1024
+        ),
+    )(kinds, local_ids.reshape(-1), tile_blocks, counts, near_obs, table, key_gain.reshape(1, D), queries_t)
 
 
 def body(
@@ -116,17 +177,20 @@
     near_ids = jnp.clip(first_block + jnp.arange(near_count, dtype=jnp.int32), 0, all_blocks - 1)
     near_kinds = instrument[near_ids]
     counts = observed_count[near_ids]
-    near_panels = table.reshape(kinds, CH, D)[near_kinds]
-    embedded = jnp.einsum(
-        "boc,bcd->bod", near_obs, near_panels, preferred_element_type=jnp.float32
-    ).astype(jnp.bfloat16)
-    keys = normalize(embedded, key_gain).astype(jnp.bfloat16)
+    near_kinds = jnp.clip(near_kinds, 0, kinds - 1).astype(jnp.int32)
     tiles = latent.shape[0] // CELLS
     queries = (latent.astype(jnp.float32) * query_gain).astype(jnp.bfloat16)
     queries_t = jnp.swapaxes(queries.reshape(tiles, CELLS, D), 1, 2)
     local_ids = jnp.clip(footprint - first_block, 0, near_count - 1).astype(jnp.int32)
     attended_t = attend(
-        local_ids, tile_blocks.astype(jnp.int32), counts, queries_t, keys, jnp.swapaxes(embedded, 1, 2)
+        near_kinds,
+        local_ids,
+        tile_blocks.astype(jnp.int32),
+        counts,
+        near_obs,
+        table,
+        key_gain.astype(jnp.float32),
+        queries_t,
     )
     projected = jnp.einsum(
         "tdq,de->tqe", attended_t, output_weight, preferred_element_type=jnp.float32

time: 116 us -> 93.9 us (0.81)
  local copies, waits for them, and re-layouts: 16.4 us -> 4.04 us
  matrix products: 9.15 us -> 2.64 us
  other arithmetic: 8.17 us -> 5.48 us
  waiting for transfers between devices: 39.8 us -> 37.3 us
  Pallas kernels: 22.2 us -> 23.9 us
    convert_element_type x1 -> x0, local copies, waits for them, and re-layouts: 6.74 us -> none  [body(): keys = normalize(embedded, key_gain).astype(jnp.bfloat16)]
    gather x1 -> x0, local copies, waits for them, and re-layouts: 5.06 us -> none  [body(): near_panels = table.reshape(kinds, CH, D)[near_kinds]]
    dot_general x1 -> x0, matrix products: 4.42 us -> none  [body(): jnp.einsum('boc,bcd->bod', near_obs, near_panels, preferred_element_type=...]
    convert_element_type x1 -> x0, other arithmetic: 3.66 us -> none  [body(): keys = normalize(embedded, key_gain).astype(jnp.bfloat16)]
    all_gather x1, waiting for transfers between devices: 39.1 us -> 36.6 us  [body(): table = lax.all_gather(panels, 'lat', axis=0, tiled=True)]
    unnamed x16 -> x12, local copies, waits for them, and re-layouts: 2.34 us -> 0.22 us
    dot_general x1, matrix products: 4.73 us -> 2.64 us  [body(): jnp.einsum('tdq,de->tqe', attended_t, output_weight, preferred_element_ty...]
    pallas_call x1, Pallas kernels: 22.2 us -> 23.9 us  [attend(): pl.pallas_call(attend_kernel, grid_spec=grid_spec, out_shape=jax.ShapeDty...]
where the time goes in v6:
time: 93.9 us; the launch traced here: 92.5 us
  waiting for transfers between devices  37.3 us (40%)
  Pallas kernels  23.9 us (25%)
  between operations  13.5 us (14%)
  starting transfers between devices  5.61 us (6%)
  other arithmetic  5.48 us (6%)
  local copies, waits for them, and re-layouts  4.04 us (4%)
  matrix products  2.64 us (3%)
    all_gather x1, waiting for transfers between devices, body(): table = lax.all_gather(panels, 'lat', axis=0, tiled=True)  36.6 us
    pallas_call x1, Pallas kernels, attend(): pl.pallas_call(attend_kernel, grid_spec=grid_spec, out_shape=jax.ShapeDty...  23.9 us
    ppermute x1, starting transfers between devices, padded(): before = lax.ppermute(value[length - width:], axis, up)  3.68 us
    dot_general x1, matrix products, body(): jnp.einsum('tdq,de->tqe', attended_t, output_weight, preferred_element_ty...  2.64 us
    ppermute x1, starting transfers between devices, padded(): after = lax.ppermute(value[:width], axis, down)  1.92 us
  transfers between devices with their start and end apart: 3, of which 1 were waited for; matrix products, arithmetic and copies ran while one was open for 8% of the time, Pallas kernels for 0%

profile of v6, /device:TPU:5, one launch (start us, length us, event | category | flops | bytes accessed | tf_op | source)
XLA Modules:
  0.0 92.5 jit_solution(8773637538844263333)
XLA Ops:
  6.5 0.0 copy-start
  6.5 0.0 all-gather.2.cloned.1.call-start
  6.5 0.7 all-gather.2.cloned.1.call-update
  7.3 3.7 %collective-permute-start = (bf16[4,128,128]{2,1,0:T(8,128)(2,1)}, bf16[4,128,128]{2,1,0:T(8,128)(2,1)S(1)}, u32[]{:S(2)}, u32[]{:S(2)}) collective-permute-start(bf16[4,128,128]{2,1,0:T(8,128)(2,1)} %param.16), channel_id=1, source_target_pairs={{0,1},{1,2},{2,3},{3,4},{4,5},{5,6},{6,7},{7,8},{8,9},{9,10},{10,1... | collective-permute-start | bytes 393224 | tf_op jit(solution)/shard_map/ppermute | solution.py:24
  10.9 1.9 %collective-permute-start.1 = (bf16[4,128,128]{2,1,0:T(8,128)(2,1)}, bf16[4,128,128]{2,1,0:T(8,128)(2,1)}, u32[]{:S(2)}, u32[]{:S(2)}) collective-permute-start(bf16[4,128,128]{2,1,0:T(8,128)(2,1)} %param.16), channel_id=1, source_target_pairs={{1,0},{2,1},{3,2},{4,3},{5,4},{6,5},{7,6},{8,7},{9,8},{10,9},{11,1... | collective-permute-start | bytes 393224 | tf_op jit(solution)/shard_map/ppermute | solution.py:25
  12.9 0.7 subtract_clamp_fusion
  13.6 0.1 reshape.41.ids_ref
  13.7 0.0 copy-done
  13.7 0.7 gather_fusion.1
  14.3 1.3 %gather_fusion = s32[12]{0:T(128)S(1)} fusion(s32[64]{0:T(128)} %param.18, s32[1024]{0:T(1024)S(1)} %pad_clamp_fusion), kind=kCustom, calls=%fused_computation | custom fusion | bytes 144 | tf_op jit(solution)/shard_map/gather | solution.py:178
  15.7 0.7 reshape.42.gain_ref
  16.4 1.7 %fusion.2 = bf16[512,1536]{1,0:T(8,128)(2,1)S(1)} fusion(bf16[512,1536]{1,0:T(8,128)(2,1)} %param.11, f32[1536]{0:T(1024)} %param.12), kind=kLoop, calls=%fused_computation.6 | loop fusion | flops 2359296 | bytes 3151872 | tf_op jit(solution)/shard_map/convert_element_type | solution.py:182
  18.1 1.0 %copy.13 = bf16[4,128,1536]{1,2,0:T(8,128)(2,1)S(1)} copy(bf16[4,128,1536]{2,1,0:T(8,128)(2,1)S(1)} %bitcast.15) | data formatting | bytes 3145728 | tf_op jit(solution)/shard_map/reshape | solution.py:183
  19.2 0.0 collective-permute-done
  19.2 0.0 collective-permute-done.1
  19.2 1.0 %pad_maximum_fusion.obs_ref = bf16[12,128,128]{2,1,0:T(8,128)(2,1)S(1)} fusion(bf16[4,128,128]{2,1,0:T(8,128)(2,1)} %collective-permute-done.1, bf16[4,128,128]{2,1,0:T(8,128)(2,1)S(1)} %copy-done.4, bf16[4,128,128]{2,1,0:T(8,128)(2,1)S(1)} %collective-permute-done), kind=kLoop, calls=%fused_computation.9 | loop fusion | flops 393216 | bytes 786432 | tf_op jit(solution)/shard_map/concatenate | solution.py:26
  20.1 36.6 %all-gather.2.cloned.1.call-done.table_ref = bf16[1024,1536]{1,0:T(8,128)(2,1)} async-done(((bf16[64,1536]{1,0:T(8,128)(2,1)}), bf16[1024,1536]{1,0:T(8,128)(2,1)}) %all-gather.2.cloned.1.call-update) | async-done | bytes 3145744 | tf_op jit(solution)/shard_map/all_gather | solution.py:173
  56.7 23.9 %shard_map.109 = bf16[4,1536,128]{2,1,0:T(8,128)(2,1)S(1)} custom-call(s32[12]{0:T(128)S(1)} %broadcast_clamp_fusion.kinds_ref, s32[24]{0:T(128)S(1)} %reshape.41.ids_ref, s32[4]{0:T(128)S(1)} %copy-done.1, s32[12]{0:T(128)S(1)} %gather_fusion.1, bf16[12,128,128]{2,1,0:T(8,128)(2,1)S(1)} %pad_maximum_fusion.obs_ref, ...), custom_call_target="tpu_custom_call" | custom-call | tf_op jit(solution)/shard_map/pallas_call | solution.py:146
  80.7 0.0 copy-start.2
  80.7 2.6 %fusion = f32[4,128,1536]{2,1,0:T(8,128)S(1)} fusion(bf16[4,1536,128]{2,1,0:T(8,128)(2,1)S(1)} %shard_map.109, bf16[1536,1536]{1,0:T(8,128)(2,1)S(1)} %copy-done.3), kind=kOutput, calls=%fused_computation.2 | convolution fusion | flops 2415919104 | bytes 9437184 | tf_op jit(solution)/shard_map/tdq,de->tqe/dot_general | solution.py:195
  83.3 0.0 copy-start.5
  83.3 0.5 multiply_reduce_fusion
  83.8 0.2 copy-done.5
  84.0 1.6 %multiply_convert_fusion = bf16[512,1536]{1,0:T(8,128)(2,1)} fusion(f32[4,128,1536]{2,1,0:T(8,128)S(1)} %fusion, bf16[512,1536]{1,0:T(8,128)(2,1)S(1)} %copy-done.2, f32[1536]{0:T(1024)S(1)} %copy-done.5, f32[512]{0:T(512)S(1)} %add_rsqrt_fusion), kind=kLoop, calls=%fused_computation.7 | loop fusion | flops 3932160 | bytes 6299648 | tf_op jit(solution)/shard_map/convert_element_type | solution.py:199
  (11 shorter events, 0.0 us)
Async XLA Ops:
  6.5 7.1 %copy-start = (s32[64]{0:T(128)S(1)}, s32[64]{0:T(128)}, u32[]{:S(2)}) copy-start(s32[64]{0:T(128)} %param.19) | copy-start | bytes 772
  6.5 50.2 %all-gather.2.cloned.1.call-start = ((), (), s32[]{:S(2)}) async-start(), calls=%async_computation | async-start | bytes 3342336 | tf_op jit(solution)/shard_map/all_gather | solution.py:173
  7.3 11.9 %collective-permute-start = (bf16[4,128,128]{2,1,0:T(8,128)(2,1)}, bf16[4,128,128]{2,1,0:T(8,128)(2,1)S(1)}, u32[]{:S(2)}, u32[]{:S(2)}) collective-permute-start(bf16[4,128,128]{2,1,0:T(8,128)(2,1)} %param.16), channel_id=1, source_target_pairs={{0,1},{1,2},{2,3},{3,4},{4,5},{5,6},{6,7},{7,8},{8,9},{9,10},{10,1... | collective-permute-start | bytes 393224 | tf_op jit(solution)/shard_map/ppermute | solution.py:24
  10.9 8.2 %collective-permute-start.1 = (bf16[4,128,128]{2,1,0:T(8,128)(2,1)}, bf16[4,128,128]{2,1,0:T(8,128)(2,1)}, u32[]{:S(2)}, u32[]{:S(2)}) collective-permute-start(bf16[4,128,128]{2,1,0:T(8,128)(2,1)} %param.16), channel_id=1, source_target_pairs={{1,0},{2,1},{3,2},{4,3},{5,4},{6,5},{7,6},{8,7},{9,8},{10,9},{11,1... | collective-permute-start | bytes 393224 | tf_op jit(solution)/shard_map/ppermute | solution.py:25
  16.4 2.8 %copy-start.4 = (bf16[4,128,128]{2,1,0:T(8,128)(2,1)S(1)}, bf16[4,128,128]{2,1,0:T(8,128)(2,1)}, u32[]{:S(2)}) copy-start(bf16[4,128,128]{2,1,0:T(8,128)(2,1)} %param.16) | copy-start | bytes 393220
  16.4 40.3 %copy-start.1 = (s32[4]{0:T(128)S(1)}, s32[4]{0:T(128)}, u32[]{:S(2)}) copy-start(s32[4]{0:T(128)} %nb_ref.1) | copy-start | bytes 52
  56.7 23.9 %copy-start.3 = (bf16[1536,1536]{1,0:T(8,128)(2,1)S(1)}, bf16[1536,1536]{1,0:T(8,128)(2,1)}, u32[]{:S(2)}) copy-start(bf16[1536,1536]{1,0:T(8,128)(2,1)} %param.15) | copy-start | bytes 14155780
  80.7 2.7 %copy-start.2 = (bf16[512,1536]{1,0:T(8,128)(2,1)S(1)}, bf16[512,1536]{1,0:T(8,128)(2,1)}, u32[]{:S(2)}) copy-start(bf16[512,1536]{1,0:T(8,128)(2,1)} %param.11) | copy-start | bytes 4718596
  83.3 0.7 copy-start.5
Sparse Core Ops, SparseCore 0:
  9.6 47.0 all-gather.1

commit v7 on v6

--- a/solution.py
+++ b/solution.py
@@ -31,45 +31,6 @@
     return values * lax.rsqrt(jnp.mean(values * values, axis=-1, keepdims=True) + 1e-06) * gain
 
 
-def attend_kernel(ids_ref, nb_ref, cnt_ref, qt_ref, k_ref, vt_ref, o_ref, s_ref):
-    tile = pl.program_id(0)
-    used = nb_ref[tile]
-    scale = 1.0 / math.sqrt(HD)
-    row = lax.broadcasted_iota(jnp.int32, (LANES, 1), 0)
-    low = row < HD
-    wide = 2 * LANES
-    for pair in range(D // LANES):
-        rows = pl.ds(pair * LANES, LANES)
-        qt = qt_ref[0, rows, :].astype(jnp.float32)
-        q2 = jnp.concatenate(
-            [jnp.where(low, qt, 0.0), jnp.where(low, 0.0, qt)], axis=1
-        ).astype(jnp.bfloat16)
-
-        high = jnp.full((1, wide), -jnp.inf, jnp.float32)
-        for j in range(MAXB):
-            block = ids_ref[tile * MAXB + j]
-            keys = k_ref[block, :, rows]
-            s = jnp.dot(keys, q2, preferred_element_type=jnp.float32) * scale
-            s = jnp.where((row < cnt_ref[block]) & (j < used), s, -jnp.inf)
-            s_ref[j] = s
-            high = jnp.maximum(high, jnp.max(s, axis=0, keepdims=True))
-        total = jnp.zeros((1, wide), jnp.float32)
-        acc = jnp.zeros((LANES, wide), jnp.float32)
-        for j in range(MAXB):
-            block = ids_ref[tile * MAXB + j]
-            w = jnp.exp(s_ref[j] - high)
-            total = total + jnp.sum(w, axis=0, keepdims=True)
-            acc = acc + jnp.dot(
-                vt_ref[block, rows, :], w.astype(jnp.bfloat16), preferred_element_type=jnp.float32
-            )
-        o_ref[0, pl.ds(pair * LANES, HD), :] = (acc[:HD, :LANES] / total[:, :LANES]).astype(
-            jnp.bfloat16
-        )
-        o_ref[0, pl.ds(pair * LANES + HD, HD), :] = (
-            acc[HD:, LANES:] / total[:, LANES:]
-        ).astype(jnp.bfloat16)
-
-
 def attend_kernel(
     kinds_ref, ids_ref, nb_ref, cnt_ref, obs_ref, table_ref, gain_ref, qt_ref, o_ref,
     k_ref, vt_ref, s_ref,
@@ -95,7 +56,7 @@
     wide = 2 * LANES
     for pair in range(D // LANES):
         rows = pl.ds(pair * LANES, LANES)
-        qt = qt_ref[0, rows, :].astype(jnp.float32)
+        qt = qt_ref[0, rows, :].astype(jnp.float32) * scale
         q2 = jnp.concatenate(
             [jnp.where(low, qt, 0.0), jnp.where(low, 0.0, qt)], axis=1
         ).astype(jnp.bfloat16)
@@ -103,18 +64,23 @@
         for j in range(MAXB):
             block = ids_ref[tile * MAXB + j]
             keys = k_ref[block, :, rows]
-            s = jnp.dot(keys, q2, preferred_element_type=jnp.float32) * scale
+            s = jnp.dot(keys, q2, preferred_element_type=jnp.float32)
             s = jnp.where((row < cnt_ref[block]) & (j < used), s, -jnp.inf)
             s_ref[j] = s
             high = jnp.maximum(high, jnp.max(s, axis=0, keepdims=True))
         total = jnp.zeros((1, wide), jnp.float32)
         acc = jnp.zeros((LANES, wide), jnp.float32)
-        for j in range(MAXB):
-            block = ids_ref[tile * MAXB + j]
-            w = jnp.exp(s_ref[j] - high)
-            total = total + jnp.sum(w, axis=0, keepdims=True)
+        for j in range(0, MAXB, 2):
+            ws, vs = [], []
+            for i in (j, j + 1):
+                w = jnp.exp(s_ref[i] - high)
+                total = total + jnp.sum(w, axis=0, keepdims=True)
+                ws.append(w.astype(jnp.bfloat16))
+                vs.append(vt_ref[ids_ref[tile * MAXB + i], rows, :])
             acc = acc + jnp.dot(
-                vt_ref[block, rows, :], w.astype(jnp.bfloat16), preferred_element_type=jnp.float32
+                jnp.concatenate(vs, axis=1),
+                jnp.concatenate(ws, axis=0),
+                preferred_element_type=jnp.float32,
             )
         o_ref[0, pl.ds(pair * LANES, HD), :] = (acc[:HD, :LANES] / total[:, :LANES]).astype(
             jnp.bfloat16

time: 93.9 us -> 97.1 us (1.034)
  Pallas kernels: 23.9 us -> 27.1 us
    pallas_call x1, Pallas kernels: 23.9 us -> 27.1 us  [attend(): pl.pallas_call(attend_kernel, grid_spec=grid_spec, out_shape=jax.ShapeDty...]
where the time goes in v7:
time: 97.1 us; the launch traced here: 95.7 us
  waiting for transfers between devices  37.3 us (38%)
  Pallas kernels  27.1 us (28%)
  between operations  13.5 us (14%)
  starting transfers between devices  5.61 us (6%)
  other arithmetic  5.48 us (6%)
  local copies, waits for them, and re-layouts  4.04 us (4%)
  matrix products  2.64 us (3%)
    all_gather x1, waiting for transfers between devices, body(): table = lax.all_gather(panels, 'lat', axis=0, tiled=True)  36.6 us
    pallas_call x1, Pallas kernels, attend(): pl.pallas_call(attend_kernel, grid_spec=grid_spec, out_shape=jax.ShapeDty...  27.1 us
    ppermute x1, starting transfers between devices, padded(): before = lax.ppermute(value[length - width:], axis, up)  3.68 us
    dot_general x1, matrix products, body(): jnp.einsum('tdq,de->tqe', attended_t, output_weight, preferred_element_ty...  2.64 us
  transfers between devices with their start and end apart: 3, of which 1 were waited for; matrix products, arithmetic and copies ran while one was open for 8% of the time, Pallas kernels for 0%

profile of v7, /device:TPU:5, one launch (start us, length us, event | category | flops | bytes accessed | tf_op | source)
XLA Modules:
  0.0 95.7 jit_solution(8956016812812153282)
XLA Ops:
  6.5 0.0 copy-start
  6.5 0.0 all-gather.2.cloned.1.call-start
  6.5 0.7 all-gather.2.cloned.1.call-update
  7.3 3.7 %collective-permute-start = (bf16[4,128,128]{2,1,0:T(8,128)(2,1)}, bf16[4,128,128]{2,1,0:T(8,128)(2,1)S(1)}, u32[]{:S(2)}, u32[]{:S(2)}) collective-permute-start(bf16[4,128,128]{2,1,0:T(8,128)(2,1)} %param.16), channel_id=1, source_target_pairs={{0,1},{1,2},{2,3},{3,4},{4,5},{5,6},{6,7},{7,8},{8,9},{9,10},{10,1... | collective-permute-start | bytes 393224 | tf_op jit(solution)/shard_map/ppermute | solution.py:24
  10.9 1.9 %collective-permute-start.1 = (bf16[4,128,128]{2,1,0:T(8,128)(2,1)}, bf16[4,128,128]{2,1,0:T(8,128)(2,1)}, u32[]{:S(2)}, u32[]{:S(2)}) collective-permute-start(bf16[4,128,128]{2,1,0:T(8,128)(2,1)} %param.16), channel_id=1, source_target_pairs={{1,0},{2,1},{3,2},{4,3},{5,4},{6,5},{7,6},{8,7},{9,8},{10,9},{11,1... | collective-permute-start | bytes 393224 | tf_op jit(solution)/shard_map/ppermute | solution.py:25
  12.9 0.7 subtract_clamp_fusion
  13.6 0.1 reshape.41.ids_ref
  13.7 0.0 copy-done
  13.7 0.7 gather_fusion.1
  14.3 1.3 %gather_fusion = s32[12]{0:T(128)S(1)} fusion(s32[64]{0:T(128)} %param.18, s32[1024]{0:T(1024)S(1)} %pad_clamp_fusion), kind=kCustom, calls=%fused_computation | custom fusion | bytes 144 | tf_op jit(solution)/shard_map/gather | solution.py:144
  15.7 0.7 reshape.42.gain_ref
  16.4 1.7 %fusion.2 = bf16[512,1536]{1,0:T(8,128)(2,1)S(1)} fusion(bf16[512,1536]{1,0:T(8,128)(2,1)} %param.11, f32[1536]{0:T(1024)} %param.12), kind=kLoop, calls=%fused_computation.6 | loop fusion | flops 2359296 | bytes 3151872 | tf_op jit(solution)/shard_map/convert_element_type | solution.py:148
  18.1 1.0 %copy.13 = bf16[4,128,1536]{1,2,0:T(8,128)(2,1)S(1)} copy(bf16[4,128,1536]{2,1,0:T(8,128)(2,1)S(1)} %bitcast.15) | data formatting | bytes 3145728 | tf_op jit(solution)/shard_map/reshape | solution.py:149
  19.2 0.0 collective-permute-done
  19.2 0.0 collective-permute-done.1
  19.2 1.0 pad_maximum_fusion.obs_ref
  20.1 36.6 %all-gather.2.cloned.1.call-done.table_ref = bf16[1024,1536]{1,0:T(8,128)(2,1)} async-done(((bf16[64,1536]{1,0:T(8,128)(2,1)}), bf16[1024,1536]{1,0:T(8,128)(2,1)}) %all-gather.2.cloned.1.call-update) | async-done | bytes 3145744 | tf_op jit(solution)/shard_map/all_gather | solution.py:139
  56.7 27.1 %shard_map.109 = bf16[4,1536,128]{2,1,0:T(8,128)(2,1)S(1)} custom-call(s32[12]{0:T(128)S(1)} %broadcast_clamp_fusion.kinds_ref, s32[24]{0:T(128)S(1)} %reshape.41.ids_ref, s32[4]{0:T(128)S(1)} %copy-done.1, s32[12]{0:T(128)S(1)} %gather_fusion.1, bf16[12,128,128]{2,1,0:T(8,128)(2,1)S(1)} %pad_maximum_fusion.obs_ref, ...), custom_call_target="tpu_custom_call" | custom-call | tf_op jit(solution)/shard_map/pallas_call | solution.py:112
  83.8 0.0 copy-start.2
  83.8 2.6 %fusion = f32[4,128,1536]{2,1,0:T(8,128)S(1)} fusion(bf16[4,1536,128]{2,1,0:T(8,128)(2,1)S(1)} %shard_map.109, bf16[1536,1536]{1,0:T(8,128)(2,1)S(1)} %copy-done.3), kind=kOutput, calls=%fused_computation.2 | convolution fusion | flops 2415919104 | bytes 9437184 | tf_op jit(solution)/shard_map/tdq,de->tqe/dot_general | solution.py:161
  86.5 0.0 copy-start.5
  86.5 0.5 multiply_reduce_fusion
  87.0 0.2 copy-done.5
  87.2 1.6 %multiply_convert_fusion = bf16[512,1536]{1,0:T(8,128)(2,1)} fusion(f32[4,128,1536]{2,1,0:T(8,128)S(1)} %fusion, bf16[512,1536]{1,0:T(8,128)(2,1)S(1)} %copy-done.2, f32[1536]{0:T(1024)S(1)} %copy-done.5, f32[512]{0:T(512)S(1)} %add_rsqrt_fusion), kind=kLoop, calls=%fused_computation.7 | loop fusion | flops 3932160 | bytes 6299648 | tf_op jit(solution)/shard_map/convert_element_type | solution.py:165
  (11 shorter events, 0.0 us)
Async XLA Ops:
  6.5 7.1 %copy-start = (s32[64]{0:T(128)S(1)}, s32[64]{0:T(128)}, u32[]{:S(2)}) copy-start(s32[64]{0:T(128)} %param.19) | copy-start | bytes 772
  6.5 50.2 %all-gather.2.cloned.1.call-start = ((), (), s32[]{:S(2)}) async-start(), calls=%async_computation | async-start | bytes 3342336 | tf_op jit(solution)/shard_map/all_gather | solution.py:139
  7.3 11.9 %collective-permute-start = (bf16[4,128,128]{2,1,0:T(8,128)(2,1)}, bf16[4,128,128]{2,1,0:T(8,128)(2,1)S(1)}, u32[]{:S(2)}, u32[]{:S(2)}) collective-permute-start(bf16[4,128,128]{2,1,0:T(8,128)(2,1)} %param.16), channel_id=1, source_target_pairs={{0,1},{1,2},{2,3},{3,4},{4,5},{5,6},{6,7},{7,8},{8,9},{9,10},{10,1... | collective-permute-start | bytes 393224 | tf_op jit(solution)/shard_map/ppermute | solution.py:24
  10.9 8.2 %collective-permute-start.1 = (bf16[4,128,128]{2,1,0:T(8,128)(2,1)}, bf16[4,128,128]{2,1,0:T(8,128)(2,1)}, u32[]{:S(2)}, u32[]{:S(2)}) collective-permute-start(bf16[4,128,128]{2,1,0:T(8,128)(2,1)} %param.16), channel_id=1, source_target_pairs={{1,0},{2,1},{3,2},{4,3},{5,4},{6,5},{7,6},{8,7},{9,8},{10,9},{11,1... | collective-permute-start | bytes 393224 | tf_op jit(solution)/shard_map/ppermute | solution.py:25
  16.4 2.8 %copy-start.4 = (bf16[4,128,128]{2,1,0:T(8,128)(2,1)S(1)}, bf16[4,128,128]{2,1,0:T(8,128)(2,1)}, u32[]{:S(2)}) copy-start(bf16[4,128,128]{2,1,0:T(8,128)(2,1)} %param.16) | copy-start | bytes 393220
  16.4 40.3 %copy-start.1 = (s32[4]{0:T(128)S(1)}, s32[4]{0:T(128)}, u32[]{:S(2)}) copy-start(s32[4]{0:T(128)} %nb_ref.1) | copy-start | bytes 52
  56.7 27.1 %copy-start.3 = (bf16[1536,1536]{1,0:T(8,128)(2,1)S(1)}, bf16[1536,1536]{1,0:T(8,128)(2,1)}, u32[]{:S(2)}) copy-start(bf16[1536,1536]{1,0:T(8,128)(2,1)} %param.15) | copy-start | bytes 14155780
  83.8 2.7 %copy-start.2 = (bf16[512,1536]{1,0:T(8,128)(2,1)S(1)}, bf16[512,1536]{1,0:T(8,128)(2,1)}, u32[]{:S(2)}) copy-start(bf16[512,1536]{1,0:T(8,128)(2,1)} %param.11) | copy-start | bytes 4718596
  86.5 0.7 copy-start.5
Sparse Core Ops, SparseCore 0:
  9.6 47.0 all-gather.1

commit v8 on v7

--- a/solution.py
+++ b/solution.py
@@ -1,4 +1,3 @@
-import functools
 import math
 
 import jax
@@ -33,7 +32,7 @@
 
 def attend_kernel(
     kinds_ref, ids_ref, nb_ref, cnt_ref, obs_ref, table_ref, gain_ref, qt_ref, o_ref,
-    k_ref, vt_ref, s_ref,
+    k_ref, vt_ref, s_ref, b_ref,
 ):
     tile = pl.program_id(0)
 
@@ -54,6 +53,9 @@
     row = lax.broadcasted_iota(jnp.int32, (LANES, 1), 0)
     low = row < HD
     wide = 2 * LANES
+    for j in range(MAXB):
+        keep = (row < cnt_ref[ids_ref[tile * MAXB + j]]) & (j < used)
+        b_ref[j] = jnp.broadcast_to(jnp.where(keep, 0.0, -jnp.inf), (OBS, wide))
     for pair in range(D // LANES):
         rows = pl.ds(pair * LANES, LANES)
         qt = qt_ref[0, rows, :].astype(jnp.float32) * scale
@@ -64,23 +66,17 @@
         for j in range(MAXB):
             block = ids_ref[tile * MAXB + j]
             keys = k_ref[block, :, rows]
-            s = jnp.dot(keys, q2, preferred_element_type=jnp.float32)
-            s = jnp.where((row < cnt_ref[block]) & (j < used), s, -jnp.inf)
+            s = jnp.dot(keys, q2, preferred_element_type=jnp.float32) + b_ref[j]
             s_ref[j] = s
             high = jnp.maximum(high, jnp.max(s, axis=0, keepdims=True))
         total = jnp.zeros((1, wide), jnp.float32)
         acc = jnp.zeros((LANES, wide), jnp.float32)
-        for j in range(0, MAXB, 2):
-            ws, vs = [], []
-            for i in (j, j + 1):
-                w = jnp.exp(s_ref[i] - high)
-                total = total + jnp.sum(w, axis=0, keepdims=True)
-                ws.append(w.astype(jnp.bfloat16))
-                vs.append(vt_ref[ids_ref[tile * MAXB + i], rows, :])
+        for j in range(MAXB):
+            block = ids_ref[tile * MAXB + j]
+            w = jnp.exp(s_ref[j] - high)
+            total = total + jnp.sum(w, axis=0, keepdims=True)
             acc = acc + jnp.dot(
-                jnp.concatenate(vs, axis=1),
-                jnp.concatenate(ws, axis=0),
-                preferred_element_type=jnp.float32,
+                vt_ref[block, rows, :], w.astype(jnp.bfloat16), preferred_element_type=jnp.float32
             )
         o_ref[0, pl.ds(pair * LANES, HD), :] = (acc[:HD, :LANES] / total[:, :LANES]).astype(
             jnp.bfloat16
@@ -106,6 +102,7 @@
         scratch_shapes=[
             pltpu.VMEM((near, OBS, D), jnp.bfloat16),
             pltpu.VMEM((near, D, OBS), jnp.bfloat16),
+            pltpu.VMEM((MAXB, OBS, 2 * LANES), jnp.float32),
             pltpu.VMEM((MAXB, OBS, 2 * LANES), jnp.float32),
         ],
     )

time: 97.1 us -> 92.2 us (0.950)
  Pallas kernels: 27.1 us -> 22.2 us
    pallas_call x1, Pallas kernels: 27.1 us -> 22.2 us  [attend(): pl.pallas_call(attend_kernel, grid_spec=grid_spec, out_shape=jax.ShapeDty...]
where the time goes in v8:
time: 92.2 us; the launch traced here: 90.7 us
  waiting for transfers between devices  37.3 us (40%)
  Pallas kernels  22.2 us (24%)
  between operations  13.5 us (15%)
  starting transfers between devices  5.61 us (6%)
  other arithmetic  5.48 us (6%)
  local copies, waits for them, and re-layouts  4.04 us (4%)
  matrix products  2.64 us (3%)
    all_gather x1, waiting for transfers between devices, body(): table = lax.all_gather(panels, 'lat', axis=0, tiled=True)  36.6 us
    pallas_call x1, Pallas kernels, attend(): pl.pallas_call(attend_kernel, grid_spec=grid_spec, out_shape=jax.ShapeDty...  22.2 us
    ppermute x1, starting transfers between devices, padded(): before = lax.ppermute(value[length - width:], axis, up)  3.68 us
    dot_general x1, matrix products, body(): jnp.einsum('tdq,de->tqe', attended_t, output_weight, preferred_element_ty...  2.64 us
    ppermute x1, starting transfers between devices, padded(): after = lax.ppermute(value[:width], axis, down)  1.92 us
  transfers between devices with their start and end apart: 3, of which 1 were waited for; matrix products, arithmetic and copies ran while one was open for 8% of the time, Pallas kernels for 0%

profile of v8, /device:TPU:5, one launch (start us, length us, event | category | flops | bytes accessed | tf_op | source)
XLA Modules:
  0.0 90.7 jit_solution(403940821723027794)
XLA Ops:
  6.5 0.0 all-gather.2.cloned.1.call-start
  6.5 0.7 all-gather.2.cloned.1.call-update
  7.3 3.7 %collective-permute-start = (bf16[4,128,128]{2,1,0:T(8,128)(2,1)}, bf16[4,128,128]{2,1,0:T(8,128)(2,1)S(1)}, u32[]{:S(2)}, u32[]{:S(2)}) collective-permute-start(bf16[4,128,128]{2,1,0:T(8,128)(2,1)} %param.16), channel_id=1, source_target_pairs={{0,1},{1,2},{2,3},{3,4},{4,5},{5,6},{6,7},{7,8},{8,9},{9,10},{10,1... | collective-permute-start | bytes 393224 | tf_op jit(solution)/shard_map/ppermute | solution.py:23
  10.9 1.9 %collective-permute-start.1 = (bf16[4,128,128]{2,1,0:T(8,128)(2,1)}, bf16[4,128,128]{2,1,0:T(8,128)(2,1)}, u32[]{:S(2)}, u32[]{:S(2)}) collective-permute-start(bf16[4,128,128]{2,1,0:T(8,128)(2,1)} %param.16), channel_id=1, source_target_pairs={{1,0},{2,1},{3,2},{4,3},{5,4},{6,5},{7,6},{8,7},{9,8},{10,9},{11,1... | collective-permute-start | bytes 393224 | tf_op jit(solution)/shard_map/ppermute | solution.py:24
  12.9 0.7 subtract_clamp_fusion
  13.6 0.1 reshape.41.ids_ref
  13.7 0.7 gather_fusion.1
  14.3 1.3 %gather_fusion = s32[12]{0:T(128)S(1)} fusion(s32[64]{0:T(128)} %param.18, s32[1024]{0:T(1024)S(1)} %pad_clamp_fusion), kind=kCustom, calls=%fused_computation | custom fusion | bytes 144 | tf_op jit(solution)/shard_map/gather | solution.py:141
  15.7 0.7 reshape.42.gain_ref
  16.4 1.7 %fusion.2 = bf16[512,1536]{1,0:T(8,128)(2,1)S(1)} fusion(bf16[512,1536]{1,0:T(8,128)(2,1)} %param.11, f32[1536]{0:T(1024)} %param.12), kind=kLoop, calls=%fused_computation.6 | loop fusion | flops 2359296 | bytes 3151872 | tf_op jit(solution)/shard_map/convert_element_type | solution.py:145
  18.1 1.0 %copy.13 = bf16[4,128,1536]{1,2,0:T(8,128)(2,1)S(1)} copy(bf16[4,128,1536]{2,1,0:T(8,128)(2,1)S(1)} %bitcast.15) | data formatting | bytes 3145728 | tf_op jit(solution)/shard_map/reshape | solution.py:146
  19.2 0.0 collective-permute-done
  19.2 0.0 collective-permute-done.1
  19.2 1.0 %pad_maximum_fusion.obs_ref = bf16[12,128,128]{2,1,0:T(8,128)(2,1)S(1)} fusion(bf16[4,128,128]{2,1,0:T(8,128)(2,1)} %collective-permute-done.1, bf16[4,128,128]{2,1,0:T(8,128)(2,1)S(1)} %copy-done.4, bf16[4,128,128]{2,1,0:T(8,128)(2,1)S(1)} %collective-permute-done), kind=kLoop, calls=%fused_computation.9 | loop fusion | flops 393216 | bytes 786432 | tf_op jit(solution)/shard_map/concatenate | solution.py:25
  20.1 36.6 %all-gather.2.cloned.1.call-done.table_ref = bf16[1024,1536]{1,0:T(8,128)(2,1)} async-done(((bf16[64,1536]{1,0:T(8,128)(2,1)}), bf16[1024,1536]{1,0:T(8,128)(2,1)}) %all-gather.2.cloned.1.call-update) | async-done | bytes 3145744 | tf_op jit(solution)/shard_map/all_gather | solution.py:136
  56.7 0.0 copy-done.1
  56.7 22.2 %shard_map.109 = bf16[4,1536,128]{2,1,0:T(8,128)(2,1)S(1)} custom-call(s32[12]{0:T(128)S(1)} %broadcast_clamp_fusion.kinds_ref, s32[24]{0:T(128)S(1)} %reshape.41.ids_ref, s32[4]{0:T(128)S(1)} %copy-done.1, s32[12]{0:T(128)S(1)} %gather_fusion.1, bf16[12,128,128]{2,1,0:T(8,128)(2,1)S(1)} %pad_maximum_fusion.obs_ref, ...), custom_call_target="tpu_custom_call" | custom-call | tf_op jit(solution)/shard_map/pallas_call | solution.py:109
  78.9 0.0 copy-done.3
  78.9 0.0 copy-start.2
  78.9 2.6 %fusion = f32[4,128,1536]{2,1,0:T(8,128)S(1)} fusion(bf16[4,1536,128]{2,1,0:T(8,128)(2,1)S(1)} %shard_map.109, bf16[1536,1536]{1,0:T(8,128)(2,1)S(1)} %copy-done.3), kind=kOutput, calls=%fused_computation.2 | convolution fusion | flops 2415919104 | bytes 9437184 | tf_op jit(solution)/shard_map/tdq,de->tqe/dot_general | solution.py:158
  81.6 0.0 copy-start.5
  81.6 0.5 multiply_reduce_fusion
  82.1 0.2 copy-done.5
  82.3 1.6 %multiply_convert_fusion = bf16[512,1536]{1,0:T(8,128)(2,1)} fusion(f32[4,128,1536]{2,1,0:T(8,128)S(1)} %fusion, bf16[512,1536]{1,0:T(8,128)(2,1)S(1)} %copy-done.2, f32[1536]{0:T(1024)S(1)} %copy-done.5, f32[512]{0:T(512)S(1)} %add_rsqrt_fusion), kind=kLoop, calls=%fused_computation.7 | loop fusion | flops 3932160 | bytes 6299648 | tf_op jit(solution)/shard_map/convert_element_type | solution.py:162
  (11 shorter events, 0.0 us)
Async XLA Ops:
  6.5 7.1 %copy-start = (s32[64]{0:T(128)S(1)}, s32[64]{0:T(128)}, u32[]{:S(2)}) copy-start(s32[64]{0:T(128)} %param.19) | copy-start | bytes 772
  6.5 50.2 %all-gather.2.cloned.1.call-start = ((), (), s32[]{:S(2)}) async-start(), calls=%async_computation | async-start | bytes 3342336 | tf_op jit(solution)/shard_map/all_gather | solution.py:136
  7.3 11.9 %collective-permute-start = (bf16[4,128,128]{2,1,0:T(8,128)(2,1)}, bf16[4,128,128]{2,1,0:T(8,128)(2,1)S(1)}, u32[]{:S(2)}, u32[]{:S(2)}) collective-permute-start(bf16[4,128,128]{2,1,0:T(8,128)(2,1)} %param.16), channel_id=1, source_target_pairs={{0,1},{1,2},{2,3},{3,4},{4,5},{5,6},{6,7},{7,8},{8,9},{9,10},{10,1... | collective-permute-start | bytes 393224 | tf_op jit(solution)/shard_map/ppermute | solution.py:23
  10.9 8.2 %collective-permute-start.1 = (bf16[4,128,128]{2,1,0:T(8,128)(2,1)}, bf16[4,128,128]{2,1,0:T(8,128)(2,1)}, u32[]{:S(2)}, u32[]{:S(2)}) collective-permute-start(bf16[4,128,128]{2,1,0:T(8,128)(2,1)} %param.16), channel_id=1, source_target_pairs={{1,0},{2,1},{3,2},{4,3},{5,4},{6,5},{7,6},{8,7},{9,8},{10,9},{11,1... | collective-permute-start | bytes 393224 | tf_op jit(solution)/shard_map/ppermute | solution.py:24
  16.4 2.8 %copy-start.4 = (bf16[4,128,128]{2,1,0:T(8,128)(2,1)S(1)}, bf16[4,128,128]{2,1,0:T(8,128)(2,1)}, u32[]{:S(2)}) copy-start(bf16[4,128,128]{2,1,0:T(8,128)(2,1)} %param.16) | copy-start | bytes 393220
  16.4 40.3 %copy-start.1 = (s32[4]{0:T(128)S(1)}, s32[4]{0:T(128)}, u32[]{:S(2)}) copy-start(s32[4]{0:T(128)} %nb_ref.1) | copy-start | bytes 52
  56.7 22.2 %copy-start.3 = (bf16[1536,1536]{1,0:T(8,128)(2,1)S(1)}, bf16[1536,1536]{1,0:T(8,128)(2,1)}, u32[]{:S(2)}) copy-start(bf16[1536,1536]{1,0:T(8,128)(2,1)} %param.15) | copy-start | bytes 14155780
  78.9 2.7 %copy-start.2 = (bf16[512,1536]{1,0:T(8,128)(2,1)S(1)}, bf16[512,1536]{1,0:T(8,128)(2,1)}, u32[]{:S(2)}) copy-start(bf16[512,1536]{1,0:T(8,128)(2,1)} %param.11) | copy-start | bytes 4718596
  81.6 0.7 copy-start.5
Sparse Core Ops, SparseCore 0:
  9.6 47.0 all-gather.1

commit v9 on v8

--- a/solution.py
+++ b/solution.py
@@ -30,14 +30,27 @@
     return values * lax.rsqrt(jnp.mean(values * values, axis=-1, keepdims=True) + 1e-06) * gain
 
 
+def finish(lat_ref, att, w_ref, ogain_ref, o_ref, tile):
+    rows = pl.ds(pl.multiple_of(tile * CELLS, CELLS), CELLS)
+    mixed = lat_ref[rows, :].astype(jnp.float32) + lax.dot_general(
+        att, w_ref[...], (((0,), (0,)), ((), ())), preferred_element_type=jnp.float32
+    )
+    norm = lax.rsqrt(jnp.mean(mixed * mixed, axis=1, keepdims=True) + 1e-06)
+    o_ref[rows, :] = (mixed * norm * ogain_ref[...]).astype(jnp.bfloat16)
+
+
 def attend_kernel(
-    kinds_ref, ids_ref, nb_ref, cnt_ref, obs_ref, table_ref, gain_ref, qt_ref, o_ref,
-    k_ref, vt_ref, s_ref, b_ref,
+    kinds_ref, ids_ref, nb_ref, cnt_ref, obs_ref, table_ref, gain_ref, qt_ref, lat_ref,
+    ogain_ref, w_hbm, o_ref, k_ref, vt_ref, s_ref, b_ref, att_ref, w_ref, sem,
 ):
     tile = pl.program_id(0)
+    tiles = pl.num_programs(0)
+    weight_copy = pltpu.make_async_copy(w_hbm, w_ref, sem)
 
     @pl.when(tile == 0)
     def _():
+        weight_copy.start()
+        att_ref[1] = jnp.zeros(att_ref.shape[1:], jnp.bfloat16)
         for b in range(k_ref.shape[0]):
             start = pl.multiple_of(kinds_ref[b] * CH, CH)
             embedded = jnp.dot(
@@ -47,6 +60,10 @@
             norm = lax.rsqrt(jnp.mean(embedded * embedded, axis=1, keepdims=True) + 1e-06)
             k_ref[b] = (embedded * norm * gain_ref[...]).astype(jnp.bfloat16)
             vt_ref[b] = embedded.T.astype(jnp.bfloat16)
+        weight_copy.wait()
+
+    slot = tile % 2
+    finish(lat_ref, att_ref[1 - slot], w_ref, ogain_ref, o_ref, (tile + tiles - 1) % tiles)
 
     used = nb_ref[tile]
     scale = 1.0 / math.sqrt(HD)
@@ -78,15 +95,22 @@
             acc = acc + jnp.dot(
                 vt_ref[block, rows, :], w.astype(jnp.bfloat16), preferred_element_type=jnp.float32
             )
-        o_ref[0, pl.ds(pair * LANES, HD), :] = (acc[:HD, :LANES] / total[:, :LANES]).astype(
-            jnp.bfloat16
-        )
-        o_ref[0, pl.ds(pair * LANES + HD, HD), :] = (
+        att_ref[slot, pl.ds(pair * LANES, HD), :] = (
+            acc[:HD, :LANES] / total[:, :LANES]
+        ).astype(jnp.bfloat16)
+        att_ref[slot, pl.ds(pair * LANES + HD, HD), :] = (
             acc[HD:, LANES:] / total[:, LANES:]
         ).astype(jnp.bfloat16)
 
-
-def attend(kinds, local_ids, tile_blocks, counts, near_obs, table, key_gain, queries_t):
+    @pl.when(tile == tiles - 1)
+    def _():
+        finish(lat_ref, att_ref[slot], w_ref, ogain_ref, o_ref, tile)
+
+
+def attend(
+    kinds, local_ids, tile_blocks, counts, near_obs, table, key_gain, queries_t, latent,
+    output_gain, output_weight,
+):
     tiles = queries_t.shape[0]
     near = near_obs.shape[0]
     grid_spec = pltpu.PrefetchScalarGridSpec(
@@ -97,23 +121,41 @@
             pl.BlockSpec(table.shape, lambda t, *_: (0, 0)),
             pl.BlockSpec((1, D), lambda t, *_: (0, 0)),
             pl.BlockSpec((1, D, CELLS), lambda t, *_: (t, 0, 0)),
+            pl.BlockSpec(latent.shape, lambda t, *_: (0, 0)),
+            pl.BlockSpec((1, D), lambda t, *_: (0, 0)),
+            pl.BlockSpec(memory_space=pl.ANY),
         ],
-        out_specs=pl.BlockSpec((1, D, CELLS), lambda t, *_: (t, 0, 0)),
+        out_specs=pl.BlockSpec(latent.shape, lambda t, *_: (0, 0)),
         scratch_shapes=[
             pltpu.VMEM((near, OBS, D), jnp.bfloat16),
             pltpu.VMEM((near, D, OBS), jnp.bfloat16),
             pltpu.VMEM((MAXB, OBS, 2 * LANES), jnp.float32),
             pltpu.VMEM((MAXB, OBS, 2 * LANES), jnp.float32),
+            pltpu.VMEM((2, D, CELLS), jnp.bfloat16),
+            pltpu.VMEM((D, D), jnp.bfloat16),
+            pltpu.SemaphoreType.DMA,
         ],
     )
     return pl.pallas_call(
         attend_kernel,
         grid_spec=grid_spec,
-        out_shape=jax.ShapeDtypeStruct(queries_t.shape, jnp.bfloat16),
+        out_shape=jax.ShapeDtypeStruct(latent.shape, jnp.bfloat16),
         compiler_params=pltpu.CompilerParams(
-            dimension_semantics=("arbitrary",), vmem_limit_bytes=48 * 1024 * 1024
+            dimension_semantics=("arbitrary",), vmem_limit_bytes=56 * 1024 * 1024
         ),
-    )(kinds, local_ids.reshape(-1), tile_blocks, counts, near_obs, table, key_gain.reshape(1, D), queries_t)
+    )(
+        kinds,
+        local_ids.reshape(-1),
+        tile_blocks,
+        counts,
+        near_obs,
+        table,
+        key_gain.reshape(1, D),
+        queries_t,
+        latent,
+        output_gain.reshape(1, D),
+        output_weight,
+    )
 
 
 def body(
@@ -145,7 +187,7 @@
     queries = (latent.astype(jnp.float32) * query_gain).astype(jnp.bfloat16)
     queries_t = jnp.swapaxes(queries.reshape(tiles, CELLS, D), 1, 2)
     local_ids = jnp.clip(footprint - first_block, 0, near_count - 1).astype(jnp.int32)
-    attended_t = attend(
+    return attend(
         near_kinds,
         local_ids,
         tile_blocks.astype(jnp.int32),
@@ -154,12 +196,10 @@
         table,
         key_gain.astype(jnp.float32),
         queries_t,
-    )
-    projected = jnp.einsum(
-        "tdq,de->tqe", attended_t, output_weight, preferred_element_type=jnp.float32
-    ).reshape(tiles * CELLS, D)
-    mixed = latent.astype(jnp.float32) + projected
-    return normalize(mixed, output_gain).astype(jnp.bfloat16)
+        latent,
+        output_gain.astype(jnp.float32),
+        output_weight,
+    )
 
 
 def solution(mesh):

time: 92.2 us -> 92.2 us (level)
  Pallas kernels: 22.2 us -> 27.1 us
  waiting for transfers between devices: 37.3 us -> 33.4 us
  local copies, waits for them, and re-layouts: 4.04 us -> 7.31 us
  matrix products: 2.64 us -> 0 us
  other arithmetic: 5.48 us -> 3.85 us
    pallas_call x1, Pallas kernels: 22.2 us -> 27.1 us  [attend(): pl.pallas_call(attend_kernel, grid_spec=grid_spec, out_shape=jax.ShapeDty...]
    all_gather x1, waiting for transfers between devices: 36.6 us -> 32.6 us  [body(): table = lax.all_gather(panels, 'lat', axis=0, tiled=True)]
    dot_general x1 -> x0, matrix products: 2.64 us -> none  [body(): jnp.einsum('tdq,de->tqe', attended_t, output_weight, preferred_element_ty...]
    convert_element_type x1 -> x0, other arithmetic: 1.62 us -> none  [body(): return normalize(mixed, output_gain).astype(jnp.bfloat16)]
    reshape x0 -> x1, local copies, waits for them, and re-layouts: none -> 1.28 us  [attend(): output_gain.reshape(1, D)]
  transfers between devices with their start and end apart: 3 -> 3, of which waited for: 1 -> 1; matrix products, arithmetic and copies ran while one was open for 8% -> 12% of each run, Pallas kernels for 0% -> 0%
where the time goes in v9:
time: 92.2 us; the launch traced here: 90.7 us
  waiting for transfers between devices  33.4 us (36%)
  Pallas kernels  27.1 us (29%)
  between operations  13.5 us (15%)
  local copies, waits for them, and re-layouts  7.31 us (8%)
  starting transfers between devices  5.61 us (6%)
  other arithmetic  3.85 us (4%)
    all_gather x1, waiting for transfers between devices, body(): table = lax.all_gather(panels, 'lat', axis=0, tiled=True)  32.6 us
    pallas_call x1, Pallas kernels, attend(): pl.pallas_call(attend_kernel, grid_spec=grid_spec, out_shape=jax.ShapeDty...  27.1 us
    ppermute x1, starting transfers between devices, padded(): before = lax.ppermute(value[length - width:], axis, up)  3.68 us
    ppermute x1, starting transfers between devices, padded(): after = lax.ppermute(value[:width], axis, down)  1.92 us
  transfers between devices with their start and end apart: 3, of which 1 were waited for; matrix products, arithmetic and copies ran while one was open for 12% of the time, Pallas kernels for 0%

profile of v9, /device:TPU:5, one launch (start us, length us, event | category | flops | bytes accessed | tf_op | source)
XLA Modules:
  0.0 90.7 jit_solution(4838551631634452201)
XLA Ops:
  6.5 0.0 copy-start
  6.5 0.0 all-gather.2.cloned.1.call-start
  6.5 0.7 all-gather.2.cloned.1.call-update
  7.3 3.7 %collective-permute-start = (bf16[4,128,128]{2,1,0:T(8,128)(2,1)}, bf16[4,128,128]{2,1,0:T(8,128)(2,1)S(1)}, u32[]{:S(2)}, u32[]{:S(2)}) collective-permute-start(bf16[4,128,128]{2,1,0:T(8,128)(2,1)} %param.16), channel_id=1, source_target_pairs={{0,1},{1,2},{2,3},{3,4},{4,5},{5,6},{6,7},{7,8},{8,9},{9,10},{10,1... | collective-permute-start | bytes 393224 | tf_op jit(solution)/shard_map/ppermute | solution.py:23
  10.9 1.9 %collective-permute-start.1 = (bf16[4,128,128]{2,1,0:T(8,128)(2,1)}, bf16[4,128,128]{2,1,0:T(8,128)(2,1)S(1)}, u32[]{:S(2)}, u32[]{:S(2)}) collective-permute-start(bf16[4,128,128]{2,1,0:T(8,128)(2,1)} %param.16), channel_id=1, source_target_pairs={{1,0},{2,1},{3,2},{4,3},{5,4},{6,5},{7,6},{8,7},{9,8},{10,9},{11,1... | collective-permute-start | bytes 393224 | tf_op jit(solution)/shard_map/ppermute | solution.py:24
  12.9 0.7 subtract_clamp_fusion
  13.6 0.7 reshape.32.ids_ref
  14.3 0.0 copy-done
  14.3 1.2 %gather_fusion.1 = s32[12]{0:T(128)} fusion(s32[64]{0:T(128)S(1)} %copy-done, s32[1024]{0:T(1024)S(1)} %pad_clamp_fusion), kind=kCustom, calls=%fused_computation.1 | custom fusion | bytes 144 | tf_op jit(solution)/shard_map/gather | solution.py:184
  15.4 1.3 %gather_fusion = s32[12]{0:T(128)S(1)} fusion(s32[64]{0:T(128)} %param.18, s32[1024]{0:T(1024)S(1)} %pad_clamp_fusion), kind=kCustom, calls=%fused_computation | custom fusion | bytes 144 | tf_op jit(solution)/shard_map/gather | solution.py:183
  16.7 1.3 %reshape.33.gain_ref = f32[1,1536]{1,0:T(1,128)} reshape(f32[1536]{0:T(1024)} %param.13) | data formatting | bytes 12288 | tf_op jit(solution)/shard_map/reshape | solution.py:153
  18.0 1.3 %reshape.35.ogain_ref = f32[1,1536]{1,0:T(1,128)} reshape(f32[1536]{0:T(1024)} %param.14) | data formatting | bytes 12288 | tf_op jit(solution)/shard_map/reshape | solution.py:156
  19.3 1.7 %multiply_convert_fusion = bf16[512,1536]{1,0:T(8,128)(2,1)S(1)} fusion(bf16[512,1536]{1,0:T(8,128)(2,1)} %lat_ref.1, f32[1536]{0:T(1024)} %param.12), kind=kLoop, calls=%fused_computation.2 | loop fusion | flops 2359296 | bytes 3151872 | tf_op jit(solution)/shard_map/convert_element_type | solution.py:187
  21.1 0.0 copy-start.1
  21.1 1.6 %copy.12 = bf16[4,128,1536]{1,2,0:T(8,128)(2,1)} copy(bf16[4,128,1536]{2,1,0:T(8,128)(2,1)S(1)} %bitcast.4) | data formatting | bytes 3145728 | tf_op jit(solution)/shard_map/reshape | solution.py:188
  22.7 0.6 broadcast_clamp_fusion.kinds_ref
  23.2 0.0 collective-permute-done
  23.2 0.0 collective-permute-done.1
  23.2 0.0 copy-done.1
  23.2 0.8 pad_maximum_fusion.obs_ref
  24.1 32.6 %all-gather.2.cloned.1.call-done.table_ref = bf16[1024,1536]{1,0:T(8,128)(2,1)} async-done(((bf16[64,1536]{1,0:T(8,128)(2,1)}), bf16[1024,1536]{1,0:T(8,128)(2,1)}) %all-gather.2.cloned.1.call-update) | async-done | bytes 3145744 | tf_op jit(solution)/shard_map/all_gather | solution.py:178
  56.7 27.1 %shard_map.109 = bf16[512,1536]{1,0:T(8,128)(2,1)} custom-call(s32[12]{0:T(128)} %broadcast_clamp_fusion.kinds_ref, s32[24]{0:T(128)} %reshape.32.ids_ref, s32[4]{0:T(128)} %nb_ref.1, s32[12]{0:T(128)} %gather_fusion.1, bf16[12,128,128]{2,1,0:T(8,128)(2,1)} %pad_maximum_fusion.obs_ref, bf16[1024,1536]{1,0:T(8,128)(2,1)} %all-gather.2.cloned.1.call-done.table_ref, ...), custom_call_target="tpu_custom_call" | custom-call | tf_op jit(solution)/shard_map/pallas_call | solution.py:139
  (2 shorter events, 0.0 us)
Async XLA Ops:
  6.5 7.7 %copy-start = (s32[64]{0:T(128)S(1)}, s32[64]{0:T(128)}, u32[]{:S(2)}) copy-start(s32[64]{0:T(128)} %param.19) | copy-start | bytes 772
  6.5 50.2 %all-gather.2.cloned.1.call-start = ((), (), s32[]{:S(2)}) async-start(), calls=%async_computation | async-start | bytes 3342336 | tf_op jit(solution)/shard_map/all_gather | solution.py:178
  7.3 16.0 %collective-permute-start = (bf16[4,128,128]{2,1,0:T(8,128)(2,1)}, bf16[4,128,128]{2,1,0:T(8,128)(2,1)S(1)}, u32[]{:S(2)}, u32[]{:S(2)}) collective-permute-start(bf16[4,128,128]{2,1,0:T(8,128)(2,1)} %param.16), channel_id=1, source_target_pairs={{0,1},{1,2},{2,3},{3,4},{4,5},{5,6},{6,7},{7,8},{8,9},{9,10},{10,1... | collective-permute-start | bytes 393224 | tf_op jit(solution)/shard_map/ppermute | solution.py:23
  10.9 12.3 %collective-permute-start.1 = (bf16[4,128,128]{2,1,0:T(8,128)(2,1)}, bf16[4,128,128]{2,1,0:T(8,128)(2,1)S(1)}, u32[]{:S(2)}, u32[]{:S(2)}) collective-permute-start(bf16[4,128,128]{2,1,0:T(8,128)(2,1)} %param.16), channel_id=1, source_target_pairs={{1,0},{2,1},{3,2},{4,3},{5,4},{6,5},{7,6},{8,7},{9,8},{10,9},{11,1... | collective-permute-start | bytes 393224 | tf_op jit(solution)/shard_map/ppermute | solution.py:24
  21.1 2.2 %copy-start.1 = (bf16[4,128,128]{2,1,0:T(8,128)(2,1)S(1)}, bf16[4,128,128]{2,1,0:T(8,128)(2,1)}, u32[]{:S(2)}) copy-start(bf16[4,128,128]{2,1,0:T(8,128)(2,1)} %param.16) | copy-start | bytes 393220
Sparse Core Ops, SparseCore 0:
  9.6 47.0 all-gather.1

commit v10 on v8

--- a/solution.py
+++ b/solution.py
@@ -32,17 +32,23 @@
 
 def attend_kernel(
     kinds_ref, ids_ref, nb_ref, cnt_ref, obs_ref, table_ref, gain_ref, qt_ref, o_ref,
-    k_ref, vt_ref, s_ref, b_ref,
+    k_ref, vt_ref, s_ref, b_ref, panel_ref, sem_ref,
 ):
     tile = pl.program_id(0)
 
     @pl.when(tile == 0)
     def _():
+        copies = []
         for b in range(k_ref.shape[0]):
             start = pl.multiple_of(kinds_ref[b] * CH, CH)
-            embedded = jnp.dot(
-                obs_ref[b], table_ref[pl.ds(start, CH), :], preferred_element_type=jnp.float32
+            copy = pltpu.make_async_copy(
+                table_ref.at[pl.ds(start, CH)], panel_ref.at[b], sem_ref.at[b]
             )
+            copy.start()
+            copies.append(copy)
+        for b in range(k_ref.shape[0]):
+            copies[b].wait()
+            embedded = jnp.dot(obs_ref[b], panel_ref[b], preferred_element_type=jnp.float32)
             embedded = embedded.astype(jnp.bfloat16).astype(jnp.float32)
             norm = lax.rsqrt(jnp.mean(embedded * embedded, axis=1, keepdims=True) + 1e-06)
             k_ref[b] = (embedded * norm * gain_ref[...]).astype(jnp.bfloat16)
@@ -94,7 +100,7 @@
         grid=(tiles,),
         in_specs=[
             pl.BlockSpec(near_obs.shape, lambda t, *_: (0, 0, 0)),
-            pl.BlockSpec(table.shape, lambda t, *_: (0, 0)),
+            pl.BlockSpec(memory_space=pl.ANY),
             pl.BlockSpec((1, D), lambda t, *_: (0, 0)),
             pl.BlockSpec((1, D, CELLS), lambda t, *_: (t, 0, 0)),
         ],
@@ -104,6 +110,8 @@
             pltpu.VMEM((near, D, OBS), jnp.bfloat16),
             pltpu.VMEM((MAXB, OBS, 2 * LANES), jnp.float32),
             pltpu.VMEM((MAXB, OBS, 2 * LANES), jnp.float32),
+            pltpu.VMEM((near, CH, D), jnp.bfloat16),
+            pltpu.SemaphoreType.DMA((near,)),
         ],
     )
     return pl.pallas_call(

time: 92.2 us -> 93.4 us (1.013)
  Pallas kernels: 22.2 us -> 23.4 us
    pallas_call x1, Pallas kernels: 22.2 us -> 23.4 us  [attend(): pl.pallas_call(attend_kernel, grid_spec=grid_spec, out_shape=jax.ShapeDty...]
where the time goes in v10:
time: 93.4 us; the launch traced here: 92 us
  waiting for transfers between devices  37.3 us (40%)
  Pallas kernels  23.4 us (25%)
  between operations  13.5 us (14%)
  starting transfers between devices  5.61 us (6%)
  other arithmetic  5.48 us (6%)
  local copies, waits for them, and re-layouts  4.04 us (4%)
  matrix products  2.64 us (3%)
    all_gather x1, waiting for transfers between devices, body(): table = lax.all_gather(panels, 'lat', axis=0, tiled=True)  36.6 us
    pallas_call x1, Pallas kernels, attend(): pl.pallas_call(attend_kernel, grid_spec=grid_spec, out_shape=jax.ShapeDty...  23.4 us
    ppermute x1, starting transfers between devices, padded(): before = lax.ppermute(value[length - width:], axis, up)  3.68 us
    dot_general x1, matrix products, body(): jnp.einsum('tdq,de->tqe', attended_t, output_weight, preferred_element_ty...  2.64 us
    ppermute x1, starting transfers between devices, padded(): after = lax.ppermute(value[:width], axis, down)  1.92 us
  transfers between devices with their start and end apart: 3, of which 1 were waited for; matrix products, arithmetic and copies ran while one was open for 8% of the time, Pallas kernels for 0%

profile of v10, /device:TPU:5, one launch (start us, length us, event | category | flops | bytes accessed | tf_op | source)
XLA Modules:
  0.0 92.0 jit_solution(528260654698146692)
XLA Ops:
  6.5 0.0 copy-start
  6.5 0.7 all-gather.2.cloned.1.call-update
  7.3 3.7 %collective-permute-start = (bf16[4,128,128]{2,1,0:T(8,128)(2,1)}, bf16[4,128,128]{2,1,0:T(8,128)(2,1)S(1)}, u32[]{:S(2)}, u32[]{:S(2)}) collective-permute-start(bf16[4,128,128]{2,1,0:T(8,128)(2,1)} %param.16), channel_id=1, source_target_pairs={{0,1},{1,2},{2,3},{3,4},{4,5},{5,6},{6,7},{7,8},{8,9},{9,10},{10,1... | collective-permute-start | bytes 393224 | tf_op jit(solution)/shard_map/ppermute | solution.py:23
  10.9 1.9 %collective-permute-start.1 = (bf16[4,128,128]{2,1,0:T(8,128)(2,1)}, bf16[4,128,128]{2,1,0:T(8,128)(2,1)}, u32[]{:S(2)}, u32[]{:S(2)}) collective-permute-start(bf16[4,128,128]{2,1,0:T(8,128)(2,1)} %param.16), channel_id=1, source_target_pairs={{1,0},{2,1},{3,2},{4,3},{5,4},{6,5},{7,6},{8,7},{9,8},{10,9},{11,1... | collective-permute-start | bytes 393224 | tf_op jit(solution)/shard_map/ppermute | solution.py:24
  12.9 0.7 subtract_clamp_fusion
  13.6 0.1 reshape.41.ids_ref
  13.7 0.0 copy-done
  13.7 0.7 gather_fusion.1
  14.3 1.3 %gather_fusion = s32[12]{0:T(128)S(1)} fusion(s32[64]{0:T(128)} %param.18, s32[1024]{0:T(1024)S(1)} %pad_clamp_fusion), kind=kCustom, calls=%fused_computation | custom fusion | bytes 144 | tf_op jit(solution)/shard_map/gather | solution.py:149
  15.7 0.7 reshape.42.gain_ref
  16.4 1.7 %fusion.2 = bf16[512,1536]{1,0:T(8,128)(2,1)S(1)} fusion(bf16[512,1536]{1,0:T(8,128)(2,1)} %param.11, f32[1536]{0:T(1024)} %param.12), kind=kLoop, calls=%fused_computation.6 | loop fusion | flops 2359296 | bytes 3151872 | tf_op jit(solution)/shard_map/convert_element_type | solution.py:153
  18.1 1.0 %copy.13 = bf16[4,128,1536]{1,2,0:T(8,128)(2,1)S(1)} copy(bf16[4,128,1536]{2,1,0:T(8,128)(2,1)S(1)} %bitcast.15) | data formatting | bytes 3145728 | tf_op jit(solution)/shard_map/reshape | solution.py:154
  19.2 0.0 collective-permute-done
  19.2 0.0 collective-permute-done.1
  19.2 1.0 %pad_maximum_fusion.obs_ref = bf16[12,128,128]{2,1,0:T(8,128)(2,1)S(1)} fusion(bf16[4,128,128]{2,1,0:T(8,128)(2,1)} %collective-permute-done.1, bf16[4,128,128]{2,1,0:T(8,128)(2,1)S(1)} %copy-done.4, bf16[4,128,128]{2,1,0:T(8,128)(2,1)S(1)} %collective-permute-done), kind=kLoop, calls=%fused_computation.9 | loop fusion | flops 393216 | bytes 786432 | tf_op jit(solution)/shard_map/concatenate | solution.py:25
  20.1 36.6 %all-gather.2.cloned.1.call-done.table_ref = bf16[1024,1536]{1,0:T(8,128)(2,1)} async-done(((bf16[64,1536]{1,0:T(8,128)(2,1)}), bf16[1024,1536]{1,0:T(8,128)(2,1)}) %all-gather.2.cloned.1.call-update) | async-done | bytes 3145744 | tf_op jit(solution)/shard_map/all_gather | solution.py:144
  56.7 23.4 %shard_map.109 = bf16[4,1536,128]{2,1,0:T(8,128)(2,1)S(1)} custom-call(s32[12]{0:T(128)S(1)} %broadcast_clamp_fusion.kinds_ref, s32[24]{0:T(128)S(1)} %reshape.41.ids_ref, s32[4]{0:T(128)S(1)} %copy-done.1, s32[12]{0:T(128)S(1)} %gather_fusion.1, bf16[12,128,128]{2,1,0:T(8,128)(2,1)S(1)} %pad_maximum_fusion.obs_ref, ...), custom_call_target="tpu_custom_call" | custom-call | tf_op jit(solution)/shard_map/pallas_call | solution.py:117
  80.2 0.0 copy-start.2
  80.2 2.6 %fusion = f32[4,128,1536]{2,1,0:T(8,128)S(1)} fusion(bf16[4,1536,128]{2,1,0:T(8,128)(2,1)S(1)} %shard_map.109, bf16[1536,1536]{1,0:T(8,128)(2,1)S(1)} %copy-done.3), kind=kOutput, calls=%fused_computation.2 | convolution fusion | flops 2415919104 | bytes 9437184 | tf_op jit(solution)/shard_map/tdq,de->tqe/dot_general | solution.py:166
  82.8 0.0 copy-done.2
  82.8 0.0 copy-start.5
  82.9 0.5 multiply_reduce_fusion
  83.4 0.2 copy-done.5
  83.5 1.6 %multiply_convert_fusion = bf16[512,1536]{1,0:T(8,128)(2,1)} fusion(f32[4,128,1536]{2,1,0:T(8,128)S(1)} %fusion, bf16[512,1536]{1,0:T(8,128)(2,1)S(1)} %copy-done.2, f32[1536]{0:T(1024)S(1)} %copy-done.5, f32[512]{0:T(512)S(1)} %add_rsqrt_fusion), kind=kLoop, calls=%fused_computation.7 | loop fusion | flops 3932160 | bytes 6299648 | tf_op jit(solution)/shard_map/convert_element_type | solution.py:170
  (11 shorter events, 0.0 us)
Async XLA Ops:
  6.5 7.1 %copy-start = (s32[64]{0:T(128)S(1)}, s32[64]{0:T(128)}, u32[]{:S(2)}) copy-start(s32[64]{0:T(128)} %param.19) | copy-start | bytes 772
  6.5 50.2 %all-gather.2.cloned.1.call-start = ((), (), s32[]{:S(2)}) async-start(), calls=%async_computation | async-start | bytes 3342336 | tf_op jit(solution)/shard_map/all_gather | solution.py:144
  7.3 11.9 %collective-permute-start = (bf16[4,128,128]{2,1,0:T(8,128)(2,1)}, bf16[4,128,128]{2,1,0:T(8,128)(2,1)S(1)}, u32[]{:S(2)}, u32[]{:S(2)}) collective-permute-start(bf16[4,128,128]{2,1,0:T(8,128)(2,1)} %param.16), channel_id=1, source_target_pairs={{0,1},{1,2},{2,3},{3,4},{4,5},{5,6},{6,7},{7,8},{8,9},{9,10},{10,1... | collective-permute-start | bytes 393224 | tf_op jit(solution)/shard_map/ppermute | solution.py:23
  10.9 8.2 %collective-permute-start.1 = (bf16[4,128,128]{2,1,0:T(8,128)(2,1)}, bf16[4,128,128]{2,1,0:T(8,128)(2,1)}, u32[]{:S(2)}, u32[]{:S(2)}) collective-permute-start(bf16[4,128,128]{2,1,0:T(8,128)(2,1)} %param.16), channel_id=1, source_target_pairs={{1,0},{2,1},{3,2},{4,3},{5,4},{6,5},{7,6},{8,7},{9,8},{10,9},{11,1... | collective-permute-start | bytes 393224 | tf_op jit(solution)/shard_map/ppermute | solution.py:24
  16.4 2.8 %copy-start.4 = (bf16[4,128,128]{2,1,0:T(8,128)(2,1)S(1)}, bf16[4,128,128]{2,1,0:T(8,128)(2,1)}, u32[]{:S(2)}) copy-start(bf16[4,128,128]{2,1,0:T(8,128)(2,1)} %param.16) | copy-start | bytes 393220
  16.4 40.3 %copy-start.1 = (s32[4]{0:T(128)S(1)}, s32[4]{0:T(128)}, u32[]{:S(2)}) copy-start(s32[4]{0:T(128)} %nb_ref.1) | copy-start | bytes 52
  56.7 23.4 %copy-start.3 = (bf16[1536,1536]{1,0:T(8,128)(2,1)S(1)}, bf16[1536,1536]{1,0:T(8,128)(2,1)}, u32[]{:S(2)}) copy-start(bf16[1536,1536]{1,0:T(8,128)(2,1)} %param.15) | copy-start | bytes 14155780
  80.2 2.7 %copy-start.2 = (bf16[512,1536]{1,0:T(8,128)(2,1)S(1)}, bf16[512,1536]{1,0:T(8,128)(2,1)}, u32[]{:S(2)}) copy-start(bf16[512,1536]{1,0:T(8,128)(2,1)} %param.11) | copy-start | bytes 4718596
  82.8 0.7 copy-start.5
Sparse Core Ops, SparseCore 0:
  9.6 47.0 all-gather.1

commit v11 on v8

--- a/solution.py
+++ b/solution.py
@@ -43,10 +43,11 @@
             embedded = jnp.dot(
                 obs_ref[b], table_ref[pl.ds(start, CH), :], preferred_element_type=jnp.float32
             )
-            embedded = embedded.astype(jnp.bfloat16).astype(jnp.float32)
+            rounded = embedded.astype(jnp.bfloat16)
+            vt_ref[b] = rounded.T
+            embedded = rounded.astype(jnp.float32)
             norm = lax.rsqrt(jnp.mean(embedded * embedded, axis=1, keepdims=True) + 1e-06)
             k_ref[b] = (embedded * norm * gain_ref[...]).astype(jnp.bfloat16)
-            vt_ref[b] = embedded.T.astype(jnp.bfloat16)
 
     used = nb_ref[tile]
     scale = 1.0 / math.sqrt(HD)

time: 92.2 us -> 91.8 us (level)
  no operation moved by 1% of the time
where the time goes in v11:
time: 91.8 us; the launch traced here: 90.3 us
  waiting for transfers between devices  37.3 us (41%)
  Pallas kernels  21.8 us (24%)
  between operations  13.5 us (15%)
  starting transfers between devices  5.61 us (6%)
  other arithmetic  5.48 us (6%)
  local copies, waits for them, and re-layouts  4.04 us (4%)
  matrix products  2.64 us (3%)
    all_gather x1, waiting for transfers between devices, body(): table = lax.all_gather(panels, 'lat', axis=0, tiled=True)  36.6 us
    pallas_call x1, Pallas kernels, attend(): pl.pallas_call(attend_kernel, grid_spec=grid_spec, out_shape=jax.ShapeDty...  21.8 us
    ppermute x1, starting transfers between devices, padded(): before = lax.ppermute(value[length - width:], axis, up)  3.68 us
    dot_general x1, matrix products, body(): jnp.einsum('tdq,de->tqe', attended_t, output_weight, preferred_element_ty...  2.64 us
    ppermute x1, starting transfers between devices, padded(): after = lax.ppermute(value[:width], axis, down)  1.92 us
  transfers between devices with their start and end apart: 3, of which 1 were waited for; matrix products, arithmetic and copies ran while one was open for 8% of the time, Pallas kernels for 0%

profile of v11, /device:TPU:5, one launch (start us, length us, event | category | flops | bytes accessed | tf_op | source)
XLA Modules:
  0.0 90.3 jit_solution(15713489234500102576)
XLA Ops:
  6.5 0.0 copy-start
  6.5 0.7 all-gather.2.cloned.1.call-update
  7.3 3.7 %collective-permute-start = (bf16[4,128,128]{2,1,0:T(8,128)(2,1)}, bf16[4,128,128]{2,1,0:T(8,128)(2,1)S(1)}, u32[]{:S(2)}, u32[]{:S(2)}) collective-permute-start(bf16[4,128,128]{2,1,0:T(8,128)(2,1)} %param.16), channel_id=1, source_target_pairs={{0,1},{1,2},{2,3},{3,4},{4,5},{5,6},{6,7},{7,8},{8,9},{9,10},{10,1... | collective-permute-start | bytes 393224 | tf_op jit(solution)/shard_map/ppermute | solution.py:23
  10.9 1.9 %collective-permute-start.1 = (bf16[4,128,128]{2,1,0:T(8,128)(2,1)}, bf16[4,128,128]{2,1,0:T(8,128)(2,1)}, u32[]{:S(2)}, u32[]{:S(2)}) collective-permute-start(bf16[4,128,128]{2,1,0:T(8,128)(2,1)} %param.16), channel_id=1, source_target_pairs={{1,0},{2,1},{3,2},{4,3},{5,4},{6,5},{7,6},{8,7},{9,8},{10,9},{11,1... | collective-permute-start | bytes 393224 | tf_op jit(solution)/shard_map/ppermute | solution.py:24
  12.9 0.7 subtract_clamp_fusion
  13.6 0.1 reshape.41.ids_ref
  13.7 0.0 copy-done
  13.7 0.7 gather_fusion.1
  14.3 1.3 %gather_fusion = s32[12]{0:T(128)S(1)} fusion(s32[64]{0:T(128)} %param.18, s32[1024]{0:T(1024)S(1)} %pad_clamp_fusion), kind=kCustom, calls=%fused_computation | custom fusion | bytes 144 | tf_op jit(solution)/shard_map/gather | solution.py:142
  15.7 0.7 reshape.42.gain_ref
  16.4 1.7 %fusion.2 = bf16[512,1536]{1,0:T(8,128)(2,1)S(1)} fusion(bf16[512,1536]{1,0:T(8,128)(2,1)} %param.11, f32[1536]{0:T(1024)} %param.12), kind=kLoop, calls=%fused_computation.6 | loop fusion | flops 2359296 | bytes 3151872 | tf_op jit(solution)/shard_map/convert_element_type | solution.py:146
  18.1 1.0 %copy.13 = bf16[4,128,1536]{1,2,0:T(8,128)(2,1)S(1)} copy(bf16[4,128,1536]{2,1,0:T(8,128)(2,1)S(1)} %bitcast.15) | data formatting | bytes 3145728 | tf_op jit(solution)/shard_map/reshape | solution.py:147
  19.2 0.0 collective-permute-done
  19.2 0.0 collective-permute-done.1
  19.2 1.0 %pad_maximum_fusion.obs_ref = bf16[12,128,128]{2,1,0:T(8,128)(2,1)S(1)} fusion(bf16[4,128,128]{2,1,0:T(8,128)(2,1)} %collective-permute-done.1, bf16[4,128,128]{2,1,0:T(8,128)(2,1)S(1)} %copy-done.4, bf16[4,128,128]{2,1,0:T(8,128)(2,1)S(1)} %collective-permute-done), kind=kLoop, calls=%fused_computation.9 | loop fusion | flops 393216 | bytes 786432 | tf_op jit(solution)/shard_map/concatenate | solution.py:25
  20.1 36.6 %all-gather.2.cloned.1.call-done.table_ref = bf16[1024,1536]{1,0:T(8,128)(2,1)} async-done(((bf16[64,1536]{1,0:T(8,128)(2,1)}), bf16[1024,1536]{1,0:T(8,128)(2,1)}) %all-gather.2.cloned.1.call-update) | async-done | bytes 3145744 | tf_op jit(solution)/shard_map/all_gather | solution.py:137
  56.7 21.8 %shard_map.109 = bf16[4,1536,128]{2,1,0:T(8,128)(2,1)S(1)} custom-call(s32[12]{0:T(128)S(1)} %broadcast_clamp_fusion.kinds_ref, s32[24]{0:T(128)S(1)} %reshape.41.ids_ref, s32[4]{0:T(128)S(1)} %copy-done.1, s32[12]{0:T(128)S(1)} %gather_fusion.1, bf16[12,128,128]{2,1,0:T(8,128)(2,1)S(1)} %pad_maximum_fusion.obs_ref, ...), custom_call_target="tpu_custom_call" | custom-call | tf_op jit(solution)/shard_map/pallas_call | solution.py:110
  78.5 0.0 copy-start.2
  78.5 2.6 %fusion = f32[4,128,1536]{2,1,0:T(8,128)S(1)} fusion(bf16[4,1536,128]{2,1,0:T(8,128)(2,1)S(1)} %shard_map.109, bf16[1536,1536]{1,0:T(8,128)(2,1)S(1)} %copy-done.3), kind=kOutput, calls=%fused_computation.2 | convolution fusion | flops 2415919104 | bytes 9437184 | tf_op jit(solution)/shard_map/tdq,de->tqe/dot_general | solution.py:159
  81.2 0.0 copy-done.2
  81.2 0.0 copy-start.5
  81.2 0.5 multiply_reduce_fusion
  81.7 0.2 copy-done.5
  81.9 1.6 %multiply_convert_fusion = bf16[512,1536]{1,0:T(8,128)(2,1)} fusion(f32[4,128,1536]{2,1,0:T(8,128)S(1)} %fusion, bf16[512,1536]{1,0:T(8,128)(2,1)S(1)} %copy-done.2, f32[1536]{0:T(1024)S(1)} %copy-done.5, f32[512]{0:T(512)S(1)} %add_rsqrt_fusion), kind=kLoop, calls=%fused_computation.7 | loop fusion | flops 3932160 | bytes 6299648 | tf_op jit(solution)/shard_map/convert_element_type | solution.py:163
  (11 shorter events, 0.0 us)
Async XLA Ops:
  6.5 7.1 %copy-start = (s32[64]{0:T(128)S(1)}, s32[64]{0:T(128)}, u32[]{:S(2)}) copy-start(s32[64]{0:T(128)} %param.19) | copy-start | bytes 772
  6.5 50.2 %all-gather.2.cloned.1.call-start = ((), (), s32[]{:S(2)}) async-start(), calls=%async_computation | async-start | bytes 3342336 | tf_op jit(solution)/shard_map/all_gather | solution.py:137
  7.3 11.9 %collective-permute-start = (bf16[4,128,128]{2,1,0:T(8,128)(2,1)}, bf16[4,128,128]{2,1,0:T(8,128)(2,1)S(1)}, u32[]{:S(2)}, u32[]{:S(2)}) collective-permute-start(bf16[4,128,128]{2,1,0:T(8,128)(2,1)} %param.16), channel_id=1, source_target_pairs={{0,1},{1,2},{2,3},{3,4},{4,5},{5,6},{6,7},{7,8},{8,9},{9,10},{10,1... | collective-permute-start | bytes 393224 | tf_op jit(solution)/shard_map/ppermute | solution.py:23
  10.9 8.2 %collective-permute-start.1 = (bf16[4,128,128]{2,1,0:T(8,128)(2,1)}, bf16[4,128,128]{2,1,0:T(8,128)(2,1)}, u32[]{:S(2)}, u32[]{:S(2)}) collective-permute-start(bf16[4,128,128]{2,1,0:T(8,128)(2,1)} %param.16), channel_id=1, source_target_pairs={{1,0},{2,1},{3,2},{4,3},{5,4},{6,5},{7,6},{8,7},{9,8},{10,9},{11,1... | collective-permute-start | bytes 393224 | tf_op jit(solution)/shard_map/ppermute | solution.py:24
  16.4 2.8 %copy-start.4 = (bf16[4,128,128]{2,1,0:T(8,128)(2,1)S(1)}, bf16[4,128,128]{2,1,0:T(8,128)(2,1)}, u32[]{:S(2)}) copy-start(bf16[4,128,128]{2,1,0:T(8,128)(2,1)} %param.16) | copy-start | bytes 393220
  16.4 40.3 %copy-start.1 = (s32[4]{0:T(128)S(1)}, s32[4]{0:T(128)}, u32[]{:S(2)}) copy-start(s32[4]{0:T(128)} %nb_ref.1) | copy-start | bytes 52
  56.7 21.8 %copy-start.3 = (bf16[1536,1536]{1,0:T(8,128)(2,1)S(1)}, bf16[1536,1536]{1,0:T(8,128)(2,1)}, u32[]{:S(2)}) copy-start(bf16[1536,1536]{1,0:T(8,128)(2,1)} %param.15) | copy-start | bytes 14155780
  78.5 2.7 %copy-start.2 = (bf16[512,1536]{1,0:T(8,128)(2,1)S(1)}, bf16[512,1536]{1,0:T(8,128)(2,1)}, u32[]{:S(2)}) copy-start(bf16[512,1536]{1,0:T(8,128)(2,1)} %param.11) | copy-start | bytes 4718596
  81.2 0.7 copy-start.5
Sparse Core Ops, SparseCore 0:
  9.6 47.0 all-gather.1
